TPU v7x, 32 devices: a whole 2x2x4 slice. The times are simulated.
32 devices in a mesh: attn: 8 (over z, y), exp: 4 (over x, core).
Axes of the slice: x: 2, y: 2, z: 4, core: 2. Of those that a mesh axis runs over, the one named last changes fastest.
Arguments:
- patches: bfloat16 [1536, 4096], P('attn', 'exp'), may hold values from -6 to 6
- grad_out: bfloat16 [1536, 4096], P('attn', 'exp'), may hold values from -6 to 6
- route_ids: int32 [1536, 2], P('attn'), may hold values from 0 to 15, all different within a row; in each aligned block of 192 rows (0 to 191, 192 to 383, ...) at most 48 rows name the same one
- gates: float32 [1536, 2], P('attn'), may hold values from 0.25 to 1
- w_up: bfloat16 [32, 4096, 768], P(('attn', 'exp')), may hold values from -0.09375 to 0.09375
- w_down: bfloat16 [32, 768, 4096], P(('attn', 'exp')), may hold values from -0.15625 to 0.15625
Outputs:
- mixed: bfloat16 [1536, 4096], P('attn', 'exp')
- grad_patches: bfloat16 [1536, 4096], P('attn', 'exp')
- grad_up: float32 [32, 4096, 768], P(('attn', 'exp'))
- grad_down: float32 [32, 768, 4096], P(('attn', 'exp'))
Inputs may be any that keep to these rules, and one draw needn't show every extreme that they name: `route_ids`: the two experts of a row differ; among the 192 rows of one index of attn, no expert is named by more than 48 rows, a bound that some block reaches.
All inputs are finite; a program needn't handle non-finite values.
Results may differ from a plain program's by a relative error of at most 0.0064.
Values may be sent and summed in bfloat16 or wider, within the bound.
No kernel may reach another device: no remote copies, remote signals or barrier semaphores. Data moves between devices by JAX's collectives and lax.ppermute only.
A program may use at most 128 MiB of HBM per device.

v0:
```python
import jax
import jax.numpy as jnp
from jax import lax
from jax.sharding import PartitionSpec as P

EXP_DEV = 2


def gelu_parts(pre_act):
    inner_arg = 0.7978845608 * (pre_act + 0.044715 * pre_act * pre_act * pre_act)
    tanh_val = jnp.tanh(inner_arg)
    gelu_value = 0.5 * pre_act * (1.0 + tanh_val)
    gelu_slope = 0.5 * (1.0 + tanh_val) + 0.5 * pre_act * (
        1.0 - tanh_val * tanh_val
    ) * 0.7978845608 * (1.0 + 0.134145 * pre_act * pre_act)
    return (gelu_value, gelu_slope)


def route_slots(route_ids, experts, capacity):
    flat_ids = route_ids.reshape(-1)
    one_hot = (flat_ids[:, None] == jnp.arange(experts, dtype=jnp.int32)[None, :]).astype(jnp.int32)
    before = jnp.cumsum(one_hot, axis=0) - one_hot
    rank_in = jnp.sum(before * one_hot, axis=1).reshape(route_ids.shape)
    return (route_ids // EXP_DEV) * capacity + rank_in


def on_device(patches, grad_out, route_ids, gates, w_up, w_down):
    sections = lax.axis_size("attn")
    n_exp = lax.axis_size("exp")
    cores = n_exp // EXP_DEV
    me = lax.axis_index("exp")
    half = me // cores
    core = me % cores
    experts = EXP_DEV * sections
    token_count, slice_w = patches.shape
    capacity = 4 * token_count // experts
    slots = sections * capacity
    n_loc, model_width, hid_loc = w_up.shape
    sub_w = EXP_DEV * slice_w
    f32 = jnp.float32
    bf16 = jnp.bfloat16

    def core_shift(s):
        return [(i, (i // cores) * cores + (i % cores + s) % cores) for i in range(n_exp)]

    half_swap = [(i, (i + cores) % n_exp) for i in range(n_exp)]

    def core_subset(local):
        other = lax.ppermute(local, "exp", half_swap)
        first = half == 0
        return jnp.concatenate(
            [jnp.where(first, local, other), jnp.where(first, other, local)], axis=1
        )

    sub_x = core_subset(patches)
    sub_dy = core_subset(grad_out)

    local_slot = route_slots(route_ids, experts, capacity)
    owned = (route_ids % EXP_DEV) == half
    slot_iota = jnp.arange(slots, dtype=jnp.int32)[:, None]
    picks = [
        (local_slot[:, k][None, :] == slot_iota) & owned[:, k][None, :]
        for k in range(route_ids.shape[1])
    ]
    dispatch = picks[0]
    for extra in picks[1:]:
        dispatch = dispatch | extra
    gate_slot = sum(
        jnp.sum(jnp.where(pick, gates[:, k][None, :], 0.0), axis=1) for k, pick in enumerate(picks)
    )
    dispatch_mat = dispatch.astype(bf16)

    x_buf = jnp.dot(dispatch_mat, sub_x, preferred_element_type=f32).astype(bf16)
    dy_buf = jnp.dot(dispatch_mat, sub_dy, preferred_element_type=f32)
    d_buf = (gate_slot[:, None] * dy_buf).astype(bf16)

    def pick_by(index, values):
        picked = values[0]
        for i, value in enumerate(values[1:], start=1):
            picked = jnp.where(index == i, value, picked)
        return picked

    def to_experts(buf):
        got = lax.all_to_all(
            buf.reshape(sections, capacity, sub_w), "attn", split_axis=0, concat_axis=0, tiled=True
        ).reshape(slots, sub_w)
        by_shift = [got] + [lax.ppermute(got, "exp", core_shift(s)) for s in range(1, cores)]
        ordered = [pick_by((core - source) % cores, by_shift) for source in range(cores)]
        return jnp.concatenate(
            [ordered[q][:, p * slice_w:(p + 1) * slice_w] for p in range(EXP_DEV) for q in range(cores)],
            axis=1,
        )

    x_rows = to_experts(x_buf)
    d_rows = to_experts(d_buf)

    if n_loc == 1:
        up_mat = w_up[0]
    else:
        up_mat = jnp.transpose(w_up, (1, 0, 2)).reshape(model_width, n_loc * hid_loc)
    down_mat = w_down.reshape(n_loc * hid_loc, model_width)

    pre_act = jnp.dot(x_rows, up_mat, preferred_element_type=f32)
    gelu_value, gelu_slope = gelu_parts(pre_act)
    activation = gelu_value.astype(bf16)
    grad_act = jnp.einsum("sd,hd->sh", d_rows, down_mat, preferred_element_type=f32)
    grad_pre = (grad_act * gelu_slope).astype(bf16)
    grad_down = jnp.einsum("sh,sd->hd", activation, d_rows, preferred_element_type=f32)
    grad_up = jnp.einsum("sd,sh->dh", x_rows, grad_pre, preferred_element_type=f32)

    out_loc = None
    dx_loc = None
    for g in range(n_loc):
        part = slice(g * hid_loc, (g + 1) * hid_loc)
        out_g = jnp.dot(activation[:, part], w_down[g], preferred_element_type=f32)
        dx_g = jnp.einsum("sh,dh->sd", grad_pre[:, part], w_up[g], preferred_element_type=f32)
        out_g = out_g.astype(bf16).astype(f32)
        dx_g = dx_g.astype(bf16).astype(f32)
        out_loc = out_g if out_loc is None else out_loc + out_g
        dx_loc = dx_g if dx_loc is None else dx_loc + dx_g

    def to_sections(rows):
        subsets = [
            jnp.concatenate(
                [rows[:, (p * cores + q) * slice_w:(p * cores + q + 1) * slice_w] for p in range(EXP_DEV)],
                axis=1,
            )
            for q in range(cores)
        ]
        summed = pick_by(core, subsets)
        for s in range(1, cores):
            theirs = pick_by((core + s) % cores, subsets)
            got = lax.ppermute(theirs.astype(bf16), "exp", core_shift(s))
            summed = summed + got.astype(f32)
        back = lax.all_to_all(
            summed.astype(bf16).reshape(sections, capacity, sub_w),
            "attn", split_axis=0, concat_axis=0, tiled=True,
        )
        return back.reshape(slots, sub_w)

    back_out = to_sections(out_loc)
    back_dx = to_sections(dx_loc)

    mixed_sub = None
    for k, pick in enumerate(picks):
        picked = jnp.dot(pick.astype(bf16).T, back_out, preferred_element_type=f32)
        term = gates[:, k][:, None] * picked
        mixed_sub = term if mixed_sub is None else mixed_sub + term
    dx_sub = jnp.dot(dispatch_mat.T, back_dx, preferred_element_type=f32)

    def finish(sub):
        pieces = [sub[:, p * slice_w:(p + 1) * slice_w] for p in range(EXP_DEV)]
        keep = pick_by(half, pieces)
        give = pick_by((half + 1) % EXP_DEV, pieces)
        return (keep + lax.ppermute(give, "exp", half_swap)).astype(bf16)

    mixed = finish(mixed_sub)
    grad_patches = finish(dx_sub)
    grad_up = jnp.transpose(grad_up.reshape(model_width, n_loc, hid_loc), (1, 0, 2))
    grad_down = grad_down.reshape(n_loc, hid_loc, model_width)
    return (mixed, grad_patches, grad_up, grad_down)


def solution(mesh):
    return jax.shard_map(
        on_device,
        mesh=mesh,
        in_specs=(
            P("attn", "exp"),
            P("attn", "exp"),
            P("attn", None),
            P("attn", None),
            P(("attn", "exp"), None, None),
            P(("attn", "exp"), None, None),
        ),
        out_specs=(
            P("attn", "exp"),
            P("attn", "exp"),
            P(("attn", "exp"), None, None),
            P(("attn", "exp"), None, None),
        ),
        check_vma=False,
    )
```

profile of v0, /device:TPU:0, one launch (start us, length us, event | category | flops | bytes accessed | tf_op | source)
XLA Modules:
  0.0 242.2 jit_solution(16690531847905804068)
XLA Ops:
  0.7 3.0 %collective-permute-start = (bf16[192,1024]{1,0:T(8,128)(2,1)}, bf16[192,1024]{1,0:T(8,128)(2,1)S(1)}, u32[]{:S(2)}, u32[]{:S(2)}) collective-permute-start(bf16[192,1024]{1,0:T(8,128)(2,1)} %param.6), channel_id=1, source_target_pairs={{0,2},{1,3},{2,0},{3,1},{4,6},{5,7},{6,4},{7,5},{8,10},{9,11},{10,... | collective-permute-start | bytes 1179656 | tf_op jit(solution)/shard_map/ppermute | solution.py:49
  3.7 0.1 collective-permute-start.4
  3.7 0.7 broadcast_compare_fusion
  4.4 0.8 copy.30
  5.2 0.1 eq.102
  5.4 0.1 eq.106
  5.5 0.2 copy.35
  5.7 0.9 reduce-window.6
  6.6 0.2 slice_reduce_fusion.4
  6.9 0.2 slice_reduce_fusion.3
  7.1 0.1 fusion.54
  7.2 0.1 reshape.68
  7.4 0.2 slice_reduce_fusion.1
  7.6 6.2 %collective-permute-done = bf16[192,1024]{1,0:T(8,128)(2,1)S(1)} collective-permute-done((bf16[192,1024]{1,0:T(8,128)(2,1)}, bf16[192,1024]{1,0:T(8,128)(2,1)S(1)}, u32[]{:S(2)}, u32[]{:S(2)}) %collective-permute-start) | collective-permute-done | bytes 393248 | tf_op jit(solution)/shard_map/ppermute | solution.py:49
  13.8 7.6 %collective-permute-done.4 = bf16[192,1024]{1,0:T(8,128)(2,1)S(1)} collective-permute-done((bf16[192,1024]{1,0:T(8,128)(2,1)}, bf16[192,1024]{1,0:T(8,128)(2,1)S(1)}, u32[]{:S(2)}, u32[]{:S(2)}) %collective-permute-start.4) | collective-permute-done | bytes 393248 | tf_op jit(solution)/shard_map/ppermute | solution.py:49
  21.4 0.1 broadcast_select_fusion.5
  21.5 1.9 convolution_convert_fusion
  23.4 6.2 %all-to-all-start = ((bf16[8,48,2048]{2,1,0:T(8,128)(2,1)}), bf16[8,48,2048]{2,1,0:T(8,128)(2,1)S(1)}, u32[]{:S(2)}, u32[]{:S(2)}) async-start(bf16[8,48,2048]{2,1,0:T(8,128)(2,1)} %bitcast.2), calls=%async_computation | async-start | bytes 3145728 | tf_op jit(solution)/shard_map/all_to_all | solution.py:84
  29.7 0.2 select_reduce_fusion.1
  29.8 0.2 select_reduce_fusion
  30.0 1.9 multiply_convert_fusion
  31.9 34.0 %all-to-all-done = bf16[8,48,2048]{2,1,0:T(8,128)(2,1)S(1)} async-done(((bf16[8,48,2048]{2,1,0:T(8,128)(2,1)}), bf16[8,48,2048]{2,1,0:T(8,128)(2,1)S(1)}, u32[]{:S(2)}, u32[]{:S(2)}) %all-to-all-start) | async-done | bytes 1572896 | tf_op jit(solution)/shard_map/all_to_all | solution.py:84
  65.9 3.8 %all-to-all-start.2 = ((bf16[8,48,2048]{2,1,0:T(8,128)(2,1)}), bf16[8,48,2048]{2,1,0:T(8,128)(2,1)S(1)}, u32[]{:S(2)}, u32[]{:S(2)}) async-start(bf16[8,48,2048]{2,1,0:T(8,128)(2,1)} %bitcast.72), calls=%async_computation.2 | async-start | bytes 3145728 | tf_op jit(solution)/shard_map/all_to_all | solution.py:84
  69.7 36.8 %all-to-all-done.2 = bf16[8,48,2048]{2,1,0:T(8,128)(2,1)S(1)} async-done(((bf16[8,48,2048]{2,1,0:T(8,128)(2,1)}), bf16[8,48,2048]{2,1,0:T(8,128)(2,1)S(1)}, u32[]{:S(2)}, u32[]{:S(2)}) %all-to-all-start.2) | async-done | bytes 1572896 | tf_op jit(solution)/shard_map/all_to_all | solution.py:84
  106.6 1.6 broadcast_select_fusion.3
  108.2 0.1 fusion.70
  108.3 0.1 fusion.71
  108.5 1.6 collective-permute-done.5
  110.1 2.4 broadcast_select_fusion.2
  112.5 0.1 fusion.68
  112.7 0.1 fusion.69
  112.9 2.6 %fusion.6 = f32[384,768]{1,0:T(8,128)S(1)} fusion(bf16[1,4096,768]{2,1,0:T(8,128)(2,1)S(1)} %bitcast.79, bf16[384,1024]{1,0:T(8,128)(2,1)S(1)} %get-tuple-element.27, bf16[384,1024]{1,0:T(8,128)(2,1)S(1)} %get-tuple-element.25, bf16[384,1024]{1,0:T(8,128)(2,1)S(1)} %get-tuple-element.26, bf16[384,1024]{1,0:T(8,128)(2,1)S(1)} %get-tuple-element.24), kind=kOutput, calls=%fused_computation.8 | convolution fusion | flops 2428502016 | bytes 10616832 | tf_op jit(solution)/shard_map/dot_general | solution.py:103
  115.6 0.4 slice-done.2
  116.0 0.8 slice-done.3
  116.8 3.1 %fusion.24 = bf16[384,768]{1,0:T(8,128)(2,1)S(1)} fusion(bf16[1,768,4096]{2,1,0:T(8,128)(2,1)S(1)} %bitcast.81, f32[384,768]{1,0:T(8,128)S(1)} %fusion.6, bf16[384,1024]{1,0:T(8,128)(2,1)S(1)} %get-tuple-element.23, bf16[384,1024]{1,0:T(8,128)(2,1)S(1)} %get-tuple-element.21, bf16[384,1024]{1,0:T(8,128)(2,1)S(1)} %get-tuple-element.22, ...), kind=kOutput, calls=%fused_computation.36 | convolution fusion | flops 2434105344 | bytes 11206656 | tf_op jit(solution)/shard_map/sd,hd->sh/dot_general | solution.py:106
  120.0 2.6 %fusion.11 = f32[384,4096]{1,0:T(8,128)S(1)} fusion(bf16[384,768]{1,0:T(8,128)(2,1)S(1)} %fusion.24, bf16[1,4096,768]{2,1,0:T(8,128)(2,1)S(1)} %bitcast.79), kind=kOutput, calls=%fused_computation.11 | convolution fusion | flops 2419064832 | bytes 13172736 | tf_op jit(solution)/shard_map/sh,dh->sd/dot_general | solution.py:116
  122.6 0.8 fusion.66
  123.5 1.9 select_convert_fusion
  125.3 0.3 copy-done.2
  125.6 0.1 collective-permute-start.6
  125.7 8.7 %fusion.17 = f32[384,4096]{1,0:T(8,128)} fusion(bf16[1,768,4096]{2,1,0:T(8,128)(2,1)} %param.11, f32[384,768]{1,0:T(8,128)} %copy-done.10), kind=kOutput, calls=%fused_computation.13 | convolution fusion | flops 2421719040 | bytes 13762560 | tf_op jit(solution)/shard_map/dot_general | solution.py:115
  134.4 3.6 %add_convert_fusion = bf16[384,2048]{1,0:T(8,128)(2,1)} fusion(bf16[384,2048]{1,0:T(8,128)(2,1)} %collective-permute-done.6, f32[384,1024]{1,0:T(8,128)S(1)} %get-tuple-element.9, f32[384,1024]{1,0:T(8,128)S(1)} %copy-done.1, f32[384,1024]{1,0:T(8,128)S(1)} %copy-done.3, f32[384,1024]{1,0:T(8,128)S(1)} %get-tuple-element.8, pred[]{:T(512)S(6)} %eq.116), kind=kLoop, calls=%fused_computation.20 | loop fusion | flops 4718592 | bytes 9437185 | tf_op jit(solution)/shard_map/convert_element_type | solution.py:136
  138.0 3.6 %all-to-all-start.3 = ((bf16[8,48,2048]{2,1,0:T(8,128)(2,1)}), bf16[8,48,2048]{2,1,0:T(8,128)(2,1)S(1)}, u32[]{:S(2)}, u32[]{:S(2)}) async-start(bf16[8,48,2048]{2,1,0:T(8,128)(2,1)} %bitcast.69), calls=%async_computation.3 | async-start | bytes 3145728 | tf_op jit(solution)/shard_map/all_to_all | solution.py:135
  141.7 3.4 %fusion.67 = (f32[384,1024]{1,0:T(8,128)S(1)}, f32[384,1024]{1,0:T(8,128)S(1)}, f32[384,1024]{1,0:T(8,128)S(1)}, f32[384,1024]{1,0:T(8,128)S(1)}) fusion(f32[384,4096]{1,0:T(8,128)} %fusion.17), kind=kLoop, calls=%fused_computation.101 | loop fusion | bytes 12582912 | tf_op jit(solution)/shard_map/slice | solution.py:125
  145.1 0.7 select_convert_fusion.1
  145.8 0.5 collective-permute-start.2
  146.2 3.0 %collective-permute-done.2 = bf16[384,2048]{1,0:T(8,128)(2,1)S(1)} collective-permute-done((bf16[384,2048]{1,0:T(8,128)(2,1)S(1)}, bf16[384,2048]{1,0:T(8,128)(2,1)S(1)}, u32[]{:S(2)}, u32[]{:S(2)}) %collective-permute-start.2) | collective-permute-done | bytes 1572896 | tf_op jit(solution)/shard_map/ppermute | solution.py:133
  149.2 2.0 add_convert_fusion.1
  151.3 28.1 %all-to-all-done.3 = bf16[8,48,2048]{2,1,0:T(8,128)(2,1)S(1)} async-done(((bf16[8,48,2048]{2,1,0:T(8,128)(2,1)}), bf16[8,48,2048]{2,1,0:T(8,128)(2,1)S(1)}, u32[]{:S(2)}, u32[]{:S(2)}) %all-to-all-start.3) | async-done | bytes 1572896 | tf_op jit(solution)/shard_map/all_to_all | solution.py:135
  179.4 1.2 copy-done.4
  180.6 3.6 %all-to-all-start.1 = ((bf16[8,48,2048]{2,1,0:T(8,128)(2,1)}), bf16[8,48,2048]{2,1,0:T(8,128)(2,1)S(1)}, u32[]{:S(2)}, u32[]{:S(2)}) async-start(bf16[8,48,2048]{2,1,0:T(8,128)(2,1)} %bitcast.68), calls=%async_computation.1 | async-start | bytes 3145728 | tf_op jit(solution)/shard_map/all_to_all | solution.py:135
  184.2 10.7 %convolution_bitcast_fusion = f32[1,768,4096]{2,1,0:T(8,128)} fusion(bf16[384,1024]{1,0:T(8,128)(2,1)} %copy-done.9, bf16[384,1024]{1,0:T(8,128)(2,1)} %copy-done.7, bf16[384,1024]{1,0:T(8,128)(2,1)} %copy-done.8, bf16[384,1024]{1,0:T(8,128)(2,1)} %copy-done.6, f32[384,768]{1,0:T(8,128)} %copy-done.10), kind=kOutput, calls=%fused_computation | convolution fusion | flops 2431156224 | bytes 16908288 | tf_op jit(solution)/shard_map/sh,sd->hd/dot_general | solution.py:108
  194.9 0.6 fusion.62
  195.6 1.0 slice_select_fusion
  196.6 1.5 collective-permute-start.7
  198.1 23.4 %all-to-all-done.1 = bf16[8,48,2048]{2,1,0:T(8,128)(2,1)S(1)} async-done(((bf16[8,48,2048]{2,1,0:T(8,128)(2,1)}), bf16[8,48,2048]{2,1,0:T(8,128)(2,1)S(1)}, u32[]{:S(2)}, u32[]{:S(2)}) %all-to-all-start.1) | async-done | bytes 1572896 | tf_op jit(solution)/shard_map/all_to_all | solution.py:135
  221.4 0.6 convolution_multiply_fusion.1
  222.1 0.6 fusion.20
  222.8 0.1 slice_select_fusion.1
  222.9 1.6 collective-permute-start.3
  224.5 7.5 %convolution_bitcast_fusion.1 = f32[1,4096,768]{2,1,0:T(8,128)} fusion(bf16[384,768]{1,0:T(8,128)(2,1)S(1)} %copy-done.23, bf16[384,1024]{1,0:T(8,128)(2,1)S(1)} %copy-done.18, bf16[384,1024]{1,0:T(8,128)(2,1)S(1)} %copy-done.14, bf16[384,1024]{1,0:T(8,128)(2,1)S(1)} %copy-done.16, bf16[384,1024]{1,0:T(8,128)(2,1)S(1)} %copy-done.12), kind=kOutput, calls=%fused_computation.1 | convolution fusion | flops 2428502016 | bytes 16318464 | tf_op jit(solution)/shard_map/sd,sh->dh/dot_general | solution.py:109
  232.0 2.0 add_convert_fusion.2
  234.0 7.3 %collective-permute-done.3 = f32[192,1024]{1,0:T(8,128)S(1)} collective-permute-done((f32[192,1024]{1,0:T(8,128)S(1)}, f32[192,1024]{1,0:T(8,128)S(1)}, u32[]{:S(2)}, u32[]{:S(2)}) %collective-permute-start.3) | collective-permute-done | bytes 786464 | tf_op jit(solution)/shard_map/ppermute | solution.py:155
  241.3 0.9 add_convert_fusion.3
  (65 shorter events, 0.4 us)
Async XLA Ops:
  0.6 20.8 %copy-start.20 = (bf16[192,1024]{1,0:T(8,128)(2,1)S(1)}, bf16[192,1024]{1,0:T(8,128)(2,1)}, u32[]{:S(2)}) copy-start(bf16[192,1024]{1,0:T(8,128)(2,1)} %param.6) | copy-start | bytes 1179652
  0.6 20.8 %copy-start.19 = (bf16[192,1024]{1,0:T(8,128)(2,1)S(1)}, bf16[192,1024]{1,0:T(8,128)(2,1)}, u32[]{:S(2)}) copy-start(bf16[192,1024]{1,0:T(8,128)(2,1)} %param.7) | copy-start | bytes 1179652
  0.7 13.2 %collective-permute-start = (bf16[192,1024]{1,0:T(8,128)(2,1)}, bf16[192,1024]{1,0:T(8,128)(2,1)S(1)}, u32[]{:S(2)}, u32[]{:S(2)}) collective-permute-start(bf16[192,1024]{1,0:T(8,128)(2,1)} %param.6), channel_id=1, source_target_pairs={{0,2},{1,3},{2,0},{3,1},{4,6},{5,7},{6,4},{7,5},{8,10},{9,11},{10,... | collective-permute-start | bytes 1179656 | tf_op jit(solution)/shard_map/ppermute | solution.py:49
  3.7 17.8 %collective-permute-start.4 = (bf16[192,1024]{1,0:T(8,128)(2,1)}, bf16[192,1024]{1,0:T(8,128)(2,1)S(1)}, u32[]{:S(2)}, u32[]{:S(2)}) collective-permute-start(bf16[192,1024]{1,0:T(8,128)(2,1)} %param.7), channel_id=1, source_target_pairs={{0,2},{1,3},{2,0},{3,1},{4,6},{5,7},{6,4},{7,5},{8,10},{9,11},{10,... | collective-permute-start | bytes 1179656 | tf_op jit(solution)/shard_map/ppermute | solution.py:49
  23.4 6.2 %copy-start.21 = (f32[192,2]{0,1:T(2,128)S(1)}, f32[192,2]{0,1:T(2,128)}, u32[]{:S(2)}) copy-start(f32[192,2]{0,1:T(2,128)} %param.9) | copy-start | bytes 4612
  23.4 42.4 %all-to-all-start = ((bf16[8,48,2048]{2,1,0:T(8,128)(2,1)}), bf16[8,48,2048]{2,1,0:T(8,128)(2,1)S(1)}, u32[]{:S(2)}, u32[]{:S(2)}) async-start(bf16[8,48,2048]{2,1,0:T(8,128)(2,1)} %bitcast.2), calls=%async_computation | async-start | bytes 3145728 | tf_op jit(solution)/shard_map/all_to_all | solution.py:84
  65.9 40.7 %all-to-all-start.2 = ((bf16[8,48,2048]{2,1,0:T(8,128)(2,1)}), bf16[8,48,2048]{2,1,0:T(8,128)(2,1)S(1)}, u32[]{:S(2)}, u32[]{:S(2)}) async-start(bf16[8,48,2048]{2,1,0:T(8,128)(2,1)} %bitcast.72), calls=%async_computation.2 | async-start | bytes 3145728 | tf_op jit(solution)/shard_map/all_to_all | solution.py:84
  69.6 36.9 %collective-permute-start.1 = (bf16[384,2048]{1,0:T(8,128)(2,1)S(1)}, bf16[384,2048]{1,0:T(8,128)(2,1)}, u32[]{:S(2)}, u32[]{:S(2)}) collective-permute-start(bf16[384,2048]{1,0:T(8,128)(2,1)S(1)} %bitcast.70), channel_id=1, source_target_pairs={{0,1},{1,0},{2,3},{3,2},{4,5},{5,4},{6,7},{7,6},{8,9},{9,8},{10,11... | collective-permute-start | bytes 4718600 | tf_op jit(solution)/shard_map/ppermute | solution.py:87
  106.6 3.5 %collective-permute-start.5 = (bf16[384,2048]{1,0:T(8,128)(2,1)S(1)}, bf16[384,2048]{1,0:T(8,128)(2,1)}, u32[]{:S(2)}, u32[]{:S(2)}) collective-permute-start(bf16[384,2048]{1,0:T(8,128)(2,1)S(1)} %bitcast.71), channel_id=1, source_target_pairs={{0,1},{1,0},{2,3},{3,2},{4,5},{5,4},{6,7},{7,6},{8,9},{9,8},{10,11... | collective-permute-start | bytes 4718600 | tf_op jit(solution)/shard_map/ppermute | solution.py:87
  108.3 4.5 %copy-start.11 = (bf16[384,1024]{1,0:T(8,128)(2,1)}, bf16[384,1024]{1,0:T(8,128)(2,1)S(1)}, u32[]{:S(2)}) copy-start(bf16[384,1024]{1,0:T(8,128)(2,1)S(1)} %get-tuple-element.24) | copy-start | bytes 2359300
  108.3 4.5 %copy-start.13 = (bf16[384,1024]{1,0:T(8,128)(2,1)}, bf16[384,1024]{1,0:T(8,128)(2,1)S(1)}, u32[]{:S(2)}) copy-start(bf16[384,1024]{1,0:T(8,128)(2,1)S(1)} %get-tuple-element.25) | copy-start | bytes 2359300
  108.3 4.5 %slice-start = ((s8[6291456]{0:T(1024)(128)(4,1)}), s8[4194304]{0:T(1024)(128)(4,1)S(1)}, s32[]{:S(2)}) async-start(s8[6291456]{0:T(1024)(128)(4,1)} %bitcast.78), calls=%async_computation.4 | async-start | bytes 8388608
  108.5 4.4 %copy-start.15 = (bf16[384,1024]{1,0:T(8,128)(2,1)}, bf16[384,1024]{1,0:T(8,128)(2,1)S(1)}, u32[]{:S(2)}) copy-start(bf16[384,1024]{1,0:T(8,128)(2,1)S(1)} %get-tuple-element.26) | copy-start | bytes 2359300
  108.5 4.4 %copy-start.17 = (bf16[384,1024]{1,0:T(8,128)(2,1)}, bf16[384,1024]{1,0:T(8,128)(2,1)S(1)}, u32[]{:S(2)}) copy-start(bf16[384,1024]{1,0:T(8,128)(2,1)S(1)} %get-tuple-element.27) | copy-start | bytes 2359300
  108.5 4.4 %slice-start.1 = ((s8[6291456]{0:T(1024)(128)(4,1)}), s8[2097152]{0:T(1024)(128)(4,1)S(1)}, s32[]{:S(2)}) async-start(s8[6291456]{0:T(1024)(128)(4,1)} %bitcast.78), calls=%async_computation.5 | async-start | bytes 4194304
  112.7 2.9 %copy-start.6 = (bf16[384,1024]{1,0:T(8,128)(2,1)}, bf16[384,1024]{1,0:T(8,128)(2,1)S(1)}, u32[]{:S(2)}) copy-start(bf16[384,1024]{1,0:T(8,128)(2,1)S(1)} %get-tuple-element.20) | copy-start | bytes 2359300
  112.7 2.9 %copy-start.7 = (bf16[384,1024]{1,0:T(8,128)(2,1)}, bf16[384,1024]{1,0:T(8,128)(2,1)S(1)}, u32[]{:S(2)}) copy-start(bf16[384,1024]{1,0:T(8,128)(2,1)S(1)} %get-tuple-element.21) | copy-start | bytes 2359300
  112.7 3.4 %slice-start.2 = ((s8[6291456]{0:T(1024)(128)(4,1)}), s8[4194304]{0:T(1024)(128)(4,1)S(1)}, s32[]{:S(2)}) async-start(s8[6291456]{0:T(1024)(128)(4,1)} %bitcast.80), calls=%async_computation.6 | async-start | bytes 8388608
  112.8 2.7 %copy-start.8 = (bf16[384,1024]{1,0:T(8,128)(2,1)}, bf16[384,1024]{1,0:T(8,128)(2,1)S(1)}, u32[]{:S(2)}) copy-start(bf16[384,1024]{1,0:T(8,128)(2,1)S(1)} %get-tuple-element.22) | copy-start | bytes 2359300
  112.8 2.7 %copy-start.9 = (bf16[384,1024]{1,0:T(8,128)(2,1)}, bf16[384,1024]{1,0:T(8,128)(2,1)S(1)}, u32[]{:S(2)}) copy-start(bf16[384,1024]{1,0:T(8,128)(2,1)S(1)} %get-tuple-element.23) | copy-start | bytes 2359300
  112.9 3.9 %slice-start.3 = ((s8[6291456]{0:T(1024)(128)(4,1)}), s8[2097152]{0:T(1024)(128)(4,1)S(1)}, s32[]{:S(2)}) async-start(s8[6291456]{0:T(1024)(128)(4,1)} %bitcast.80), calls=%async_computation.7 | async-start | bytes 4194304
  115.5 4.4 %copy-start.10 = (f32[384,768]{1,0:T(8,128)}, f32[384,768]{1,0:T(8,128)S(1)}, u32[]{:S(2)}) copy-start(f32[384,768]{1,0:T(8,128)S(1)} %fusion.6) | copy-start | bytes 3538948
  120.0 2.7 %copy-start.22 = (bf16[384,768]{1,0:T(8,128)(2,1)}, bf16[384,768]{1,0:T(8,128)(2,1)S(1)}, u32[]{:S(2)}) copy-start(bf16[384,768]{1,0:T(8,128)(2,1)S(1)} %fusion.24) | copy-start | bytes 1769476
  123.5 1.9 copy-start
  123.5 2.1 copy-start.2
  125.6 8.8 %collective-permute-start.6 = (bf16[384,2048]{1,0:T(8,128)(2,1)}, bf16[384,2048]{1,0:T(8,128)(2,1)}, u32[]{:S(2)}, u32[]{:S(2)}) collective-permute-start(bf16[384,2048]{1,0:T(8,128)(2,1)} %select_convert_fusion), channel_id=1, source_target_pairs={{0,1},{1,0},{2,3},{3,2},{4,5},{5,4},{6,7},{7,6},{8,9},{9,8},{10,11... | collective-permute-start | bytes 4718600 | tf_op jit(solution)/shard_map/ppermute | solution.py:133
  125.7 8.7 %copy-start.1 = (f32[384,1024]{1,0:T(8,128)S(1)}, f32[384,1024]{1,0:T(8,128)}, u32[]{:S(2)}) copy-start(f32[384,1024]{1,0:T(8,128)} %copy-done) | copy-start | bytes 4718596
  125.7 8.7 %copy-start.3 = (f32[384,1024]{1,0:T(8,128)S(1)}, f32[384,1024]{1,0:T(8,128)}, u32[]{:S(2)}) copy-start(f32[384,1024]{1,0:T(8,128)} %copy-done.2) | copy-start | bytes 4718596
  138.0 41.4 %all-to-all-start.3 = ((bf16[8,48,2048]{2,1,0:T(8,128)(2,1)}), bf16[8,48,2048]{2,1,0:T(8,128)(2,1)S(1)}, u32[]{:S(2)}, u32[]{:S(2)}) async-start(bf16[8,48,2048]{2,1,0:T(8,128)(2,1)} %bitcast.69), calls=%async_computation.3 | async-start | bytes 3145728 | tf_op jit(solution)/shard_map/all_to_all | solution.py:135
  145.8 3.5 %collective-permute-start.2 = (bf16[384,2048]{1,0:T(8,128)(2,1)S(1)}, bf16[384,2048]{1,0:T(8,128)(2,1)S(1)}, u32[]{:S(2)}, u32[]{:S(2)}) collective-permute-start(bf16[384,2048]{1,0:T(8,128)(2,1)S(1)} %select_convert_fusion.1), channel_id=1, source_target_pairs={{0,1},{1,0},{2,3},{3,2},{4,5},{5,4},{6,7},{7,6},{8,9},{9,8},{10,11... | collective-permute-start | bytes 4718600 | tf_op jit(solution)/shard_map/ppermute | solution.py:133
  179.4 1.2 copy-start.4
  180.6 40.8 %all-to-all-start.1 = ((bf16[8,48,2048]{2,1,0:T(8,128)(2,1)}), bf16[8,48,2048]{2,1,0:T(8,128)(2,1)S(1)}, u32[]{:S(2)}, u32[]{:S(2)}) async-start(bf16[8,48,2048]{2,1,0:T(8,128)(2,1)} %bitcast.68), calls=%async_computation.1 | async-start | bytes 3145728 | tf_op jit(solution)/shard_map/all_to_all | solution.py:135
  184.2 10.7 %copy-start.5 = (bf16[8,48,2048]{2,1,0:T(8,128)(2,1)S(1)}, bf16[8,48,2048]{2,1,0:T(8,128)(2,1)}, u32[]{:S(2)}) copy-start(bf16[8,48,2048]{2,1,0:T(8,128)(2,1)} %copy-done.4) | copy-start | bytes 4718596
  196.6 35.4 %collective-permute-start.7 = (f32[192,1024]{1,0:T(8,128)}, f32[192,1024]{1,0:T(8,128)}, u32[]{:S(2)}, u32[]{:S(2)}) collective-permute-start(f32[192,1024]{1,0:T(8,128)} %slice_select_fusion), channel_id=1, source_target_pairs={{0,2},{1,3},{2,0},{3,1},{4,6},{5,7},{6,4},{7,5},{8,10},{9,11},{10,... | collective-permute-start | bytes 2359304 | tf_op jit(solution)/shard_map/ppermute | solution.py:155
  222.1 2.4 copy-start.18
  222.1 2.4 copy-start.23
  222.7 1.7 copy-start.12
  222.7 1.7 copy-start.14
  222.8 1.7 copy-start.16
  222.9 18.4 %collective-permute-start.3 = (f32[192,1024]{1,0:T(8,128)S(1)}, f32[192,1024]{1,0:T(8,128)S(1)}, u32[]{:S(2)}, u32[]{:S(2)}) collective-permute-start(f32[192,1024]{1,0:T(8,128)S(1)} %slice_select_fusion.1), channel_id=1, source_target_pairs={{0,2},{1,3},{2,0},{3,1},{4,6},{5,7},{6,4},{7,5},{8,10},{9,11},{10,... | collective-permute-start | bytes 2359304 | tf_op jit(solution)/shard_map/ppermute | solution.py:155
where the time goes:
time: 243 us; the launch traced here: 242 us
  waiting for transfers between devices  148 us (61%)
  matrix products  41 us (17%)
  starting transfers between devices  24 us (10%)
  other arithmetic  18.5 us (8%)
  local copies, waits for them, and re-layouts  9.51 us (4%)
    all_to_all x2, waiting for transfers between devices, to_experts(): lax.all_to_all(buf.reshape(sections, capacity, sub_w), 'attn', split_axis...  70.8 us
    all_to_all x2, waiting for transfers between devices, to_sections(): lax.all_to_all(summed.astype(bf16).reshape(sections, capacity, sub_w), 'a...  51.5 us
    ppermute x2, waiting for transfers between devices, core_subset(): other = lax.ppermute(local, 'exp', half_swap)  13.8 us
    dot_general x1, matrix products, on_device(): jnp.einsum('sh,sd->hd', activation, d_rows, preferred_element_type=f32)  10.7 us
    all_to_all x2, starting transfers between devices, to_experts(): lax.all_to_all(buf.reshape(sections, capacity, sub_w), 'attn', split_axis...  9.98 us
    dot_general x1, matrix products, on_device(): out_g = jnp.dot(activation[:, part], w_down[g], preferred_element_type=f32)  8.7 us
    dot_general x1, matrix products, on_device(): jnp.einsum('sd,sh->dh', x_rows, grad_pre, preferred_element_type=f32)  7.55 us
    ppermute x2, waiting for transfers between devices, finish(): return (keep + lax.ppermute(give, 'exp', half_swap)).astype(bf16)  7.29 us
  transfers between devices with their start and end apart: 12, of which 9 were waited for; matrix products, arithmetic and copies ran while one was open for 19% of the time, Pallas kernels for 0%

commit v1 on v0

--- a/solution.py
+++ b/solution.py
@@ -53,7 +53,6 @@
         )
 
     sub_x = core_subset(patches)
-    sub_dy = core_subset(grad_out)
 
     local_slot = route_slots(route_ids, experts, capacity)
     owned = (route_ids % EXP_DEV) == half
@@ -71,6 +70,8 @@
     dispatch_mat = dispatch.astype(bf16)
 
     x_buf = jnp.dot(dispatch_mat, sub_x, preferred_element_type=f32).astype(bf16)
+    grad_out, x_buf = lax.optimization_barrier((grad_out, x_buf))
+    sub_dy = core_subset(grad_out)
     dy_buf = jnp.dot(dispatch_mat, sub_dy, preferred_element_type=f32)
     d_buf = (gate_slot[:, None] * dy_buf).astype(bf16)
 
@@ -92,6 +93,7 @@
         )
 
     x_rows = to_experts(x_buf)
+    d_buf, x_rows = lax.optimization_barrier((d_buf, x_rows))
     d_rows = to_experts(d_buf)
 
     if n_loc == 1:
@@ -105,8 +107,6 @@
     activation = gelu_value.astype(bf16)
     grad_act = jnp.einsum("sd,hd->sh", d_rows, down_mat, preferred_element_type=f32)
     grad_pre = (grad_act * gelu_slope).astype(bf16)
-    grad_down = jnp.einsum("sh,sd->hd", activation, d_rows, preferred_element_type=f32)
-    grad_up = jnp.einsum("sd,sh->dh", x_rows, grad_pre, preferred_element_type=f32)
 
     out_loc = None
     dx_loc = None
@@ -119,7 +119,7 @@
         out_loc = out_g if out_loc is None else out_loc + out_g
         dx_loc = dx_g if dx_loc is None else dx_loc + dx_g
 
-    def to_sections(rows):
+    def to_sections(rows, hold):
         subsets = [
             jnp.concatenate(
                 [rows[:, (p * cores + q) * slice_w:(p * cores + q + 1) * slice_w] for p in range(EXP_DEV)],
@@ -132,14 +132,16 @@
             theirs = pick_by((core + s) % cores, subsets)
             got = lax.ppermute(theirs.astype(bf16), "exp", core_shift(s))
             summed = summed + got.astype(f32)
+        sent, hold = lax.optimization_barrier((summed.astype(bf16), hold))
         back = lax.all_to_all(
-            summed.astype(bf16).reshape(sections, capacity, sub_w),
-            "attn", split_axis=0, concat_axis=0, tiled=True,
+            sent.reshape(sections, capacity, sub_w), "attn", split_axis=0, concat_axis=0, tiled=True
         )
-        return back.reshape(slots, sub_w)
+        return back.reshape(slots, sub_w), hold
 
-    back_out = to_sections(out_loc)
-    back_dx = to_sections(dx_loc)
+    back_out, (act_late, d_late) = to_sections(out_loc, (activation, d_rows))
+    grad_down = jnp.einsum("sh,sd->hd", act_late, d_late, preferred_element_type=f32)
+    back_dx, (x_late, pre_late) = to_sections(dx_loc, (x_rows, grad_pre))
+    grad_up = jnp.einsum("sd,sh->dh", x_late, pre_late, preferred_element_type=f32)
 
     mixed_sub = None
     for k, pick in enumerate(picks):

time: 243 us -> 238 us (0.979)
  waiting for transfers between devices: 148 us -> 96.5 us
  blocking collectives: 0 us -> 42.2 us
  other arithmetic: 18.5 us -> 22.4 us
  local copies, waits for them, and re-layouts: 9.51 us -> 12.5 us
  starting transfers between devices: 24 us -> 21.5 us
    all_to_all x2 -> x1, waiting for transfers between devices: 70.8 us -> 20.6 us  [to_experts(): lax.all_to_all(buf.reshape(sections, capacity, sub_w), 'attn', split_axis...]
    all_to_all x0 -> x1, blocking collectives: none -> 42.2 us  [to_experts(): lax.all_to_all(buf.reshape(sections, capacity, sub_w), 'attn', split_axis...]
    all_to_all x2, waiting for transfers between devices: 51.5 us -> 57.4 us  [to_sections(): lax.all_to_all(sent.reshape(sections, capacity, sub_w), 'attn', split_axi...]
    ppermute x2, waiting for transfers between devices: 7.29 us -> 1.58 us  [finish(): return (keep + lax.ppermute(give, 'exp', half_swap)).astype(bf16)]
    all_to_all x2 -> x1, starting transfers between devices: 9.98 us -> 4.49 us  [to_experts(): lax.all_to_all(buf.reshape(sections, capacity, sub_w), 'attn', split_axis...]
    dot_general x2, matrix products: 18.2 us -> 13.2 us  [the longest x1 6.61 us: on_device(): jnp.einsum('sd,sh->dh', x_late, pre_late, preferred_element_type=f32)]
    dot_general x1, matrix products: 8.7 us -> 4.75 us  [on_device(): out_g = jnp.dot(activation[:, part], w_down[g], preferred_element_type=f32)]
    dot_general x1, matrix products: 2.6 us -> 6.47 us  [on_device(): pre_act = jnp.dot(x_rows, up_mat, preferred_element_type=f32)]
  transfers between devices with their start and end apart: 12 -> 11, of which waited for: 9 -> 7; matrix products, arithmetic and copies ran while one was open for 19% -> 24% of each run, Pallas kernels for 0% -> 0%
where the time goes in v1:
time: 238 us
  waiting for transfers between devices  96.5 us (41%)
  blocking collectives  42.2 us (18%)
  matrix products  41.7 us (18%)
  other arithmetic  22.4 us (9%)
  starting transfers between devices  21.5 us (9%)
  local copies, waits for them, and re-layouts  12.5 us (5%)
    all_to_all x2, waiting for transfers between devices, to_sections(): lax.all_to_all(sent.reshape(sections, capacity, sub_w), 'attn', split_axi...  57.4 us
    all_to_all x1, blocking collectives, to_experts(): lax.all_to_all(buf.reshape(sections, capacity, sub_w), 'attn', split_axis...  42.2 us
    all_to_all x1, waiting for transfers between devices, to_experts(): lax.all_to_all(buf.reshape(sections, capacity, sub_w), 'attn', split_axis...  20.6 us
    ppermute x2, waiting for transfers between devices, core_subset(): other = lax.ppermute(local, 'exp', half_swap)  13.8 us
    all_to_all x2, starting transfers between devices, to_sections(): lax.all_to_all(sent.reshape(sections, capacity, sub_w), 'attn', split_axi...  8.95 us
    convert_element_type x2, other arithmetic, to_sections(): sent, hold = lax.optimization_barrier((summed.astype(bf16), hold))  7.3 us
    dot_general x1, matrix products, on_device(): jnp.einsum('sd,sh->dh', x_late, pre_late, preferred_element_type=f32)  6.61 us
    dot_general x1, matrix products, on_device(): jnp.einsum('sh,sd->hd', act_late, d_late, preferred_element_type=f32)  6.6 us
  transfers between devices with their start and end apart: 11, of which 7 were waited for; matrix products, arithmetic and copies ran while one was open for 24% of the time, Pallas kernels for 0%

profile of v1, /device:TPU:0, one launch (start us, length us, event | category | flops | bytes accessed | tf_op | source)
XLA Modules:
  0.0 237.9 jit_solution(8648551464089877427)
XLA Ops:
  0.6 3.0 %collective-permute-start = (bf16[192,1024]{1,0:T(8,128)(2,1)}, bf16[192,1024]{1,0:T(8,128)(2,1)S(1)}, u32[]{:S(2)}, u32[]{:S(2)}) collective-permute-start(bf16[192,1024]{1,0:T(8,128)(2,1)} %param.6), channel_id=1, source_target_pairs={{0,2},{1,3},{2,0},{3,1},{4,6},{5,7},{6,4},{7,5},{8,10},{9,11},{10,... | collective-permute-start | bytes 1179656 | tf_op jit(solution)/shard_map/ppermute | solution.py:49
  3.6 0.7 broadcast_compare_fusion
  4.3 0.8 copy.30
  5.1 0.1 eq.102
  5.3 0.1 eq.106
  5.4 0.2 copy.35
  5.6 0.9 reduce-window.6
  6.5 0.2 slice_reduce_fusion.4
  6.8 0.2 slice_reduce_fusion.2
  7.1 0.1 reshape.68
  7.4 0.2 slice_reduce_fusion
  7.6 5.4 %collective-permute-done = bf16[192,1024]{1,0:T(8,128)(2,1)S(1)} collective-permute-done((bf16[192,1024]{1,0:T(8,128)(2,1)}, bf16[192,1024]{1,0:T(8,128)(2,1)S(1)}, u32[]{:S(2)}, u32[]{:S(2)}) %collective-permute-start) | collective-permute-done | bytes 393248 | tf_op jit(solution)/shard_map/ppermute | solution.py:49
  13.0 0.8 convolution_convert_fusion
  13.8 42.2 %all_to_all.20 = bf16[8,48,2048]{2,1,0:T(8,128)(2,1)S(1)} all-to-all(bf16[8,48,2048]{2,1,0:T(8,128)(2,1)S(1)} %bitcast.78), channel_id=1, replica_groups=mesh['attn'=8,'exp'=4] {'attn'}, dimensions={0} | all-to-all | bytes 3145728 | tf_op jit(solution)/shard_map/all_to_all | solution.py:85
  56.0 1.5 collective-permute-start.1
  57.5 0.8 fusion.68
  58.3 0.9 select_reduce_fusion
  59.2 8.5 %collective-permute-done.1 = bf16[192,1024]{1,0:T(8,128)(2,1)} collective-permute-done((bf16[192,1024]{1,0:T(8,128)(2,1)S(1)}, bf16[192,1024]{1,0:T(8,128)(2,1)}, u32[]{:S(2)}, u32[]{:S(2)}) %collective-permute-start.1) | collective-permute-done | bytes 393248 | tf_op jit(solution)/shard_map/ppermute | solution.py:49
  67.7 1.1 broadcast_select_fusion.5
  68.7 2.6 %multiply_convert_fusion = bf16[384,2048]{1,0:T(8,128)(2,1)} fusion(f32[384]{0:T(512)S(1)} %add.78, bf16[192,1024]{1,0:T(8,128)(2,1)S(1)} %get-tuple-element.49, bf16[192,1024]{1,0:T(8,128)(2,1)S(1)} %get-tuple-element.48, s32[192]{0:T(256)S(1)} %get-tuple-element.24, s32[192]{0:T(256)S(1)} %get-tuple-element.25, pred[192]{0:T(512)(128)(4,1)} %copy-done.13, ...), kind=kOutput, calls=%fused_computation.24 | convolution fusion | flops 305504256 | bytes 2362752 | tf_op jit(solution)/shard_map/dot_general | solution.py:75
  71.3 0.3 broadcast_select_fusion.3
  71.6 0.4 fusion.66
  72.0 0.3 pad_maximum_fusion
  72.3 4.5 %all-to-all-start.1 = ((bf16[8,48,2048]{2,1,0:T(8,128)(2,1)}), bf16[8,48,2048]{2,1,0:T(8,128)(2,1)}, u32[]{:S(2)}, u32[]{:S(2)}) async-start(bf16[8,48,2048]{2,1,0:T(8,128)(2,1)} %bitcast.77), calls=%async_computation.1 | async-start | bytes 3145728 | tf_op jit(solution)/shard_map/all_to_all | solution.py:85
  76.8 6.5 %multiply_convert_fusion.1 = (bf16[384,768]{1,0:T(8,128)(2,1)S(1)}, f32[384,768]{1,0:T(8,128)}) fusion(bf16[384,4096]{1,0:T(8,128)(2,1)S(1)} %pad_maximum_fusion, bf16[1,4096,768]{2,1,0:T(8,128)(2,1)} %param.10), kind=kOutput, calls=%fused_computation.42 | convolution fusion | flops 2418573312 | bytes 11206656 | tf_op jit(solution)/shard_map/dot_general | solution.py:105
  83.3 0.8 copy-done.7
  84.1 4.7 %fusion.17 = f32[384,4096]{1,0:T(8,128)S(1)} fusion(bf16[384,768]{1,0:T(8,128)(2,1)S(1)} %get-tuple-element.22, bf16[1,768,4096]{2,1,0:T(8,128)(2,1)} %param.11), kind=kOutput, calls=%fused_computation.13 | convolution fusion | flops 2419064832 | bytes 13172736 | tf_op jit(solution)/shard_map/dot_general | solution.py:115
  88.9 1.1 fusion.63
  90.0 1.9 select_convert_fusion.1
  92.0 0.2 copy-done.3
  92.1 0.6 copy-done.4
  92.7 0.5 copy-done.5
  93.2 20.6 %all-to-all-done.1 = bf16[8,48,2048]{2,1,0:T(8,128)(2,1)} async-done(((bf16[8,48,2048]{2,1,0:T(8,128)(2,1)}), bf16[8,48,2048]{2,1,0:T(8,128)(2,1)}, u32[]{:S(2)}, u32[]{:S(2)}) %all-to-all-start.1) | async-done | bytes 1572896 | tf_op jit(solution)/shard_map/all_to_all | solution.py:85
  113.8 5.3 %add_convert_fusion.1 = bf16[384,2048]{1,0:T(8,128)(2,1)} fusion(bf16[384,2048]{1,0:T(8,128)(2,1)} %collective-permute-done.3, f32[384,1024]{1,0:T(8,128)} %copy-done.3, f32[384,1024]{1,0:T(8,128)} %copy-done.4, f32[384,1024]{1,0:T(8,128)} %copy-done.5, f32[384,1024]{1,0:T(8,128)} %copy-done.2, pred[]{:T(512)S(6)} %eq.116), kind=kLoop, calls=%fused_computation.22 | loop fusion | flops 4718592 | bytes 9437185 | tf_op jit(solution)/shard_map/convert_element_type | solution.py:135
  119.1 2.2 broadcast_select_fusion.2
  121.3 0.1 fusion.64
  121.5 0.1 fusion.65
  121.7 1.8 pad_maximum_fusion.3
  123.5 0.5 slice-done.1
  123.9 0.7 copy-done.17
  124.7 3.1 %fusion.24 = bf16[384,768]{1,0:T(8,128)(2,1)S(1)} fusion(bf16[1,768,4096]{2,1,0:T(8,128)(2,1)S(1)} %bitcast.73, f32[384,768]{1,0:T(8,128)S(1)} %copy-done.17, bf16[384,1024]{1,0:T(8,128)(2,1)S(1)} %get-tuple-element.43, bf16[384,1024]{1,0:T(8,128)(2,1)S(1)} %get-tuple-element.41, bf16[384,1024]{1,0:T(8,128)(2,1)S(1)} %get-tuple-element.42, ...), kind=kOutput, calls=%fused_computation.36 | convolution fusion | flops 2434105344 | bytes 11206656 | tf_op jit(solution)/shard_map/sd,hd->sh/dot_general | solution.py:108
  127.8 4.5 %fusion.11 = f32[384,4096]{1,0:T(8,128)} fusion(bf16[384,768]{1,0:T(8,128)(2,1)S(1)} %fusion.24, bf16[1,4096,768]{2,1,0:T(8,128)(2,1)S(1)} %bitcast.85), kind=kOutput, calls=%fused_computation.11 | convolution fusion | flops 2419064832 | bytes 13172736 | tf_op jit(solution)/shard_map/sh,dh->sd/dot_general | solution.py:116
  132.4 4.5 %all-to-all-start.2 = ((bf16[8,48,2048]{2,1,0:T(8,128)(2,1)}), bf16[8,48,2048]{2,1,0:T(8,128)(2,1)}, u32[]{:S(2)}, u32[]{:S(2)}) async-start(bf16[8,48,2048]{2,1,0:T(8,128)(2,1)} %bitcast.74), calls=%async_computation.2 | async-start | bytes 3145728 | tf_op jit(solution)/shard_map/all_to_all | solution.py:136
  136.9 3.4 %fusion.62 = (f32[384,1024]{1,0:T(8,128)S(1)}, f32[384,1024]{1,0:T(8,128)S(1)}, f32[384,1024]{1,0:T(8,128)S(1)}, f32[384,1024]{1,0:T(8,128)S(1)}) fusion(f32[384,4096]{1,0:T(8,128)} %fusion.11), kind=kLoop, calls=%fused_computation.96 | loop fusion | bytes 12582912 | tf_op jit(solution)/shard_map/slice | solution.py:125
  140.3 0.7 select_convert_fusion
  141.0 0.6 collective-permute-start.6
  141.6 3.0 %collective-permute-done.6 = bf16[384,2048]{1,0:T(8,128)(2,1)S(1)} collective-permute-done((bf16[384,2048]{1,0:T(8,128)(2,1)S(1)}, bf16[384,2048]{1,0:T(8,128)(2,1)S(1)}, u32[]{:S(2)}, u32[]{:S(2)}) %collective-permute-start.6) | collective-permute-done | bytes 1572896 | tf_op jit(solution)/shard_map/ppermute | solution.py:133
  144.6 2.0 add_convert_fusion
  146.6 28.0 %all-to-all-done.2 = bf16[8,48,2048]{2,1,0:T(8,128)(2,1)} async-done(((bf16[8,48,2048]{2,1,0:T(8,128)(2,1)}), bf16[8,48,2048]{2,1,0:T(8,128)(2,1)}, u32[]{:S(2)}, u32[]{:S(2)}) %all-to-all-start.2) | async-done | bytes 1572896 | tf_op jit(solution)/shard_map/all_to_all | solution.py:136
  174.6 4.4 %all-to-all-start.3 = ((bf16[8,48,2048]{2,1,0:T(8,128)(2,1)}), bf16[8,48,2048]{2,1,0:T(8,128)(2,1)}, u32[]{:S(2)}, u32[]{:S(2)}) async-start(bf16[8,48,2048]{2,1,0:T(8,128)(2,1)} %bitcast.75), calls=%async_computation.3 | async-start | bytes 3145728 | tf_op jit(solution)/shard_map/all_to_all | solution.py:136
  179.1 2.0 convolution_multiply_fusion.1
  181.2 2.0 fusion.20
  183.2 1.1 copy-done
  184.4 1.0 slice_select_fusion.1
  185.3 1.5 collective-permute-start.5
  186.8 29.4 %all-to-all-done.3 = bf16[8,48,2048]{2,1,0:T(8,128)(2,1)} async-done(((bf16[8,48,2048]{2,1,0:T(8,128)(2,1)}), bf16[8,48,2048]{2,1,0:T(8,128)(2,1)}, u32[]{:S(2)}, u32[]{:S(2)}) %all-to-all-start.3) | async-done | bytes 1572896 | tf_op jit(solution)/shard_map/all_to_all | solution.py:136
  216.2 2.2 fusion.58
  218.4 0.1 slice_select_fusion
  218.6 1.5 collective-permute-start.7
  220.1 6.6 %convolution_bitcast_fusion = f32[1,768,4096]{2,1,0:T(8,128)} fusion(bf16[384,768]{1,0:T(8,128)(2,1)S(1)} %copy-done.8, bf16[384,4096]{1,0:T(8,128)(2,1)S(1)} %copy-done.6), kind=kOutput, calls=%fused_computation | convolution fusion | flops 2415919104 | bytes 16318464 | tf_op jit(solution)/shard_map/sh,sd->hd/dot_general | solution.py:142
  226.7 6.6 %convolution_bitcast_fusion.1 = f32[1,4096,768]{2,1,0:T(8,128)} fusion(bf16[384,4096]{1,0:T(8,128)(2,1)S(1)} %pad_maximum_fusion, bf16[384,768]{1,0:T(8,128)(2,1)S(1)} %copy-done.10), kind=kOutput, calls=%fused_computation.1 | convolution fusion | flops 2415919104 | bytes 16318464 | tf_op jit(solution)/shard_map/sd,sh->dh/dot_general | solution.py:144
  233.4 2.0 add_convert_fusion.3
  235.4 1.6 collective-permute-done.7
  237.0 0.9 add_convert_fusion.2
  (53 shorter events, 0.4 us)
Async XLA Ops:
  0.6 12.3 %copy-start.11 = (bf16[192,1024]{1,0:T(8,128)(2,1)S(1)}, bf16[192,1024]{1,0:T(8,128)(2,1)}, u32[]{:S(2)}) copy-start(bf16[192,1024]{1,0:T(8,128)(2,1)} %param.6) | copy-start | bytes 1179652
  0.6 12.3 %collective-permute-start = (bf16[192,1024]{1,0:T(8,128)(2,1)}, bf16[192,1024]{1,0:T(8,128)(2,1)S(1)}, u32[]{:S(2)}, u32[]{:S(2)}) collective-permute-start(bf16[192,1024]{1,0:T(8,128)(2,1)} %param.6), channel_id=1, source_target_pairs={{0,2},{1,3},{2,0},{3,1},{4,6},{5,7},{6,4},{7,5},{8,10},{9,11},{10,... | collective-permute-start | bytes 1179656 | tf_op jit(solution)/shard_map/ppermute | solution.py:49
  7.0 6.8 %copy-start.13 = (pred[192]{0:T(512)(128)(4,1)}, pred[192]{0:T(512)(128)(4,1)S(1)}, u32[]{:S(2)}) copy-start(pred[192]{0:T(512)(128)(4,1)S(1)} %get-tuple-element.26) | copy-start | bytes 580
  7.0 6.8 %copy-start.15 = (pred[192]{0:T(512)(128)(4,1)}, pred[192]{0:T(512)(128)(4,1)S(1)}, u32[]{:S(2)}) copy-start(pred[192]{0:T(512)(128)(4,1)S(1)} %get-tuple-element.27) | copy-start | bytes 580
  13.8 42.2 %copy-start.12 = (bf16[192,1024]{1,0:T(8,128)(2,1)S(1)}, bf16[192,1024]{1,0:T(8,128)(2,1)}, u32[]{:S(2)}) copy-start(bf16[192,1024]{1,0:T(8,128)(2,1)} %param.7) | copy-start | bytes 1179652
  56.0 15.3 %collective-permute-start.2 = (bf16[384,2048]{1,0:T(8,128)(2,1)S(1)}, bf16[384,2048]{1,0:T(8,128)(2,1)S(1)}, u32[]{:S(2)}, u32[]{:S(2)}) collective-permute-start(bf16[384,2048]{1,0:T(8,128)(2,1)S(1)} %bitcast.76), channel_id=1, source_target_pairs={{0,1},{1,0},{2,3},{3,2},{4,5},{5,4},{6,7},{7,6},{8,9},{9,8},{10,11... | collective-permute-start | bytes 4718600 | tf_op jit(solution)/shard_map/ppermute | solution.py:88
  56.0 11.6 %collective-permute-start.1 = (bf16[192,1024]{1,0:T(8,128)(2,1)S(1)}, bf16[192,1024]{1,0:T(8,128)(2,1)}, u32[]{:S(2)}, u32[]{:S(2)}) collective-permute-start(bf16[192,1024]{1,0:T(8,128)(2,1)S(1)} %copy-done.12), channel_id=1, source_target_pairs={{0,2},{1,3},{2,0},{3,1},{4,6},{5,7},{6,4},{7,5},{8,10},{9,11},{10,... | collective-permute-start | bytes 1179656 | tf_op jit(solution)/shard_map/ppermute | solution.py:49
  72.3 41.5 %all-to-all-start.1 = ((bf16[8,48,2048]{2,1,0:T(8,128)(2,1)}), bf16[8,48,2048]{2,1,0:T(8,128)(2,1)}, u32[]{:S(2)}, u32[]{:S(2)}) async-start(bf16[8,48,2048]{2,1,0:T(8,128)(2,1)} %bitcast.77), calls=%async_computation.1 | async-start | bytes 3145728 | tf_op jit(solution)/shard_map/all_to_all | solution.py:85
  83.3 0.8 copy-start.7
  90.0 2.0 copy-start.2
  90.0 2.1 copy-start.3
  90.0 2.7 %copy-start.4 = (f32[384,1024]{1,0:T(8,128)}, f32[384,1024]{1,0:T(8,128)S(1)}, u32[]{:S(2)}) copy-start(f32[384,1024]{1,0:T(8,128)S(1)} %get-tuple-element.34) | copy-start | bytes 4718596
  90.0 3.1 %copy-start.5 = (f32[384,1024]{1,0:T(8,128)}, f32[384,1024]{1,0:T(8,128)S(1)}, u32[]{:S(2)}) copy-start(f32[384,1024]{1,0:T(8,128)S(1)} %get-tuple-element.35) | copy-start | bytes 4718596
  93.2 20.6 %collective-permute-start.3 = (bf16[384,2048]{1,0:T(8,128)(2,1)}, bf16[384,2048]{1,0:T(8,128)(2,1)}, u32[]{:S(2)}, u32[]{:S(2)}) collective-permute-start(bf16[384,2048]{1,0:T(8,128)(2,1)} %select_convert_fusion.1), channel_id=1, source_target_pairs={{0,1},{1,0},{2,3},{3,2},{4,5},{5,4},{6,7},{7,6},{8,9},{9,8},{10,11... | collective-permute-start | bytes 4718600 | tf_op jit(solution)/shard_map/ppermute | solution.py:133
  113.8 5.3 %collective-permute-start.4 = (bf16[384,2048]{1,0:T(8,128)(2,1)}, bf16[384,2048]{1,0:T(8,128)(2,1)}, u32[]{:S(2)}, u32[]{:S(2)}) collective-permute-start(bf16[384,2048]{1,0:T(8,128)(2,1)} %bitcast.8), channel_id=1, source_target_pairs={{0,1},{1,0},{2,3},{3,2},{4,5},{5,4},{6,7},{7,6},{8,9},{9,8},{10,11... | collective-permute-start | bytes 4718600 | tf_op jit(solution)/shard_map/ppermute | solution.py:88
  119.1 4.4 %slice-start = ((s8[6291456]{0:T(1024)(128)(4,1)}), s8[4194304]{0:T(1024)(128)(4,1)S(1)}, s32[]{:S(2)}) async-start(s8[6291456]{0:T(1024)(128)(4,1)} %bitcast.72), calls=%async_computation.4 | async-start | bytes 8388608
  121.5 2.4 %slice-start.1 = ((s8[6291456]{0:T(1024)(128)(4,1)}), s8[2097152]{0:T(1024)(128)(4,1)S(1)}, s32[]{:S(2)}) async-start(s8[6291456]{0:T(1024)(128)(4,1)} %bitcast.72), calls=%async_computation.5 | async-start | bytes 4194304
  121.6 3.0 %copy-start.17 = (f32[384,768]{1,0:T(8,128)S(1)}, f32[384,768]{1,0:T(8,128)}, u32[]{:S(2)}) copy-start(f32[384,768]{1,0:T(8,128)} %get-tuple-element.55) | copy-start | bytes 3538948
  121.7 6.1 %slice-start.2 = ((s8[6291456]{0:T(1024)(128)(4,1)}), s8[4194304]{0:T(1024)(128)(4,1)S(1)}, s32[]{:S(2)}) async-start(s8[6291456]{0:T(1024)(128)(4,1)} %bitcast.84), calls=%async_computation.6 | async-start | bytes 8388608
  124.6 3.2 %slice-start.3 = ((s8[6291456]{0:T(1024)(128)(4,1)}), s8[2097152]{0:T(1024)(128)(4,1)S(1)}, s32[]{:S(2)}) async-start(s8[6291456]{0:T(1024)(128)(4,1)} %bitcast.84), calls=%async_computation.7 | async-start | bytes 4194304
  127.8 4.5 %copy-start.9 = (bf16[384,768]{1,0:T(8,128)(2,1)}, bf16[384,768]{1,0:T(8,128)(2,1)S(1)}, u32[]{:S(2)}) copy-start(bf16[384,768]{1,0:T(8,128)(2,1)S(1)} %fusion.24) | copy-start | bytes 1769476
  132.4 42.3 %all-to-all-start.2 = ((bf16[8,48,2048]{2,1,0:T(8,128)(2,1)}), bf16[8,48,2048]{2,1,0:T(8,128)(2,1)}, u32[]{:S(2)}, u32[]{:S(2)}) async-start(bf16[8,48,2048]{2,1,0:T(8,128)(2,1)} %bitcast.74), calls=%async_computation.2 | async-start | bytes 3145728 | tf_op jit(solution)/shard_map/all_to_all | solution.py:136
  141.0 3.6 %collective-permute-start.6 = (bf16[384,2048]{1,0:T(8,128)(2,1)S(1)}, bf16[384,2048]{1,0:T(8,128)(2,1)S(1)}, u32[]{:S(2)}, u32[]{:S(2)}) collective-permute-start(bf16[384,2048]{1,0:T(8,128)(2,1)S(1)} %select_convert_fusion), channel_id=1, source_target_pairs={{0,1},{1,0},{2,3},{3,2},{4,5},{5,4},{6,7},{7,6},{8,9},{9,8},{10,11... | collective-permute-start | bytes 4718600 | tf_op jit(solution)/shard_map/ppermute | solution.py:133
  174.6 4.5 %copy-start.16 = (pred[192]{0:T(512)(128)(4,1)S(1)}, pred[192]{0:T(512)(128)(4,1)}, u32[]{:S(2)}) copy-start(pred[192]{0:T(512)(128)(4,1)} %copy-done.15) | copy-start | bytes 580
  174.6 41.6 %all-to-all-start.3 = ((bf16[8,48,2048]{2,1,0:T(8,128)(2,1)}), bf16[8,48,2048]{2,1,0:T(8,128)(2,1)}, u32[]{:S(2)}, u32[]{:S(2)}) async-start(bf16[8,48,2048]{2,1,0:T(8,128)(2,1)} %bitcast.75), calls=%async_computation.3 | async-start | bytes 3145728 | tf_op jit(solution)/shard_map/all_to_all | solution.py:136
  179.1 2.1 copy-start.14
  183.2 1.2 copy-start
  185.3 48.0 %collective-permute-start.5 = (f32[192,1024]{1,0:T(8,128)}, f32[192,1024]{1,0:T(8,128)}, u32[]{:S(2)}, u32[]{:S(2)}) collective-permute-start(f32[192,1024]{1,0:T(8,128)} %slice_select_fusion.1), channel_id=1, source_target_pairs={{0,2},{1,3},{2,0},{3,1},{4,6},{5,7},{6,4},{7,5},{8,10},{9,11},{10,... | collective-permute-start | bytes 2359304 | tf_op jit(solution)/shard_map/ppermute | solution.py:157
  216.2 3.9 %copy-start.6 = (bf16[384,4096]{1,0:T(8,128)(2,1)S(1)}, bf16[384,4096]{1,0:T(8,128)(2,1)}, u32[]{:S(2)}) copy-start(bf16[384,4096]{1,0:T(8,128)(2,1)} %pad_maximum_fusion.3) | copy-start | bytes 9437188
  218.4 1.7 copy-start.8
  218.6 8.2 %copy-start.10 = (bf16[384,768]{1,0:T(8,128)(2,1)S(1)}, bf16[384,768]{1,0:T(8,128)(2,1)}, u32[]{:S(2)}) copy-start(bf16[384,768]{1,0:T(8,128)(2,1)} %copy-done.9) | copy-start | bytes 1769476
  218.6 18.4 %collective-permute-start.7 = (f32[192,1024]{1,0:T(8,128)S(1)}, f32[192,1024]{1,0:T(8,128)S(1)}, u32[]{:S(2)}, u32[]{:S(2)}) collective-permute-start(f32[192,1024]{1,0:T(8,128)S(1)} %slice_select_fusion), channel_id=1, source_target_pairs={{0,2},{1,3},{2,0},{3,1},{4,6},{5,7},{6,4},{7,5},{8,10},{9,11},{10,... | collective-permute-start | bytes 2359304 | tf_op jit(solution)/shard_map/ppermute | solution.py:157
  226.7 6.6 %copy-start.1 = (f32[192,2048]{1,0:T(8,128)S(1)}, f32[192,2048]{1,0:T(8,128)}, u32[]{:S(2)}) copy-start(f32[192,2048]{1,0:T(8,128)} %copy-done) | copy-start | bytes 4718596

commit v2 on v1

--- a/solution.py
+++ b/solution.py
@@ -140,8 +140,9 @@
 
     back_out, (act_late, d_late) = to_sections(out_loc, (activation, d_rows))
     grad_down = jnp.einsum("sh,sd->hd", act_late, d_late, preferred_element_type=f32)
-    back_dx, (x_late, pre_late) = to_sections(dx_loc, (x_rows, grad_pre))
+    back_dx, (x_late, pre_late, grad_down) = to_sections(dx_loc, (x_rows, grad_pre, grad_down))
     grad_up = jnp.einsum("sd,sh->dh", x_late, pre_late, preferred_element_type=f32)
+    back_dx, grad_up = lax.optimization_barrier((back_dx, grad_up))
 
     mixed_sub = None
     for k, pick in enumerate(picks):

time: 238 us -> 240 us (level)
    ppermute x2, waiting for transfers between devices: 1.58 us -> 15.1 us  [finish(): return (keep + lax.ppermute(give, 'exp', half_swap)).astype(bf16)]
    all_to_all x2, waiting for transfers between devices: 57.4 us -> 46.5 us  [to_sections(): lax.all_to_all(sent.reshape(sections, capacity, sub_w), 'attn', split_axi...]
    ppermute x2, waiting for transfers between devices: 3.04 us -> 0.01 us  [to_sections(): got = lax.ppermute(theirs.astype(bf16), 'exp', core_shift(s))]
    unnamed x45 -> x43, local copies, waits for them, and re-layouts: 5.24 us -> 4.88 us
  transfers between devices with their start and end apart: 11 -> 11, of which waited for: 7 -> 6; matrix products, arithmetic and copies ran while one was open for 24% -> 24% of each run, Pallas kernels for 0% -> 0%
where the time goes in v2:
time: 240 us; the launch traced here: 239 us
  waiting for transfers between devices  95.8 us (40%)
  blocking collectives  42.2 us (18%)
  matrix products  42 us (18%)
  other arithmetic  24.7 us (10%)
  starting transfers between devices  21.4 us (9%)
  local copies, waits for them, and re-layouts  12 us (5%)
    all_to_all x2, waiting for transfers between devices, to_sections(): lax.all_to_all(sent.reshape(sections, capacity, sub_w), 'attn', split_axi...  46.5 us
    all_to_all x1, blocking collectives, to_experts(): lax.all_to_all(buf.reshape(sections, capacity, sub_w), 'attn', split_axis...  42.2 us
    all_to_all x1, waiting for transfers between devices, to_experts(): lax.all_to_all(buf.reshape(sections, capacity, sub_w), 'attn', split_axis...  20.5 us
    ppermute x2, waiting for transfers between devices, finish(): return (keep + lax.ppermute(give, 'exp', half_swap)).astype(bf16)  15.1 us
    ppermute x2, waiting for transfers between devices, core_subset(): other = lax.ppermute(local, 'exp', half_swap)  13.7 us
    all_to_all x2, starting transfers between devices, to_sections(): lax.all_to_all(sent.reshape(sections, capacity, sub_w), 'attn', split_axi...  8.79 us
    dot_general x1, matrix products, on_device(): jnp.einsum('sd,sh->dh', x_late, pre_late, preferred_element_type=f32)  7.7 us
    convert_element_type x2, other arithmetic, to_sections(): sent, hold = lax.optimization_barrier((summed.astype(bf16), hold))  7.3 us
  transfers between devices with their start and end apart: 11, of which 6 were waited for; matrix products, arithmetic and copies ran while one was open for 24% of the time, Pallas kernels for 0%

profile of v2, /device:TPU:0, one launch (start us, length us, event | category | flops | bytes accessed | tf_op | source)
XLA Modules:
  0.0 239.2 jit_solution(7885978921937437085)
XLA Ops:
  0.6 3.0 %collective-permute-start = (bf16[192,1024]{1,0:T(8,128)(2,1)}, bf16[192,1024]{1,0:T(8,128)(2,1)S(1)}, u32[]{:S(2)}, u32[]{:S(2)}) collective-permute-start(bf16[192,1024]{1,0:T(8,128)(2,1)} %param.6), channel_id=1, source_target_pairs={{0,2},{1,3},{2,0},{3,1},{4,6},{5,7},{6,4},{7,5},{8,10},{9,11},{10,... | collective-permute-start | bytes 1179656 | tf_op jit(solution)/shard_map/ppermute | solution.py:49
  3.6 0.7 broadcast_compare_fusion
  4.3 0.8 copy.30
  5.1 0.1 eq.102
  5.3 0.1 eq.106
  5.4 0.2 copy.35
  5.6 0.9 reduce-window.6
  6.5 0.2 slice_reduce_fusion.4
  6.8 0.2 slice_reduce_fusion.2
  7.0 0.1 fusion.54
  7.1 0.1 reshape.68
  7.4 0.2 slice_reduce_fusion
  7.6 5.4 %collective-permute-done = bf16[192,1024]{1,0:T(8,128)(2,1)S(1)} collective-permute-done((bf16[192,1024]{1,0:T(8,128)(2,1)}, bf16[192,1024]{1,0:T(8,128)(2,1)S(1)}, u32[]{:S(2)}, u32[]{:S(2)}) %collective-permute-start) | collective-permute-done | bytes 393248 | tf_op jit(solution)/shard_map/ppermute | solution.py:49
  13.0 0.8 convolution_convert_fusion
  13.8 42.2 %all_to_all.20 = bf16[8,48,2048]{2,1,0:T(8,128)(2,1)S(1)} all-to-all(bf16[8,48,2048]{2,1,0:T(8,128)(2,1)S(1)} %bitcast.78), channel_id=1, replica_groups=mesh['attn'=8,'exp'=4] {'attn'}, dimensions={0} | all-to-all | bytes 3145728 | tf_op jit(solution)/shard_map/all_to_all | solution.py:85
  56.0 1.6 collective-permute-start.1
  57.6 0.8 fusion.68
  58.4 0.9 select_reduce_fusion
  59.3 8.3 %collective-permute-done.1 = bf16[192,1024]{1,0:T(8,128)(2,1)S(1)} collective-permute-done((bf16[192,1024]{1,0:T(8,128)(2,1)S(1)}, bf16[192,1024]{1,0:T(8,128)(2,1)S(1)}, u32[]{:S(2)}, u32[]{:S(2)}) %collective-permute-start.1) | collective-permute-done | bytes 393248 | tf_op jit(solution)/shard_map/ppermute | solution.py:49
  67.6 1.9 multiply_convert_fusion
  69.5 1.6 broadcast_select_fusion.3
  71.2 0.4 fusion.66
  71.6 0.3 pad_maximum_fusion
  71.8 4.5 %all-to-all-start.1 = ((bf16[8,48,2048]{2,1,0:T(8,128)(2,1)}), bf16[8,48,2048]{2,1,0:T(8,128)(2,1)}, u32[]{:S(2)}, u32[]{:S(2)}) async-start(bf16[8,48,2048]{2,1,0:T(8,128)(2,1)} %bitcast.77), calls=%async_computation.1 | async-start | bytes 3145728 | tf_op jit(solution)/shard_map/all_to_all | solution.py:85
  76.3 6.5 %multiply_convert_fusion.1 = (bf16[384,768]{1,0:T(8,128)(2,1)S(1)}, f32[384,768]{1,0:T(8,128)}) fusion(bf16[384,4096]{1,0:T(8,128)(2,1)S(1)} %pad_maximum_fusion, bf16[1,4096,768]{2,1,0:T(8,128)(2,1)} %param.10), kind=kOutput, calls=%fused_computation.40 | convolution fusion | flops 2418573312 | bytes 11206656 | tf_op jit(solution)/shard_map/dot_general | solution.py:105
  82.8 0.8 copy-done.5
  83.6 4.7 %fusion.17 = f32[384,4096]{1,0:T(8,128)S(1)} fusion(bf16[384,768]{1,0:T(8,128)(2,1)S(1)} %get-tuple-element.22, bf16[1,768,4096]{2,1,0:T(8,128)(2,1)} %param.11), kind=kOutput, calls=%fused_computation.11 | convolution fusion | flops 2419064832 | bytes 13172736 | tf_op jit(solution)/shard_map/dot_general | solution.py:115
  88.4 1.1 fusion.63
  89.6 1.9 select_convert_fusion.1
  91.4 0.2 copy-done.1
  91.6 0.6 copy-done.2
  92.2 0.5 copy-done.3
  92.7 20.5 %all-to-all-done.1 = bf16[8,48,2048]{2,1,0:T(8,128)(2,1)} async-done(((bf16[8,48,2048]{2,1,0:T(8,128)(2,1)}), bf16[8,48,2048]{2,1,0:T(8,128)(2,1)}, u32[]{:S(2)}, u32[]{:S(2)}) %all-to-all-start.1) | async-done | bytes 1572896 | tf_op jit(solution)/shard_map/all_to_all | solution.py:85
  113.2 5.3 %add_convert_fusion.1 = bf16[384,2048]{1,0:T(8,128)(2,1)} fusion(bf16[384,2048]{1,0:T(8,128)(2,1)} %collective-permute-done.3, f32[384,1024]{1,0:T(8,128)} %copy-done.1, f32[384,1024]{1,0:T(8,128)} %copy-done.2, f32[384,1024]{1,0:T(8,128)} %copy-done.3, f32[384,1024]{1,0:T(8,128)} %copy-done, pred[]{:T(512)S(6)} %eq.116), kind=kLoop, calls=%fused_computation.20 | loop fusion | flops 4718592 | bytes 9437185 | tf_op jit(solution)/shard_map/convert_element_type | solution.py:135
  118.5 2.2 broadcast_select_fusion.2
  120.8 0.1 fusion.64
  120.9 0.1 fusion.65
  121.0 1.8 pad_maximum_fusion.3
  122.9 0.5 slice-done.1
  123.4 0.7 copy-done.16
  124.1 3.1 %fusion.24 = bf16[384,768]{1,0:T(8,128)(2,1)S(1)} fusion(bf16[1,768,4096]{2,1,0:T(8,128)(2,1)S(1)} %bitcast.73, f32[384,768]{1,0:T(8,128)S(1)} %copy-done.16, bf16[384,1024]{1,0:T(8,128)(2,1)S(1)} %get-tuple-element.49, bf16[384,1024]{1,0:T(8,128)(2,1)S(1)} %get-tuple-element.47, bf16[384,1024]{1,0:T(8,128)(2,1)S(1)} %get-tuple-element.48, ...), kind=kOutput, calls=%fused_computation.34 | convolution fusion | flops 2434105344 | bytes 11206656 | tf_op jit(solution)/shard_map/sd,hd->sh/dot_general | solution.py:108
  127.2 4.5 %fusion.11 = f32[384,4096]{1,0:T(8,128)} fusion(bf16[384,768]{1,0:T(8,128)(2,1)S(1)} %fusion.24, bf16[1,4096,768]{2,1,0:T(8,128)(2,1)S(1)} %bitcast.85), kind=kOutput, calls=%fused_computation.9 | convolution fusion | flops 2419064832 | bytes 13172736 | tf_op jit(solution)/shard_map/sh,dh->sd/dot_general | solution.py:116
  131.8 4.5 %all-to-all-start.2 = ((bf16[8,48,2048]{2,1,0:T(8,128)(2,1)}), bf16[8,48,2048]{2,1,0:T(8,128)(2,1)}, u32[]{:S(2)}, u32[]{:S(2)}) async-start(bf16[8,48,2048]{2,1,0:T(8,128)(2,1)} %bitcast.74), calls=%async_computation.2 | async-start | bytes 3145728 | tf_op jit(solution)/shard_map/all_to_all | solution.py:136
  136.3 3.4 %fusion.62 = (f32[384,1024]{1,0:T(8,128)S(1)}, f32[384,1024]{1,0:T(8,128)S(1)}, f32[384,1024]{1,0:T(8,128)S(1)}, f32[384,1024]{1,0:T(8,128)S(1)}) fusion(f32[384,4096]{1,0:T(8,128)} %fusion.11), kind=kLoop, calls=%fused_computation.94 | loop fusion | bytes 12582912 | tf_op jit(solution)/shard_map/slice | solution.py:125
  139.7 0.7 select_convert_fusion
  140.4 0.6 collective-permute-start.6
  141.0 0.6 copy-done.4
  141.6 0.1 copy-done.6
  141.7 6.6 %fusion.69 = f32[768,4096]{1,0:T(8,128)} fusion(bf16[384,768]{1,0:T(8,128)(2,1)S(1)} %copy-done.6, bf16[384,4096]{1,0:T(8,128)(2,1)S(1)} %copy-done.4), kind=kOutput, calls=%fused_computation.101 | convolution fusion | flops 2415919104 | bytes 16318464 | tf_op jit(solution)/shard_map/sh,sd->hd/dot_general | solution.py:142
  148.3 2.0 add_convert_fusion
  150.4 23.6 %all-to-all-done.2 = bf16[8,48,2048]{2,1,0:T(8,128)(2,1)} async-done(((bf16[8,48,2048]{2,1,0:T(8,128)(2,1)}), bf16[8,48,2048]{2,1,0:T(8,128)(2,1)}, u32[]{:S(2)}, u32[]{:S(2)}) %all-to-all-start.2) | async-done | bytes 1572896 | tf_op jit(solution)/shard_map/all_to_all | solution.py:136
  174.0 4.3 %all-to-all-start.3 = ((bf16[8,48,2048]{2,1,0:T(8,128)(2,1)}), bf16[8,48,2048]{2,1,0:T(8,128)(2,1)}, u32[]{:S(2)}, u32[]{:S(2)}) async-start(bf16[8,48,2048]{2,1,0:T(8,128)(2,1)} %bitcast.75), calls=%async_computation.3 | async-start | bytes 3145728 | tf_op jit(solution)/shard_map/all_to_all | solution.py:136
  178.3 7.7 %fusion.70 = f32[4096,768]{1,0:T(8,128)} fusion(bf16[384,4096]{1,0:T(8,128)(2,1)S(1)} %pad_maximum_fusion, bf16[384,768]{1,0:T(8,128)(2,1)} %copy-done.7), kind=kOutput, calls=%fused_computation.102 | convolution fusion | flops 2415919104 | bytes 16318464 | tf_op jit(solution)/shard_map/sd,sh->dh/dot_general | solution.py:144
  186.0 2.0 convolution_multiply_fusion.1
  188.1 2.0 fusion.20
  190.2 1.0 slice_select_fusion.1
  191.2 1.5 collective-permute-start.5
  192.6 22.8 %all-to-all-done.3 = bf16[8,48,2048]{2,1,0:T(8,128)(2,1)} async-done(((bf16[8,48,2048]{2,1,0:T(8,128)(2,1)}), bf16[8,48,2048]{2,1,0:T(8,128)(2,1)}, u32[]{:S(2)}, u32[]{:S(2)}) %all-to-all-start.3) | async-done | bytes 1572896 | tf_op jit(solution)/shard_map/all_to_all | solution.py:136
  215.5 2.1 fusion.58
  217.5 1.0 slice_select_fusion
  218.5 1.5 collective-permute-start.7
  220.0 2.0 add_convert_fusion.3
  222.1 15.1 %collective-permute-done.7 = f32[192,1024]{1,0:T(8,128)} collective-permute-done((f32[192,1024]{1,0:T(8,128)}, f32[192,1024]{1,0:T(8,128)}, u32[]{:S(2)}, u32[]{:S(2)}) %collective-permute-start.7) | collective-permute-done | bytes 786464 | tf_op jit(solution)/shard_map/ppermute | solution.py:158
  237.2 2.0 add_convert_fusion.2
  (51 shorter events, 0.4 us)
Async XLA Ops:
  0.6 12.3 %copy-start.8 = (bf16[192,1024]{1,0:T(8,128)(2,1)S(1)}, bf16[192,1024]{1,0:T(8,128)(2,1)}, u32[]{:S(2)}) copy-start(bf16[192,1024]{1,0:T(8,128)(2,1)} %param.6) | copy-start | bytes 1179652
  0.6 12.3 %collective-permute-start = (bf16[192,1024]{1,0:T(8,128)(2,1)}, bf16[192,1024]{1,0:T(8,128)(2,1)S(1)}, u32[]{:S(2)}, u32[]{:S(2)}) collective-permute-start(bf16[192,1024]{1,0:T(8,128)(2,1)} %param.6), channel_id=1, source_target_pairs={{0,2},{1,3},{2,0},{3,1},{4,6},{5,7},{6,4},{7,5},{8,10},{9,11},{10,... | collective-permute-start | bytes 1179656 | tf_op jit(solution)/shard_map/ppermute | solution.py:49
  7.0 6.8 %copy-start.10 = (pred[192]{0:T(512)(128)(4,1)}, pred[192]{0:T(512)(128)(4,1)S(1)}, u32[]{:S(2)}) copy-start(pred[192]{0:T(512)(128)(4,1)S(1)} %get-tuple-element.32) | copy-start | bytes 580
  7.0 6.8 %copy-start.13 = (pred[192]{0:T(512)(128)(4,1)}, pred[192]{0:T(512)(128)(4,1)S(1)}, u32[]{:S(2)}) copy-start(pred[192]{0:T(512)(128)(4,1)S(1)} %get-tuple-element.33) | copy-start | bytes 580
  13.8 42.2 %copy-start.9 = (bf16[192,1024]{1,0:T(8,128)(2,1)S(1)}, bf16[192,1024]{1,0:T(8,128)(2,1)}, u32[]{:S(2)}) copy-start(bf16[192,1024]{1,0:T(8,128)(2,1)} %param.7) | copy-start | bytes 1179652
  56.0 11.6 %copy-start.11 = (pred[192]{0:T(512)(128)(4,1)S(1)}, pred[192]{0:T(512)(128)(4,1)}, u32[]{:S(2)}) copy-start(pred[192]{0:T(512)(128)(4,1)} %copy-done.10) | copy-start | bytes 580
  56.0 11.6 %copy-start.14 = (pred[192]{0:T(512)(128)(4,1)S(1)}, pred[192]{0:T(512)(128)(4,1)}, u32[]{:S(2)}) copy-start(pred[192]{0:T(512)(128)(4,1)} %copy-done.13) | copy-start | bytes 580
  56.0 13.5 %collective-permute-start.2 = (bf16[384,2048]{1,0:T(8,128)(2,1)S(1)}, bf16[384,2048]{1,0:T(8,128)(2,1)}, u32[]{:S(2)}, u32[]{:S(2)}) collective-permute-start(bf16[384,2048]{1,0:T(8,128)(2,1)S(1)} %bitcast.76), channel_id=1, source_target_pairs={{0,1},{1,0},{2,3},{3,2},{4,5},{5,4},{6,7},{7,6},{8,9},{9,8},{10,11... | collective-permute-start | bytes 4718600 | tf_op jit(solution)/shard_map/ppermute | solution.py:88
  56.0 11.5 %collective-permute-start.1 = (bf16[192,1024]{1,0:T(8,128)(2,1)S(1)}, bf16[192,1024]{1,0:T(8,128)(2,1)S(1)}, u32[]{:S(2)}, u32[]{:S(2)}) collective-permute-start(bf16[192,1024]{1,0:T(8,128)(2,1)S(1)} %copy-done.9), channel_id=1, source_target_pairs={{0,2},{1,3},{2,0},{3,1},{4,6},{5,7},{6,4},{7,5},{8,10},{9,11},{10,... | collective-permute-start | bytes 1179656 | tf_op jit(solution)/shard_map/ppermute | solution.py:49
  71.8 41.4 %all-to-all-start.1 = ((bf16[8,48,2048]{2,1,0:T(8,128)(2,1)}), bf16[8,48,2048]{2,1,0:T(8,128)(2,1)}, u32[]{:S(2)}, u32[]{:S(2)}) async-start(bf16[8,48,2048]{2,1,0:T(8,128)(2,1)} %bitcast.77), calls=%async_computation.1 | async-start | bytes 3145728 | tf_op jit(solution)/shard_map/all_to_all | solution.py:85
  82.8 0.8 copy-start.5
  89.5 1.9 copy-start
  89.5 2.1 copy-start.1
  89.5 2.7 %copy-start.2 = (f32[384,1024]{1,0:T(8,128)}, f32[384,1024]{1,0:T(8,128)S(1)}, u32[]{:S(2)}) copy-start(f32[384,1024]{1,0:T(8,128)S(1)} %get-tuple-element.40) | copy-start | bytes 4718596
  89.5 3.1 %copy-start.3 = (f32[384,1024]{1,0:T(8,128)}, f32[384,1024]{1,0:T(8,128)S(1)}, u32[]{:S(2)}) copy-start(f32[384,1024]{1,0:T(8,128)S(1)} %get-tuple-element.41) | copy-start | bytes 4718596
  92.7 20.6 %collective-permute-start.3 = (bf16[384,2048]{1,0:T(8,128)(2,1)}, bf16[384,2048]{1,0:T(8,128)(2,1)}, u32[]{:S(2)}, u32[]{:S(2)}) collective-permute-start(bf16[384,2048]{1,0:T(8,128)(2,1)} %select_convert_fusion.1), channel_id=1, source_target_pairs={{0,1},{1,0},{2,3},{3,2},{4,5},{5,4},{6,7},{7,6},{8,9},{9,8},{10,11... | collective-permute-start | bytes 4718600 | tf_op jit(solution)/shard_map/ppermute | solution.py:133
  113.2 5.3 %collective-permute-start.4 = (bf16[384,2048]{1,0:T(8,128)(2,1)}, bf16[384,2048]{1,0:T(8,128)(2,1)}, u32[]{:S(2)}, u32[]{:S(2)}) collective-permute-start(bf16[384,2048]{1,0:T(8,128)(2,1)} %bitcast.8), channel_id=1, source_target_pairs={{0,1},{1,0},{2,3},{3,2},{4,5},{5,4},{6,7},{7,6},{8,9},{9,8},{10,11... | collective-permute-start | bytes 4718600 | tf_op jit(solution)/shard_map/ppermute | solution.py:88
  118.5 4.3 %slice-start = ((s8[6291456]{0:T(1024)(128)(4,1)}), s8[4194304]{0:T(1024)(128)(4,1)S(1)}, s32[]{:S(2)}) async-start(s8[6291456]{0:T(1024)(128)(4,1)} %bitcast.72), calls=%async_computation.4 | async-start | bytes 8388608
  120.9 2.5 %slice-start.1 = ((s8[6291456]{0:T(1024)(128)(4,1)}), s8[2097152]{0:T(1024)(128)(4,1)S(1)}, s32[]{:S(2)}) async-start(s8[6291456]{0:T(1024)(128)(4,1)} %bitcast.72), calls=%async_computation.5 | async-start | bytes 4194304
  121.0 3.0 %copy-start.16 = (f32[384,768]{1,0:T(8,128)S(1)}, f32[384,768]{1,0:T(8,128)}, u32[]{:S(2)}) copy-start(f32[384,768]{1,0:T(8,128)} %get-tuple-element.61) | copy-start | bytes 3538948
  121.0 6.2 %slice-start.2 = ((s8[6291456]{0:T(1024)(128)(4,1)}), s8[4194304]{0:T(1024)(128)(4,1)S(1)}, s32[]{:S(2)}) async-start(s8[6291456]{0:T(1024)(128)(4,1)} %bitcast.84), calls=%async_computation.6 | async-start | bytes 8388608
  124.1 3.2 %slice-start.3 = ((s8[6291456]{0:T(1024)(128)(4,1)}), s8[2097152]{0:T(1024)(128)(4,1)S(1)}, s32[]{:S(2)}) async-start(s8[6291456]{0:T(1024)(128)(4,1)} %bitcast.84), calls=%async_computation.7 | async-start | bytes 4194304
  127.2 4.5 %copy-start.7 = (bf16[384,768]{1,0:T(8,128)(2,1)}, bf16[384,768]{1,0:T(8,128)(2,1)S(1)}, u32[]{:S(2)}) copy-start(bf16[384,768]{1,0:T(8,128)(2,1)S(1)} %fusion.24) | copy-start | bytes 1769476
  131.8 42.2 %all-to-all-start.2 = ((bf16[8,48,2048]{2,1,0:T(8,128)(2,1)}), bf16[8,48,2048]{2,1,0:T(8,128)(2,1)}, u32[]{:S(2)}, u32[]{:S(2)}) async-start(bf16[8,48,2048]{2,1,0:T(8,128)(2,1)} %bitcast.74), calls=%async_computation.2 | async-start | bytes 3145728 | tf_op jit(solution)/shard_map/all_to_all | solution.py:136
  139.7 1.9 copy-start.4
  139.7 2.0 copy-start.6
  140.4 7.9 %collective-permute-start.6 = (bf16[384,2048]{1,0:T(8,128)(2,1)S(1)}, bf16[384,2048]{1,0:T(8,128)(2,1)S(1)}, u32[]{:S(2)}, u32[]{:S(2)}) collective-permute-start(bf16[384,2048]{1,0:T(8,128)(2,1)S(1)} %select_convert_fusion), channel_id=1, source_target_pairs={{0,1},{1,0},{2,3},{3,2},{4,5},{5,4},{6,7},{7,6},{8,9},{9,8},{10,11... | collective-permute-start | bytes 4718600 | tf_op jit(solution)/shard_map/ppermute | solution.py:133
  174.0 41.5 %all-to-all-start.3 = ((bf16[8,48,2048]{2,1,0:T(8,128)(2,1)}), bf16[8,48,2048]{2,1,0:T(8,128)(2,1)}, u32[]{:S(2)}, u32[]{:S(2)}) async-start(bf16[8,48,2048]{2,1,0:T(8,128)(2,1)} %bitcast.75), calls=%async_computation.3 | async-start | bytes 3145728 | tf_op jit(solution)/shard_map/all_to_all | solution.py:136
  178.3 7.7 %copy-start.15 = (pred[192]{0:T(512)(128)(4,1)S(1)}, pred[192]{0:T(512)(128)(4,1)}, u32[]{:S(2)}) copy-start(pred[192]{0:T(512)(128)(4,1)} %copy-done.13) | copy-start | bytes 580
  186.0 2.1 copy-start.12
  191.2 28.9 %collective-permute-start.5 = (f32[192,1024]{1,0:T(8,128)}, f32[192,1024]{1,0:T(8,128)}, u32[]{:S(2)}, u32[]{:S(2)}) collective-permute-start(f32[192,1024]{1,0:T(8,128)} %slice_select_fusion.1), channel_id=1, source_target_pairs={{0,2},{1,3},{2,0},{3,1},{4,6},{5,7},{6,4},{7,5},{8,10},{9,11},{10,... | collective-permute-start | bytes 2359304 | tf_op jit(solution)/shard_map/ppermute | solution.py:158
  218.5 18.6 %collective-permute-start.7 = (f32[192,1024]{1,0:T(8,128)}, f32[192,1024]{1,0:T(8,128)}, u32[]{:S(2)}, u32[]{:S(2)}) collective-permute-start(f32[192,1024]{1,0:T(8,128)} %slice_select_fusion), channel_id=1, source_target_pairs={{0,2},{1,3},{2,0},{3,1},{4,6},{5,7},{6,4},{7,5},{8,10},{9,11},{10,... | collective-permute-start | bytes 2359304 | tf_op jit(solution)/shard_map/ppermute | solution.py:158

commit v3 on v1

--- a/solution.py
+++ b/solution.py
@@ -52,7 +52,19 @@
             [jnp.where(first, local, other), jnp.where(first, other, local)], axis=1
         )
 
-    sub_x = core_subset(patches)
+    def pick_by(index, values):
+        picked = values[0]
+        for i, value in enumerate(values[1:], start=1):
+            picked = jnp.where(index == i, value, picked)
+        return picked
+
+    def to_experts(got):
+        by_shift = [got] + [lax.ppermute(got, "exp", core_shift(s)) for s in range(1, cores)]
+        ordered = [pick_by((core - source) % cores, by_shift) for source in range(cores)]
+        return jnp.concatenate(
+            [ordered[q][:, p * slice_w:(p + 1) * slice_w] for p in range(EXP_DEV) for q in range(cores)],
+            axis=1,
+        )
 
     local_slot = route_slots(route_ids, experts, capacity)
     owned = (route_ids % EXP_DEV) == half
@@ -69,32 +81,26 @@
     )
     dispatch_mat = dispatch.astype(bf16)
 
-    x_buf = jnp.dot(dispatch_mat, sub_x, preferred_element_type=f32).astype(bf16)
-    grad_out, x_buf = lax.optimization_barrier((grad_out, x_buf))
+    def send(buf):
+        width = buf.shape[-1]
+        return lax.all_to_all(
+            buf.reshape(sections, capacity, width), "attn", split_axis=0, concat_axis=0, tiled=True
+        ).reshape(slots, width)
+
+    got_own = send(jnp.dot(dispatch_mat, patches, preferred_element_type=f32).astype(bf16))
+    x_other = lax.ppermute(patches, "exp", half_swap)
+    got_other = send(jnp.dot(dispatch_mat, x_other, preferred_element_type=f32).astype(bf16))
+    first = half == 0
+    got_x = jnp.concatenate(
+        [jnp.where(first, got_own, got_other), jnp.where(first, got_other, got_own)], axis=1
+    )
+    grad_out, got_x = lax.optimization_barrier((grad_out, got_x))
     sub_dy = core_subset(grad_out)
     dy_buf = jnp.dot(dispatch_mat, sub_dy, preferred_element_type=f32)
     d_buf = (gate_slot[:, None] * dy_buf).astype(bf16)
-
-    def pick_by(index, values):
-        picked = values[0]
-        for i, value in enumerate(values[1:], start=1):
-            picked = jnp.where(index == i, value, picked)
-        return picked
-
-    def to_experts(buf):
-        got = lax.all_to_all(
-            buf.reshape(sections, capacity, sub_w), "attn", split_axis=0, concat_axis=0, tiled=True
-        ).reshape(slots, sub_w)
-        by_shift = [got] + [lax.ppermute(got, "exp", core_shift(s)) for s in range(1, cores)]
-        ordered = [pick_by((core - source) % cores, by_shift) for source in range(cores)]
-        return jnp.concatenate(
-            [ordered[q][:, p * slice_w:(p + 1) * slice_w] for p in range(EXP_DEV) for q in range(cores)],
-            axis=1,
-        )
-
-    x_rows = to_experts(x_buf)
+    x_rows = to_experts(got_x)
     d_buf, x_rows = lax.optimization_barrier((d_buf, x_rows))
-    d_rows = to_experts(d_buf)
+    d_rows = to_experts(send(d_buf))
 
     if n_loc == 1:
         up_mat = w_up[0]
@@ -119,7 +125,7 @@
         out_loc = out_g if out_loc is None else out_loc + out_g
         dx_loc = dx_g if dx_loc is None else dx_loc + dx_g
 
-    def to_sections(rows, hold):
+    def group_sum(rows, hold):
         subsets = [
             jnp.concatenate(
                 [rows[:, (p * cores + q) * slice_w:(p * cores + q + 1) * slice_w] for p in range(EXP_DEV)],
@@ -132,23 +138,7 @@
             theirs = pick_by((core + s) % cores, subsets)
             got = lax.ppermute(theirs.astype(bf16), "exp", core_shift(s))
             summed = summed + got.astype(f32)
-        sent, hold = lax.optimization_barrier((summed.astype(bf16), hold))
-        back = lax.all_to_all(
-            sent.reshape(sections, capacity, sub_w), "attn", split_axis=0, concat_axis=0, tiled=True
-        )
-        return back.reshape(slots, sub_w), hold
-
-    back_out, (act_late, d_late) = to_sections(out_loc, (activation, d_rows))
-    grad_down = jnp.einsum("sh,sd->hd", act_late, d_late, preferred_element_type=f32)
-    back_dx, (x_late, pre_late) = to_sections(dx_loc, (x_rows, grad_pre))
-    grad_up = jnp.einsum("sd,sh->dh", x_late, pre_late, preferred_element_type=f32)
-
-    mixed_sub = None
-    for k, pick in enumerate(picks):
-        picked = jnp.dot(pick.astype(bf16).T, back_out, preferred_element_type=f32)
-        term = gates[:, k][:, None] * picked
-        mixed_sub = term if mixed_sub is None else mixed_sub + term
-    dx_sub = jnp.dot(dispatch_mat.T, back_dx, preferred_element_type=f32)
+        return lax.optimization_barrier((summed.astype(bf16), hold))
 
     def finish(sub):
         pieces = [sub[:, p * slice_w:(p + 1) * slice_w] for p in range(EXP_DEV)]
@@ -156,8 +146,25 @@
         give = pick_by((half + 1) % EXP_DEV, pieces)
         return (keep + lax.ppermute(give, "exp", half_swap)).astype(bf16)
 
+    sum_out, (act_late, d_late) = group_sum(out_loc, (activation, d_rows))
+    back_out = send(sum_out)
+    grad_down = jnp.einsum("sh,sd->hd", act_late, d_late, preferred_element_type=f32)
+    sum_dx, (x_late, pre_late, grad_down) = group_sum(dx_loc, (x_rows, grad_pre, grad_down))
+    dx_pieces = [sum_dx[:, p * slice_w:(p + 1) * slice_w] for p in range(EXP_DEV)]
+    back_give = send(pick_by((half + 1) % EXP_DEV, dx_pieces))
+    grad_up = jnp.einsum("sd,sh->dh", x_late, pre_late, preferred_element_type=f32)
+    back_give, grad_up = lax.optimization_barrier((back_give, grad_up))
+    dx_give = jnp.dot(dispatch_mat.T, back_give, preferred_element_type=f32)
+    dx_came = lax.ppermute(dx_give, "exp", half_swap)
+    back_keep = send(pick_by(half, dx_pieces))
+    grad_patches = (jnp.dot(dispatch_mat.T, back_keep, preferred_element_type=f32) + dx_came).astype(bf16)
+
+    mixed_sub = None
+    for k, pick in enumerate(picks):
+        picked = jnp.dot(pick.astype(bf16).T, back_out, preferred_element_type=f32)
+        term = gates[:, k][:, None] * picked
+        mixed_sub = term if mixed_sub is None else mixed_sub + term
     mixed = finish(mixed_sub)
-    grad_patches = finish(dx_sub)
     grad_up = jnp.transpose(grad_up.reshape(model_width, n_loc, hid_loc), (1, 0, 2))
     grad_down = grad_down.reshape(n_loc, hid_loc, model_width)
     return (mixed, grad_patches, grad_up, grad_down)

time: 238 us -> 236 us (level)
  blocking collectives: 42.2 us -> 0 us
  starting transfers between devices: 21.5 us -> 35 us
  waiting for transfers between devices: 96.5 us -> 109 us
  matrix products: 41.7 us -> 51 us
    all_to_all x1 -> x0, blocking collectives: 42.2 us -> none  [to_experts(): lax.all_to_all(buf.reshape(sections, capacity, sub_w), 'attn', split_axis...]
    all_to_all x3 -> x6, starting transfers between devices: 13.4 us -> 28.3 us  [send(): lax.all_to_all(buf.reshape(sections, capacity, width), 'attn', split_axis...]
    ppermute x2 -> x4, waiting for transfers between devices: 3.04 us -> 17.2 us  [the longest x1 9.08 us: on_device(): x_other = lax.ppermute(patches, 'exp', half_swap)]
    all_to_all x3 -> x6, waiting for transfers between devices: 78 us -> 84.2 us  [send(): lax.all_to_all(buf.reshape(sections, capacity, width), 'attn', split_axis...]
    ppermute x2 -> x1, waiting for transfers between devices: 13.8 us -> 8.01 us  [core_subset(): other = lax.ppermute(local, 'exp', half_swap)]
    dot_general x2 -> x4, matrix products: 2.96 us -> 7.9 us  [the longest x1 2.44 us: on_device(): jnp.dot(dispatch_mat, patches, preferred_element_type=f32).astype(bf16)]
    dot_general x1, matrix products: 6.6 us -> 10.5 us  [on_device(): jnp.einsum('sh,sd->hd', act_late, d_late, preferred_element_type=f32)]
    ppermute x2 -> x4, starting transfers between devices: 0.57 us -> 3.63 us  [the longest x1 1.57 us: on_device(): dx_came = lax.ppermute(dx_give, 'exp', half_swap)]
  transfers between devices with their start and end apart: 11 -> 14, of which waited for: 7 -> 9; matrix products, arithmetic and copies ran while one was open for 24% -> 26% of each run, Pallas kernels for 0% -> 0%
where the time goes in v3:
time: 236 us; the launch traced here: 235 us
  waiting for transfers between devices  109 us (46%)
  matrix products  51 us (22%)
  starting transfers between devices  35 us (15%)
  other arithmetic  23.6 us (10%)
  local copies, waits for them, and re-layouts  14.8 us (6%)
    all_to_all x6, waiting for transfers between devices, send(): lax.all_to_all(buf.reshape(sections, capacity, width), 'attn', split_axis...  84.2 us
    all_to_all x6, starting transfers between devices, send(): lax.all_to_all(buf.reshape(sections, capacity, width), 'attn', split_axis...  28.3 us
    dot_general x1, matrix products, on_device(): jnp.einsum('sh,sd->hd', act_late, d_late, preferred_element_type=f32)  10.5 us
    ppermute x1, waiting for transfers between devices, on_device(): x_other = lax.ppermute(patches, 'exp', half_swap)  9.08 us
    ppermute x1, waiting for transfers between devices, on_device(): dx_came = lax.ppermute(dx_give, 'exp', half_swap)  8.11 us
    ppermute x1, waiting for transfers between devices, core_subset(): other = lax.ppermute(local, 'exp', half_swap)  8.01 us
    dot_general x1, matrix products, on_device(): jnp.einsum('sd,sh->dh', x_late, pre_late, preferred_element_type=f32)  7.7 us
    convert_element_type x2, other arithmetic, group_sum(): return lax.optimization_barrier((summed.astype(bf16), hold))  7.61 us
  transfers between devices with their start and end apart: 14, of which 9 were waited for; matrix products, arithmetic and copies ran while one was open for 26% of the time, Pallas kernels for 0%

profile of v3, /device:TPU:0, one launch (start us, length us, event | category | flops | bytes accessed | tf_op | source)
XLA Modules:
  0.0 234.8 jit_solution(3912431646740720626)
XLA Ops:
  0.6 0.7 broadcast_compare_fusion
  1.3 0.8 copy.30
  2.6 0.9 reduce-window.6
  3.8 0.2 slice_reduce_fusion.2
  4.3 0.2 slice_reduce_fusion
  4.6 2.4 %convolution_convert_fusion.1 = bf16[384,1024]{1,0:T(8,128)(2,1)} fusion(bf16[192,1024]{1,0:T(8,128)(2,1)} %param.6, s32[192]{0:T(256)S(1)} %get-tuple-element.30, s32[192]{0:T(256)S(1)} %get-tuple-element.31, pred[192]{0:T(512)(128)(4,1)S(1)} %get-tuple-element.32, pred[192]{0:T(512)(128)(4,1)S(1)} %get-tuple-element.33), kind=kOutput, calls=%fused_computation.35 | convolution fusion | flops 151756800 | bytes 1181568 | tf_op jit(solution)/shard_map/dot_general | solution.py:90
  7.0 7.3 %all-to-all-start = ((bf16[8,48,1024]{2,1,0:T(8,128)(2,1)}), bf16[8,48,1024]{2,1,0:T(8,128)(2,1)S(1)}, u32[]{:S(2)}, u32[]{:S(2)}) async-start(bf16[8,48,1024]{2,1,0:T(8,128)(2,1)} %bitcast.3), calls=%async_computation | async-start | bytes 1572864 | tf_op jit(solution)/shard_map/all_to_all | solution.py:86
  14.3 1.6 collective-permute-start
  15.9 9.1 %collective-permute-done = bf16[192,1024]{1,0:T(8,128)(2,1)S(1)} collective-permute-done((bf16[192,1024]{1,0:T(8,128)(2,1)S(1)}, bf16[192,1024]{1,0:T(8,128)(2,1)S(1)}, u32[]{:S(2)}, u32[]{:S(2)}) %collective-permute-start) | collective-permute-done | bytes 393248 | tf_op jit(solution)/shard_map/ppermute | solution.py:91
  24.9 1.4 convolution_convert_fusion
  26.4 8.1 %all-to-all-done = bf16[8,48,1024]{2,1,0:T(8,128)(2,1)S(1)} async-done(((bf16[8,48,1024]{2,1,0:T(8,128)(2,1)}), bf16[8,48,1024]{2,1,0:T(8,128)(2,1)S(1)}, u32[]{:S(2)}, u32[]{:S(2)}) %all-to-all-start) | async-done | bytes 786464 | tf_op jit(solution)/shard_map/all_to_all | solution.py:86
  34.5 3.6 %all-to-all-start.1 = ((bf16[8,48,1024]{2,1,0:T(8,128)(2,1)}), bf16[8,48,1024]{2,1,0:T(8,128)(2,1)S(1)}, u32[]{:S(2)}, u32[]{:S(2)}) async-start(bf16[8,48,1024]{2,1,0:T(8,128)(2,1)} %bitcast.4), calls=%async_computation.1 | async-start | bytes 1572864 | tf_op jit(solution)/shard_map/all_to_all | solution.py:86
  38.0 20.4 %all-to-all-done.1 = bf16[8,48,1024]{2,1,0:T(8,128)(2,1)S(1)} async-done(((bf16[8,48,1024]{2,1,0:T(8,128)(2,1)}), bf16[8,48,1024]{2,1,0:T(8,128)(2,1)S(1)}, u32[]{:S(2)}, u32[]{:S(2)}) %all-to-all-start.1) | async-done | bytes 786464 | tf_op jit(solution)/shard_map/all_to_all | solution.py:86
  58.7 0.8 copy-done.17
  59.5 1.5 collective-permute-start.1
  61.0 0.8 fusion.67
  61.8 0.2 select_reduce_fusion
  62.0 0.3 copy-done.18
  62.3 8.0 %collective-permute-done.1 = bf16[192,1024]{1,0:T(8,128)(2,1)} collective-permute-done((bf16[192,1024]{1,0:T(8,128)(2,1)S(1)}, bf16[192,1024]{1,0:T(8,128)(2,1)}, u32[]{:S(2)}, u32[]{:S(2)}) %collective-permute-start.1) | collective-permute-done | bytes 393248 | tf_op jit(solution)/shard_map/ppermute | solution.py:49
  70.4 1.1 broadcast_select_fusion.9
  71.4 1.9 multiply_convert_fusion
  73.6 0.4 fusion.65
  74.0 0.3 pad_maximum_fusion
  74.3 4.5 %all-to-all-start.2 = ((bf16[8,48,2048]{2,1,0:T(8,128)(2,1)}), bf16[8,48,2048]{2,1,0:T(8,128)(2,1)}, u32[]{:S(2)}, u32[]{:S(2)}) async-start(bf16[8,48,2048]{2,1,0:T(8,128)(2,1)} %bitcast.84), calls=%async_computation.2 | async-start | bytes 3145728 | tf_op jit(solution)/shard_map/all_to_all | solution.py:86
  78.8 6.5 %multiply_convert_fusion.1 = (bf16[384,768]{1,0:T(8,128)(2,1)S(1)}, f32[384,768]{1,0:T(8,128)}) fusion(bf16[384,4096]{1,0:T(8,128)(2,1)S(1)} %pad_maximum_fusion, bf16[1,4096,768]{2,1,0:T(8,128)(2,1)} %param.10), kind=kOutput, calls=%fused_computation.44 | convolution fusion | flops 2418573312 | bytes 11206656 | tf_op jit(solution)/shard_map/dot_general | solution.py:111
  85.3 0.8 copy-done.14
  86.1 4.8 %fusion.17 = f32[384,4096]{1,0:T(8,128)S(1)} fusion(bf16[384,768]{1,0:T(8,128)(2,1)S(1)} %get-tuple-element.22, bf16[1,768,4096]{2,1,0:T(8,128)(2,1)} %param.11), kind=kOutput, calls=%fused_computation.11 | convolution fusion | flops 2419064832 | bytes 13172736 | tf_op jit(solution)/shard_map/dot_general | solution.py:121
  90.9 1.1 fusion.62
  92.0 1.9 select_convert_fusion.1
  94.1 0.6 copy-done.12
  94.7 0.5 copy-done.13
  95.2 19.7 %all-to-all-done.2 = bf16[8,48,2048]{2,1,0:T(8,128)(2,1)} async-done(((bf16[8,48,2048]{2,1,0:T(8,128)(2,1)}), bf16[8,48,2048]{2,1,0:T(8,128)(2,1)}, u32[]{:S(2)}, u32[]{:S(2)}) %all-to-all-start.2) | async-done | bytes 1572896 | tf_op jit(solution)/shard_map/all_to_all | solution.py:86
  114.9 5.3 %add_convert_fusion.1 = bf16[384,2048]{1,0:T(8,128)(2,1)} fusion(bf16[384,2048]{1,0:T(8,128)(2,1)} %collective-permute-done.3, f32[384,1024]{1,0:T(8,128)} %copy-done.11, f32[384,1024]{1,0:T(8,128)} %copy-done.12, f32[384,1024]{1,0:T(8,128)} %copy-done.13, f32[384,1024]{1,0:T(8,128)} %copy-done.10, pred[]{:T(512)S(6)} %eq.116), kind=kLoop, calls=%fused_computation.20 | loop fusion | flops 4718592 | bytes 9437185 | tf_op jit(solution)/shard_map/convert_element_type | solution.py:141
  120.2 2.2 broadcast_select_fusion.2
  122.7 1.8 pad_maximum_fusion.3
  124.5 0.5 slice-done.1
  125.0 0.7 copy-done.22
  125.7 3.1 %fusion.24 = bf16[384,768]{1,0:T(8,128)(2,1)S(1)} fusion(bf16[1,768,4096]{2,1,0:T(8,128)(2,1)S(1)} %bitcast.78, f32[384,768]{1,0:T(8,128)S(1)} %copy-done.22, bf16[384,1024]{1,0:T(8,128)(2,1)S(1)} %get-tuple-element.51, bf16[384,1024]{1,0:T(8,128)(2,1)S(1)} %get-tuple-element.49, bf16[384,1024]{1,0:T(8,128)(2,1)S(1)} %get-tuple-element.50, ...), kind=kOutput, calls=%fused_computation.36 | convolution fusion | flops 2434105344 | bytes 11206656 | tf_op jit(solution)/shard_map/sd,hd->sh/dot_general | solution.py:114
  128.9 4.5 %fusion.11 = f32[384,4096]{1,0:T(8,128)} fusion(bf16[384,768]{1,0:T(8,128)(2,1)S(1)} %fusion.24, bf16[1,4096,768]{2,1,0:T(8,128)(2,1)S(1)} %bitcast.91), kind=kOutput, calls=%fused_computation.9 | convolution fusion | flops 2419064832 | bytes 13172736 | tf_op jit(solution)/shard_map/sh,dh->sd/dot_general | solution.py:122
  133.4 4.5 %all-to-all-start.3 = ((bf16[8,48,2048]{2,1,0:T(8,128)(2,1)}), bf16[8,48,2048]{2,1,0:T(8,128)(2,1)}, u32[]{:S(2)}, u32[]{:S(2)}) async-start(bf16[8,48,2048]{2,1,0:T(8,128)(2,1)} %bitcast.79), calls=%async_computation.3 | async-start | bytes 3145728 | tf_op jit(solution)/shard_map/all_to_all | solution.py:86
  138.0 3.4 %fusion.61 = (f32[384,1024]{1,0:T(8,128)S(1)}, f32[384,1024]{1,0:T(8,128)S(1)}, f32[384,1024]{1,0:T(8,128)S(1)}, f32[384,1024]{1,0:T(8,128)S(1)}) fusion(f32[384,4096]{1,0:T(8,128)} %fusion.11), kind=kLoop, calls=%fused_computation.94 | loop fusion | bytes 12582912 | tf_op jit(solution)/shard_map/slice | solution.py:131
  141.4 1.9 select_convert_fusion
  143.5 0.6 copy-done.4
  144.1 0.4 copy-done.6
  144.5 0.5 collective-permute-start.6
  145.0 10.5 %fusion.68 = f32[768,4096]{1,0:T(8,128)} fusion(bf16[384,768]{1,0:T(8,128)(2,1)} %copy-done.14, bf16[384,4096]{1,0:T(8,128)(2,1)} %pad_maximum_fusion.3), kind=kOutput, calls=%fused_computation.101 | convolution fusion | flops 2415919104 | bytes 16318464 | tf_op jit(solution)/shard_map/sh,sd->hd/dot_general | solution.py:151
  155.5 2.3 add_convert_fusion
  157.8 1.2 broadcast_select_fusion.5
  159.1 16.6 %all-to-all-done.3 = bf16[8,48,2048]{2,1,0:T(8,128)(2,1)} async-done(((bf16[8,48,2048]{2,1,0:T(8,128)(2,1)}), bf16[8,48,2048]{2,1,0:T(8,128)(2,1)}, u32[]{:S(2)}, u32[]{:S(2)}) %all-to-all-start.3) | async-done | bytes 1572896 | tf_op jit(solution)/shard_map/all_to_all | solution.py:86
  175.7 4.2 %all-to-all-start.5 = ((bf16[8,48,1024]{2,1,0:T(8,128)(2,1)}), bf16[8,48,1024]{2,1,0:T(8,128)(2,1)}, u32[]{:S(2)}, u32[]{:S(2)}) async-start(bf16[8,48,1024]{2,1,0:T(8,128)(2,1)} %bitcast.81), calls=%async_computation.5 | async-start | bytes 1572864 | tf_op jit(solution)/shard_map/all_to_all | solution.py:86
  180.0 2.0 convolution_multiply_fusion.1
  182.0 2.0 fusion.20
  184.1 1.2 copy-done.8
  185.2 1.0 slice_select_fusion
  186.2 1.5 collective-permute-start.5
  187.7 12.6 %all-to-all-done.5 = bf16[8,48,1024]{2,1,0:T(8,128)(2,1)} async-done(((bf16[8,48,1024]{2,1,0:T(8,128)(2,1)}), bf16[8,48,1024]{2,1,0:T(8,128)(2,1)}, u32[]{:S(2)}, u32[]{:S(2)}) %all-to-all-start.5) | async-done | bytes 786464 | tf_op jit(solution)/shard_map/all_to_all | solution.py:86
  200.3 4.2 %all-to-all-start.4 = ((bf16[8,48,1024]{2,1,0:T(8,128)(2,1)}), bf16[8,48,1024]{2,1,0:T(8,128)(2,1)}, u32[]{:S(2)}, u32[]{:S(2)}) async-start(bf16[8,48,1024]{2,1,0:T(8,128)(2,1)} %bitcast.80), calls=%async_computation.4 | async-start | bytes 1572864 | tf_op jit(solution)/shard_map/all_to_all | solution.py:86
  204.5 7.7 %fusion.69 = f32[4096,768]{1,0:T(8,128)} fusion(bf16[384,4096]{1,0:T(8,128)(2,1)S(1)} %pad_maximum_fusion, bf16[384,768]{1,0:T(8,128)(2,1)} %copy-done.15), kind=kOutput, calls=%fused_computation.102 | convolution fusion | flops 2415919104 | bytes 16318464 | tf_op jit(solution)/shard_map/sd,sh->dh/dot_general | solution.py:155
  212.2 1.7 fusion.55
  213.9 1.6 collective-permute-start.7
  215.5 2.0 add_convert_fusion.2
  217.5 6.8 %all-to-all-done.4 = bf16[8,48,1024]{2,1,0:T(8,128)(2,1)} async-done(((bf16[8,48,1024]{2,1,0:T(8,128)(2,1)}), bf16[8,48,1024]{2,1,0:T(8,128)(2,1)}, u32[]{:S(2)}, u32[]{:S(2)}) %all-to-all-start.4) | async-done | bytes 786464 | tf_op jit(solution)/shard_map/all_to_all | solution.py:86
  224.3 8.1 %collective-permute-done.7 = f32[192,1024]{1,0:T(8,128)S(1)} collective-permute-done((f32[192,1024]{1,0:T(8,128)S(1)}, f32[192,1024]{1,0:T(8,128)S(1)}, u32[]{:S(2)}, u32[]{:S(2)}) %collective-permute-start.7) | collective-permute-done | bytes 786464 | tf_op jit(solution)/shard_map/ppermute | solution.py:158
  232.5 2.3 fusion.27
  (70 shorter events, 2.4 us)
Async XLA Ops:
  4.3 10.0 %copy-start.16 = (bf16[192,1024]{1,0:T(8,128)(2,1)S(1)}, bf16[192,1024]{1,0:T(8,128)(2,1)}, u32[]{:S(2)}) copy-start(bf16[192,1024]{1,0:T(8,128)(2,1)} %param.6) | copy-start | bytes 1179652
  7.0 27.5 %all-to-all-start = ((bf16[8,48,1024]{2,1,0:T(8,128)(2,1)}), bf16[8,48,1024]{2,1,0:T(8,128)(2,1)S(1)}, u32[]{:S(2)}, u32[]{:S(2)}) async-start(bf16[8,48,1024]{2,1,0:T(8,128)(2,1)} %bitcast.3), calls=%async_computation | async-start | bytes 1572864 | tf_op jit(solution)/shard_map/all_to_all | solution.py:86
  14.3 10.6 %collective-permute-start = (bf16[192,1024]{1,0:T(8,128)(2,1)S(1)}, bf16[192,1024]{1,0:T(8,128)(2,1)S(1)}, u32[]{:S(2)}, u32[]{:S(2)}) collective-permute-start(bf16[192,1024]{1,0:T(8,128)(2,1)S(1)} %copy-done.16), channel_id=1, source_target_pairs={{0,2},{1,3},{2,0},{3,1},{4,6},{5,7},{6,4},{7,5},{8,10},{9,11},{10,... | collective-permute-start | bytes 1179656 | tf_op jit(solution)/shard_map/ppermute | solution.py:91
  34.5 23.9 %all-to-all-start.1 = ((bf16[8,48,1024]{2,1,0:T(8,128)(2,1)}), bf16[8,48,1024]{2,1,0:T(8,128)(2,1)S(1)}, u32[]{:S(2)}, u32[]{:S(2)}) async-start(bf16[8,48,1024]{2,1,0:T(8,128)(2,1)} %bitcast.4), calls=%async_computation.1 | async-start | bytes 1572864 | tf_op jit(solution)/shard_map/all_to_all | solution.py:86
  58.5 1.0 copy-start.17
  58.7 14.7 %collective-permute-start.2 = (bf16[384,2048]{1,0:T(8,128)(2,1)S(1)}, bf16[384,2048]{1,0:T(8,128)(2,1)S(1)}, u32[]{:S(2)}, u32[]{:S(2)}) collective-permute-start(bf16[384,2048]{1,0:T(8,128)(2,1)S(1)} %pad_maximum_fusion.6), channel_id=1, source_target_pairs={{0,1},{1,0},{2,3},{3,2},{4,5},{5,4},{6,7},{7,6},{8,9},{9,8},{10,11... | collective-permute-start | bytes 4718600 | tf_op jit(solution)/shard_map/ppermute | solution.py:62
  59.5 10.8 %collective-permute-start.1 = (bf16[192,1024]{1,0:T(8,128)(2,1)S(1)}, bf16[192,1024]{1,0:T(8,128)(2,1)}, u32[]{:S(2)}, u32[]{:S(2)}) collective-permute-start(bf16[192,1024]{1,0:T(8,128)(2,1)S(1)} %copy-done.17), channel_id=1, source_target_pairs={{0,2},{1,3},{2,0},{3,1},{4,6},{5,7},{6,4},{7,5},{8,10},{9,11},{10,... | collective-permute-start | bytes 1179656 | tf_op jit(solution)/shard_map/ppermute | solution.py:49
  61.8 0.6 copy-start.18
  61.8 0.6 copy-start.20
  74.3 40.6 %all-to-all-start.2 = ((bf16[8,48,2048]{2,1,0:T(8,128)(2,1)}), bf16[8,48,2048]{2,1,0:T(8,128)(2,1)}, u32[]{:S(2)}, u32[]{:S(2)}) async-start(bf16[8,48,2048]{2,1,0:T(8,128)(2,1)} %bitcast.84), calls=%async_computation.2 | async-start | bytes 3145728 | tf_op jit(solution)/shard_map/all_to_all | solution.py:86
  85.3 0.8 copy-start.14
  92.0 1.9 copy-start.10
  92.0 2.1 copy-start.11
  92.0 2.7 %copy-start.12 = (f32[384,1024]{1,0:T(8,128)}, f32[384,1024]{1,0:T(8,128)S(1)}, u32[]{:S(2)}) copy-start(f32[384,1024]{1,0:T(8,128)S(1)} %get-tuple-element.40) | copy-start | bytes 4718596
  92.0 3.2 %copy-start.13 = (f32[384,1024]{1,0:T(8,128)}, f32[384,1024]{1,0:T(8,128)S(1)}, u32[]{:S(2)}) copy-start(f32[384,1024]{1,0:T(8,128)S(1)} %get-tuple-element.41) | copy-start | bytes 4718596
  95.2 19.7 %collective-permute-start.3 = (bf16[384,2048]{1,0:T(8,128)(2,1)}, bf16[384,2048]{1,0:T(8,128)(2,1)}, u32[]{:S(2)}, u32[]{:S(2)}) collective-permute-start(bf16[384,2048]{1,0:T(8,128)(2,1)} %select_convert_fusion.1), channel_id=1, source_target_pairs={{0,1},{1,0},{2,3},{3,2},{4,5},{5,4},{6,7},{7,6},{8,9},{9,8},{10,11... | collective-permute-start | bytes 4718600 | tf_op jit(solution)/shard_map/ppermute | solution.py:139
  114.8 5.3 %collective-permute-start.4 = (bf16[384,2048]{1,0:T(8,128)(2,1)}, bf16[384,2048]{1,0:T(8,128)(2,1)}, u32[]{:S(2)}, u32[]{:S(2)}) collective-permute-start(bf16[384,2048]{1,0:T(8,128)(2,1)} %bitcast.10), channel_id=1, source_target_pairs={{0,1},{1,0},{2,3},{3,2},{4,5},{5,4},{6,7},{7,6},{8,9},{9,8},{10,11... | collective-permute-start | bytes 4718600 | tf_op jit(solution)/shard_map/ppermute | solution.py:62
  120.2 4.4 %slice-start = ((s8[6291456]{0:T(1024)(128)(4,1)}), s8[4194304]{0:T(1024)(128)(4,1)S(1)}, s32[]{:S(2)}) async-start(s8[6291456]{0:T(1024)(128)(4,1)} %bitcast.77), calls=%async_computation.6 | async-start | bytes 8388608
  122.5 2.4 %slice-start.1 = ((s8[6291456]{0:T(1024)(128)(4,1)}), s8[2097152]{0:T(1024)(128)(4,1)S(1)}, s32[]{:S(2)}) async-start(s8[6291456]{0:T(1024)(128)(4,1)} %bitcast.77), calls=%async_computation.7 | async-start | bytes 4194304
  122.7 3.0 %copy-start.22 = (f32[384,768]{1,0:T(8,128)S(1)}, f32[384,768]{1,0:T(8,128)}, u32[]{:S(2)}) copy-start(f32[384,768]{1,0:T(8,128)} %get-tuple-element.63) | copy-start | bytes 3538948
  122.7 6.2 %slice-start.2 = ((s8[6291456]{0:T(1024)(128)(4,1)}), s8[4194304]{0:T(1024)(128)(4,1)S(1)}, s32[]{:S(2)}) async-start(s8[6291456]{0:T(1024)(128)(4,1)} %bitcast.90), calls=%async_computation.8 | async-start | bytes 8388608
  125.7 3.2 %slice-start.3 = ((s8[6291456]{0:T(1024)(128)(4,1)}), s8[2097152]{0:T(1024)(128)(4,1)S(1)}, s32[]{:S(2)}) async-start(s8[6291456]{0:T(1024)(128)(4,1)} %bitcast.90), calls=%async_computation.9 | async-start | bytes 4194304
  128.9 4.5 %copy-start.15 = (bf16[384,768]{1,0:T(8,128)(2,1)}, bf16[384,768]{1,0:T(8,128)(2,1)S(1)}, u32[]{:S(2)}) copy-start(bf16[384,768]{1,0:T(8,128)(2,1)S(1)} %fusion.24) | copy-start | bytes 1769476
  133.4 42.3 %all-to-all-start.3 = ((bf16[8,48,2048]{2,1,0:T(8,128)(2,1)}), bf16[8,48,2048]{2,1,0:T(8,128)(2,1)}, u32[]{:S(2)}, u32[]{:S(2)}) async-start(bf16[8,48,2048]{2,1,0:T(8,128)(2,1)} %bitcast.79), calls=%async_computation.3 | async-start | bytes 3145728 | tf_op jit(solution)/shard_map/all_to_all | solution.py:86
  141.4 1.9 copy-start
  141.4 2.1 copy-start.2
  141.4 2.7 %copy-start.4 = (f32[384,1024]{1,0:T(8,128)}, f32[384,1024]{1,0:T(8,128)S(1)}, u32[]{:S(2)}) copy-start(f32[384,1024]{1,0:T(8,128)S(1)} %get-tuple-element.36) | copy-start | bytes 4718596
  141.4 3.1 %copy-start.6 = (f32[384,1024]{1,0:T(8,128)}, f32[384,1024]{1,0:T(8,128)S(1)}, u32[]{:S(2)}) copy-start(f32[384,1024]{1,0:T(8,128)S(1)} %get-tuple-element.37) | copy-start | bytes 4718596
  144.5 11.0 %collective-permute-start.6 = (bf16[384,2048]{1,0:T(8,128)(2,1)}, bf16[384,2048]{1,0:T(8,128)(2,1)}, u32[]{:S(2)}, u32[]{:S(2)}) collective-permute-start(bf16[384,2048]{1,0:T(8,128)(2,1)} %select_convert_fusion), channel_id=1, source_target_pairs={{0,1},{1,0},{2,3},{3,2},{4,5},{5,4},{6,7},{7,6},{8,9},{9,8},{10,11... | collective-permute-start | bytes 4718600 | tf_op jit(solution)/shard_map/ppermute | solution.py:139
  145.0 10.5 %copy-start.1 = (f32[384,1024]{1,0:T(8,128)S(1)}, f32[384,1024]{1,0:T(8,128)}, u32[]{:S(2)}) copy-start(f32[384,1024]{1,0:T(8,128)} %copy-done) | copy-start | bytes 4718596
  145.0 10.5 %copy-start.3 = (f32[384,1024]{1,0:T(8,128)S(1)}, f32[384,1024]{1,0:T(8,128)}, u32[]{:S(2)}) copy-start(f32[384,1024]{1,0:T(8,128)} %copy-done.2) | copy-start | bytes 4718596
  145.0 10.5 %copy-start.5 = (f32[384,1024]{1,0:T(8,128)S(1)}, f32[384,1024]{1,0:T(8,128)}, u32[]{:S(2)}) copy-start(f32[384,1024]{1,0:T(8,128)} %copy-done.4) | copy-start | bytes 4718596
  145.0 10.5 %copy-start.7 = (f32[384,1024]{1,0:T(8,128)S(1)}, f32[384,1024]{1,0:T(8,128)}, u32[]{:S(2)}) copy-start(f32[384,1024]{1,0:T(8,128)} %copy-done.6) | copy-start | bytes 4718596
  159.1 20.9 %copy-start.21 = (f32[192,1]{0,1:T(1,128)S(1)}, f32[192,1]{0,1:T(1,128)}, u32[]{:S(2)}) copy-start(f32[192,1]{0,1:T(1,128)} %copy-done.20) | copy-start | bytes 2308
  175.7 24.6 %all-to-all-start.5 = ((bf16[8,48,1024]{2,1,0:T(8,128)(2,1)}), bf16[8,48,1024]{2,1,0:T(8,128)(2,1)}, u32[]{:S(2)}, u32[]{:S(2)}) async-start(bf16[8,48,1024]{2,1,0:T(8,128)(2,1)} %bitcast.81), calls=%async_computation.5 | async-start | bytes 1572864 | tf_op jit(solution)/shard_map/all_to_all | solution.py:86
  179.9 2.1 copy-start.19
  184.0 1.2 copy-start.8
  186.2 29.3 %collective-permute-start.5 = (f32[192,1024]{1,0:T(8,128)}, f32[192,1024]{1,0:T(8,128)}, u32[]{:S(2)}, u32[]{:S(2)}) collective-permute-start(f32[192,1024]{1,0:T(8,128)} %slice_select_fusion), channel_id=1, source_target_pairs={{0,2},{1,3},{2,0},{3,1},{4,6},{5,7},{6,4},{7,5},{8,10},{9,11},{10,... | collective-permute-start | bytes 2359304 | tf_op jit(solution)/shard_map/ppermute | solution.py:147
  200.3 24.1 %all-to-all-start.4 = ((bf16[8,48,1024]{2,1,0:T(8,128)(2,1)}), bf16[8,48,1024]{2,1,0:T(8,128)(2,1)}, u32[]{:S(2)}, u32[]{:S(2)}) async-start(bf16[8,48,1024]{2,1,0:T(8,128)(2,1)} %bitcast.80), calls=%async_computation.4 | async-start | bytes 1572864 | tf_op jit(solution)/shard_map/all_to_all | solution.py:86
  212.2 3.3 %copy-start.9 = (f32[192,2048]{1,0:T(8,128)S(1)}, f32[192,2048]{1,0:T(8,128)}, u32[]{:S(2)}) copy-start(f32[192,2048]{1,0:T(8,128)} %copy-done.8) | copy-start | bytes 4718596
  213.9 18.5 %collective-permute-start.7 = (f32[192,1024]{1,0:T(8,128)S(1)}, f32[192,1024]{1,0:T(8,128)S(1)}, u32[]{:S(2)}, u32[]{:S(2)}) collective-permute-start(f32[192,1024]{1,0:T(8,128)S(1)} %fusion.55), channel_id=1, source_target_pairs={{0,2},{1,3},{2,0},{3,1},{4,6},{5,7},{6,4},{7,5},{8,10},{9,11},{10,... | collective-permute-start | bytes 2359304 | tf_op jit(solution)/shard_map/ppermute | solution.py:158

commit v4 on v3

--- a/solution.py
+++ b/solution.py
@@ -89,18 +89,19 @@
 
     got_own = send(jnp.dot(dispatch_mat, patches, preferred_element_type=f32).astype(bf16))
     x_other = lax.ppermute(patches, "exp", half_swap)
-    got_other = send(jnp.dot(dispatch_mat, x_other, preferred_element_type=f32).astype(bf16))
+    other_buf = jnp.dot(dispatch_mat, x_other, preferred_element_type=f32).astype(bf16)
+    sub_dy = core_subset(grad_out)
+    sub_dy, other_buf = lax.optimization_barrier((sub_dy, other_buf))
+    got_other = send(other_buf)
     first = half == 0
     got_x = jnp.concatenate(
         [jnp.where(first, got_own, got_other), jnp.where(first, got_other, got_own)], axis=1
     )
-    grad_out, got_x = lax.optimization_barrier((grad_out, got_x))
-    sub_dy = core_subset(grad_out)
     dy_buf = jnp.dot(dispatch_mat, sub_dy, preferred_element_type=f32)
     d_buf = (gate_slot[:, None] * dy_buf).astype(bf16)
     x_rows = to_experts(got_x)
     d_buf, x_rows = lax.optimization_barrier((d_buf, x_rows))
-    d_rows = to_experts(send(d_buf))
+    got_d = send(d_buf)
 
     if n_loc == 1:
         up_mat = w_up[0]
@@ -111,19 +112,13 @@
     pre_act = jnp.dot(x_rows, up_mat, preferred_element_type=f32)
     gelu_value, gelu_slope = gelu_parts(pre_act)
     activation = gelu_value.astype(bf16)
-    grad_act = jnp.einsum("sd,hd->sh", d_rows, down_mat, preferred_element_type=f32)
-    grad_pre = (grad_act * gelu_slope).astype(bf16)
 
     out_loc = None
-    dx_loc = None
     for g in range(n_loc):
         part = slice(g * hid_loc, (g + 1) * hid_loc)
         out_g = jnp.dot(activation[:, part], w_down[g], preferred_element_type=f32)
-        dx_g = jnp.einsum("sh,dh->sd", grad_pre[:, part], w_up[g], preferred_element_type=f32)
         out_g = out_g.astype(bf16).astype(f32)
-        dx_g = dx_g.astype(bf16).astype(f32)
         out_loc = out_g if out_loc is None else out_loc + out_g
-        dx_loc = dx_g if dx_loc is None else dx_loc + dx_g
 
     def group_sum(rows, hold):
         subsets = [
@@ -146,9 +141,18 @@
         give = pick_by((half + 1) % EXP_DEV, pieces)
         return (keep + lax.ppermute(give, "exp", half_swap)).astype(bf16)
 
-    sum_out, (act_late, d_late) = group_sum(out_loc, (activation, d_rows))
+    sum_out, got_d = group_sum(out_loc, got_d)
     back_out = send(sum_out)
-    grad_down = jnp.einsum("sh,sd->hd", act_late, d_late, preferred_element_type=f32)
+    d_rows = to_experts(got_d)
+    grad_act = jnp.einsum("sd,hd->sh", d_rows, down_mat, preferred_element_type=f32)
+    grad_pre = (grad_act * gelu_slope).astype(bf16)
+    dx_loc = None
+    for g in range(n_loc):
+        part = slice(g * hid_loc, (g + 1) * hid_loc)
+        dx_g = jnp.einsum("sh,dh->sd", grad_pre[:, part], w_up[g], preferred_element_type=f32)
+        dx_g = dx_g.astype(bf16).astype(f32)
+        dx_loc = dx_g if dx_loc is None else dx_loc + dx_g
+    grad_down = jnp.einsum("sh,sd->hd", activation, d_rows, preferred_element_type=f32)
     sum_dx, (x_late, pre_late, grad_down) = group_sum(dx_loc, (x_rows, grad_pre, grad_down))
     dx_pieces = [sum_dx[:, p * slice_w:(p + 1) * slice_w] for p in range(EXP_DEV)]
     back_give = send(pick_by((half + 1) % EXP_DEV, dx_pieces))

time: 236 us -> 209 us (0.89)
  waiting for transfers between devices: 109 us -> 65.5 us
  blocking collectives: 0 us -> 23.7 us
  starting transfers between devices: 35 us -> 30.5 us
  local copies, waits for them, and re-layouts: 14.8 us -> 12.1 us
    all_to_all x6 -> x5, waiting for transfers between devices: 84.2 us -> 37.7 us  [send(): lax.all_to_all(buf.reshape(sections, capacity, width), 'attn', split_axis...]
    all_to_all x0 -> x1, blocking collectives: none -> 23.7 us  [send(): lax.all_to_all(buf.reshape(sections, capacity, width), 'attn', split_axis...]
    ppermute x2, waiting for transfers between devices: 0.01 us -> 3.72 us  [group_sum(): got = lax.ppermute(theirs.astype(bf16), 'exp', core_shift(s))]
    all_to_all x6 -> x5, starting transfers between devices: 28.3 us -> 24.8 us  [send(): lax.all_to_all(buf.reshape(sections, capacity, width), 'attn', split_axis...]
    dot_general x1, matrix products: 3.14 us -> 6.46 us  [on_device(): jnp.einsum('sd,hd->sh', d_rows, down_mat, preferred_element_type=f32)]
    ppermute x1, waiting for transfers between devices: 9.08 us -> 5.96 us  [on_device(): x_other = lax.ppermute(patches, 'exp', half_swap)]
    unnamed x55 -> x53, local copies, waits for them, and re-layouts: 7.55 us -> 8.13 us
  transfers between devices with their start and end apart: 14 -> 13, of which waited for: 9 -> 9; matrix products, arithmetic and copies ran while one was open for 26% -> 33% of each run, Pallas kernels for 0% -> 0%
where the time goes in v4:
time: 209 us; the launch traced here: 208 us
  waiting for transfers between devices  65.5 us (31%)
  matrix products  51.9 us (25%)
  starting transfers between devices  30.5 us (15%)
  blocking collectives  23.7 us (11%)
  other arithmetic  23.5 us (11%)
  local copies, waits for them, and re-layouts  12.1 us (6%)
    all_to_all x5, waiting for transfers between devices, send(): lax.all_to_all(buf.reshape(sections, capacity, width), 'attn', split_axis...  37.7 us
    all_to_all x5, starting transfers between devices, send(): lax.all_to_all(buf.reshape(sections, capacity, width), 'attn', split_axis...  24.8 us
    all_to_all x1, blocking collectives, send(): lax.all_to_all(buf.reshape(sections, capacity, width), 'attn', split_axis...  23.7 us
    dot_general x1, matrix products, on_device(): jnp.einsum('sh,sd->hd', activation, d_rows, preferred_element_type=f32)  10.7 us
    ppermute x1, waiting for transfers between devices, core_subset(): other = lax.ppermute(local, 'exp', half_swap)  10 us
    unnamed x53, local copies, waits for them, and re-layouts  8.13 us
    ppermute x1, waiting for transfers between devices, on_device(): dx_came = lax.ppermute(dx_give, 'exp', half_swap)  8.11 us
    dot_general x1, matrix products, on_device(): jnp.einsum('sd,sh->dh', x_late, pre_late, preferred_element_type=f32)  7.7 us
  transfers between devices with their start and end apart: 13, of which 9 were waited for; matrix products, arithmetic and copies ran while one was open for 33% of the time, Pallas kernels for 0%

profile of v4, /device:TPU:0, one launch (start us, length us, event | category | flops | bytes accessed | tf_op | source)
XLA Modules:
  0.0 208.4 jit_solution(15186548311497573408)
XLA Ops:
  0.6 0.7 broadcast_compare_fusion
  1.3 0.8 copy.30
  2.6 0.9 reduce-window.6
  4.5 2.4 %convolution_convert_fusion = bf16[384,1024]{1,0:T(8,128)(2,1)} fusion(bf16[192,1024]{1,0:T(8,128)(2,1)} %param.6, s32[192]{0:T(256)S(1)} %get-tuple-element.29, s32[192]{0:T(256)S(1)} %get-tuple-element.28, pred[192]{0:T(512)(128)(4,1)S(1)} %get-tuple-element.31, pred[192]{0:T(512)(128)(4,1)S(1)} %get-tuple-element.30), kind=kOutput, calls=%fused_computation.34 | convolution fusion | flops 151756800 | bytes 1181568 | tf_op jit(solution)/shard_map/dot_general | solution.py:90
  7.0 7.3 %all-to-all-start = ((bf16[8,48,1024]{2,1,0:T(8,128)(2,1)}), bf16[8,48,1024]{2,1,0:T(8,128)(2,1)S(1)}, u32[]{:S(2)}, u32[]{:S(2)}) async-start(bf16[8,48,1024]{2,1,0:T(8,128)(2,1)} %bitcast.3), calls=%async_computation | async-start | bytes 1572864 | tf_op jit(solution)/shard_map/all_to_all | solution.py:86
  14.3 1.6 collective-permute-start
  15.8 0.5 collective-permute-start.1
  16.3 10.0 %collective-permute-done = bf16[192,1024]{1,0:T(8,128)(2,1)S(1)} collective-permute-done((bf16[192,1024]{1,0:T(8,128)(2,1)S(1)}, bf16[192,1024]{1,0:T(8,128)(2,1)S(1)}, u32[]{:S(2)}, u32[]{:S(2)}) %collective-permute-start) | collective-permute-done | bytes 393248 | tf_op jit(solution)/shard_map/ppermute | solution.py:49
  26.4 0.9 pad_maximum_fusion.7
  27.4 6.0 %collective-permute-done.1 = bf16[192,1024]{1,0:T(8,128)(2,1)S(1)} collective-permute-done((bf16[192,1024]{1,0:T(8,128)(2,1)S(1)}, bf16[192,1024]{1,0:T(8,128)(2,1)S(1)}, u32[]{:S(2)}, u32[]{:S(2)}) %collective-permute-start.1) | collective-permute-done | bytes 393248 | tf_op jit(solution)/shard_map/ppermute | solution.py:91
  33.3 0.6 convolution_convert_fusion.1
  33.9 0.5 all-to-all-done
  34.4 23.7 %all_to_all.30 = bf16[8,48,1024]{2,1,0:T(8,128)(2,1)S(1)} all-to-all(bf16[8,48,1024]{2,1,0:T(8,128)(2,1)S(1)} %bitcast.78), channel_id=1, replica_groups=mesh['attn'=8,'exp'=4] {'attn'}, dimensions={0} | all-to-all | bytes 1572864 | tf_op jit(solution)/shard_map/all_to_all | solution.py:86
  58.5 0.4 copy-done.23
  58.9 0.2 select_reduce_fusion
  59.2 3.0 %multiply_convert_fusion = bf16[384,2048]{1,0:T(8,128)(2,1)} fusion(bf16[192,2048]{1,0:T(8,128)(2,1)} %pad_maximum_fusion.7, f32[384]{0:T(512)S(1)} %add.78, s32[192]{0:T(256)S(1)} %get-tuple-element.29, s32[192]{0:T(256)S(1)} %get-tuple-element.28, pred[192]{0:T(512)(128)(4,1)S(1)} %get-tuple-element.31, pred[192]{0:T(512)(128)(4,1)S(1)} %get-tuple-element.30), kind=kOutput, calls=%fused_computation.22 | convolution fusion | flops 303931392 | bytes 2362752 | tf_op jit(solution)/shard_map/dot_general | solution.py:100
  62.2 2.2 %broadcast_select_fusion.3 = (bf16[384,2048]{1,0:T(8,128)(2,1)S(1)}, bf16[384,2048]{1,0:T(8,128)(2,1)S(1)}) fusion(bf16[384,2048]{1,0:T(8,128)(2,1)} %collective-permute-done.2, pred[]{:T(512)S(6)} %eq.122, bf16[384,1024]{1,0:T(8,128)(2,1)S(1)} %bitcast.74, bf16[384,1024]{1,0:T(8,128)(2,1)S(1)} %bitcast.72, pred[]{:T(512)S(6)} %eq.123), kind=kLoop, calls=%fused_computation.32 | loop fusion | flops 4718592 | bytes 6291458 | tf_op jit(solution)/shard_map/jit(_where)/select_n | solution.py:58
  64.4 0.3 fusion.64
  64.7 0.3 pad_maximum_fusion
  65.0 4.3 %all-to-all-start.2 = ((bf16[8,48,2048]{2,1,0:T(8,128)(2,1)}), bf16[8,48,2048]{2,1,0:T(8,128)(2,1)}, u32[]{:S(2)}, u32[]{:S(2)}) async-start(bf16[8,48,2048]{2,1,0:T(8,128)(2,1)} %bitcast.79), calls=%async_computation.2 | async-start | bytes 3145728 | tf_op jit(solution)/shard_map/all_to_all | solution.py:86
  69.3 5.4 %fusion.6 = f32[384,768]{1,0:T(8,128)S(1)} fusion(bf16[384,4096]{1,0:T(8,128)(2,1)S(1)} %pad_maximum_fusion, bf16[1,4096,768]{2,1,0:T(8,128)(2,1)} %param.10), kind=kOutput, calls=%fused_computation.6 | convolution fusion | flops 2415919104 | bytes 10616832 | tf_op jit(solution)/shard_map/dot_general | solution.py:112
  74.7 1.0 copy-done.18
  75.8 4.9 %fusion.17 = f32[384,4096]{1,0:T(8,128)S(1)} fusion(bf16[1,768,4096]{2,1,0:T(8,128)(2,1)} %param.11, f32[384,768]{1,0:T(8,128)S(1)} %fusion.6), kind=kOutput, calls=%fused_computation.11 | convolution fusion | flops 2421719040 | bytes 13762560 | tf_op jit(solution)/shard_map/dot_general | solution.py:119
  80.7 1.1 fusion.61
  81.8 1.9 select_convert_fusion.1
  83.9 0.5 copy-done.12
  84.5 0.6 copy-done.13
  85.1 3.7 %collective-permute-done.3 = bf16[384,2048]{1,0:T(8,128)(2,1)} collective-permute-done((bf16[384,2048]{1,0:T(8,128)(2,1)}, bf16[384,2048]{1,0:T(8,128)(2,1)}, u32[]{:S(2)}, u32[]{:S(2)}) %collective-permute-start.3) | collective-permute-done | bytes 1572896 | tf_op jit(solution)/shard_map/ppermute | solution.py:134
  88.8 5.3 %add_convert_fusion.1 = bf16[384,2048]{1,0:T(8,128)(2,1)} fusion(bf16[384,2048]{1,0:T(8,128)(2,1)} %collective-permute-done.3, f32[384,1024]{1,0:T(8,128)} %copy-done.11, f32[384,1024]{1,0:T(8,128)} %copy-done.12, f32[384,1024]{1,0:T(8,128)} %copy-done.13, f32[384,1024]{1,0:T(8,128)} %copy-done.10, pred[]{:T(512)S(6)} %eq.116), kind=kLoop, calls=%fused_computation.20 | loop fusion | flops 4718592 | bytes 9437185 | tf_op jit(solution)/shard_map/convert_element_type | solution.py:136
  94.2 12.7 %all-to-all-done.2 = bf16[8,48,2048]{2,1,0:T(8,128)(2,1)} async-done(((bf16[8,48,2048]{2,1,0:T(8,128)(2,1)}), bf16[8,48,2048]{2,1,0:T(8,128)(2,1)}, u32[]{:S(2)}, u32[]{:S(2)}) %all-to-all-start.2) | async-done | bytes 1572896 | tf_op jit(solution)/shard_map/all_to_all | solution.py:86
  106.8 4.5 %all-to-all-start.3 = ((bf16[8,48,2048]{2,1,0:T(8,128)(2,1)}), bf16[8,48,2048]{2,1,0:T(8,128)(2,1)}, u32[]{:S(2)}, u32[]{:S(2)}) async-start(bf16[8,48,2048]{2,1,0:T(8,128)(2,1)} %bitcast.75), calls=%async_computation.3 | async-start | bytes 3145728 | tf_op jit(solution)/shard_map/all_to_all | solution.py:86
  111.3 2.1 %broadcast_select_fusion.2 = (bf16[384,2048]{1,0:T(8,128)(2,1)S(1)}, bf16[384,2048]{1,0:T(8,128)(2,1)S(1)}) fusion(bf16[384,2048]{1,0:T(8,128)(2,1)} %collective-permute-done.5, bf16[384,2048]{1,0:T(8,128)(2,1)} %bitcast.10, pred[]{:T(512)S(6)} %eq.122, pred[]{:T(512)S(6)} %eq.123), kind=kLoop, calls=%fused_computation.31 | loop fusion | flops 1572864 | bytes 6291458 | tf_op jit(solution)/shard_map/jit(_where)/select_n | solution.py:58
  113.8 0.7 copy-done.14
  114.5 0.2 copy-done.15
  114.7 0.2 copy-done.16
  114.9 0.3 copy-done.17
  115.2 0.5 copy-done.19
  115.8 6.5 %fusion.24 = bf16[384,768]{1,0:T(8,128)(2,1)S(1)} fusion(bf16[1,768,4096]{2,1,0:T(8,128)(2,1)} %param.11, f32[384,768]{1,0:T(8,128)S(1)} %copy-done.19, bf16[384,1024]{1,0:T(8,128)(2,1)S(1)} %get-tuple-element.49, bf16[384,1024]{1,0:T(8,128)(2,1)S(1)} %get-tuple-element.47, bf16[384,1024]{1,0:T(8,128)(2,1)S(1)} %get-tuple-element.48, ...), kind=kOutput, calls=%fused_computation.36 | convolution fusion | flops 2434105344 | bytes 11206656 | tf_op jit(solution)/shard_map/sd,hd->sh/dot_general | solution.py:147
  122.3 2.6 %fusion.11 = f32[384,4096]{1,0:T(8,128)S(1)} fusion(bf16[384,768]{1,0:T(8,128)(2,1)S(1)} %fusion.24, bf16[1,4096,768]{2,1,0:T(8,128)(2,1)S(1)} %bitcast.86), kind=kOutput, calls=%fused_computation.9 | convolution fusion | flops 2419064832 | bytes 13172736 | tf_op jit(solution)/shard_map/sh,dh->sd/dot_general | solution.py:152
  124.9 1.1 fusion.60
  126.1 1.8 select_convert_fusion
  127.9 0.3 copy-done.2
  128.2 0.6 copy-done.4
  128.8 0.5 copy-done.6
  129.2 0.5 collective-permute-start.6
  129.8 10.7 %fusion.33 = f32[768,4096]{1,0:T(8,128)} fusion(bf16[384,1024]{1,0:T(8,128)(2,1)} %copy-done.17, bf16[384,1024]{1,0:T(8,128)(2,1)} %copy-done.15, bf16[384,1024]{1,0:T(8,128)(2,1)} %copy-done.16, bf16[384,1024]{1,0:T(8,128)(2,1)} %copy-done.14, f32[384,768]{1,0:T(8,128)} %copy-done.18), kind=kOutput, calls=%fused_computation.52 | convolution fusion | flops 2431156224 | bytes 16908288 | tf_op jit(solution)/shard_map/sh,sd->hd/dot_general | solution.py:155
  140.5 2.3 %add_convert_fusion = bf16[384,2048]{1,0:T(8,128)(2,1)S(1)} fusion(bf16[384,2048]{1,0:T(8,128)(2,1)} %collective-permute-done.6, f32[384,1024]{1,0:T(8,128)S(1)} %copy-done.3, f32[384,1024]{1,0:T(8,128)S(1)} %copy-done.5, f32[384,1024]{1,0:T(8,128)S(1)} %copy-done.7, f32[384,1024]{1,0:T(8,128)S(1)} %copy-done.1, pred[]{:T(512)S(6)} %eq.116), kind=kLoop, calls=%fused_computation.18 | loop fusion | flops 4718592 | bytes 9437185 | tf_op jit(solution)/shard_map/convert_element_type | solution.py:136
  142.8 1.2 broadcast_select_fusion.5
  144.1 5.0 %all-to-all-done.3 = bf16[8,48,2048]{2,1,0:T(8,128)(2,1)} async-done(((bf16[8,48,2048]{2,1,0:T(8,128)(2,1)}), bf16[8,48,2048]{2,1,0:T(8,128)(2,1)}, u32[]{:S(2)}, u32[]{:S(2)}) %all-to-all-start.3) | async-done | bytes 1572896 | tf_op jit(solution)/shard_map/all_to_all | solution.py:86
  149.1 4.2 %all-to-all-start.5 = ((bf16[8,48,1024]{2,1,0:T(8,128)(2,1)}), bf16[8,48,1024]{2,1,0:T(8,128)(2,1)}, u32[]{:S(2)}, u32[]{:S(2)}) async-start(bf16[8,48,1024]{2,1,0:T(8,128)(2,1)} %bitcast.77), calls=%async_computation.5 | async-start | bytes 1572864 | tf_op jit(solution)/shard_map/all_to_all | solution.py:86
  153.3 2.0 convolution_multiply_fusion.1
  155.4 2.0 fusion.20
  157.4 1.2 copy-done.8
  158.6 1.0 slice_select_fusion
  159.6 1.5 collective-permute-start.4
  161.1 12.6 %all-to-all-done.5 = bf16[8,48,1024]{2,1,0:T(8,128)(2,1)} async-done(((bf16[8,48,1024]{2,1,0:T(8,128)(2,1)}), bf16[8,48,1024]{2,1,0:T(8,128)(2,1)}, u32[]{:S(2)}, u32[]{:S(2)}) %all-to-all-start.5) | async-done | bytes 786464 | tf_op jit(solution)/shard_map/all_to_all | solution.py:86
  173.7 4.4 %all-to-all-start.4 = ((bf16[8,48,1024]{2,1,0:T(8,128)(2,1)}), bf16[8,48,1024]{2,1,0:T(8,128)(2,1)}, u32[]{:S(2)}, u32[]{:S(2)}) async-start(bf16[8,48,1024]{2,1,0:T(8,128)(2,1)} %bitcast.76), calls=%async_computation.4 | async-start | bytes 1572864 | tf_op jit(solution)/shard_map/all_to_all | solution.py:86
  178.1 7.7 %fusion.67 = f32[4096,768]{1,0:T(8,128)} fusion(bf16[384,4096]{1,0:T(8,128)(2,1)S(1)} %pad_maximum_fusion, bf16[384,768]{1,0:T(8,128)(2,1)} %copy-done.20), kind=kOutput, calls=%fused_computation.101 | convolution fusion | flops 2415919104 | bytes 16318464 | tf_op jit(solution)/shard_map/sd,sh->dh/dot_general | solution.py:159
  185.8 1.7 fusion.54
  187.5 1.6 collective-permute-start.7
  189.1 2.0 add_convert_fusion.2
  191.1 6.8 %all-to-all-done.4 = bf16[8,48,1024]{2,1,0:T(8,128)(2,1)} async-done(((bf16[8,48,1024]{2,1,0:T(8,128)(2,1)}), bf16[8,48,1024]{2,1,0:T(8,128)(2,1)}, u32[]{:S(2)}, u32[]{:S(2)}) %all-to-all-start.4) | async-done | bytes 786464 | tf_op jit(solution)/shard_map/all_to_all | solution.py:86
  198.0 8.1 %collective-permute-done.7 = f32[192,1024]{1,0:T(8,128)S(1)} collective-permute-done((f32[192,1024]{1,0:T(8,128)S(1)}, f32[192,1024]{1,0:T(8,128)S(1)}, u32[]{:S(2)}, u32[]{:S(2)}) %collective-permute-start.7) | collective-permute-done | bytes 786464 | tf_op jit(solution)/shard_map/ppermute | solution.py:162
  206.1 2.3 %fusion.27 = bf16[192,1024]{1,0:T(8,128)(2,1)} fusion(f32[192,1024]{1,0:T(8,128)S(1)} %collective-permute-done.7, bf16[384,1024]{1,0:T(8,128)(2,1)} %bitcast.14, s32[192]{0:T(256)S(1)} %get-tuple-element.29, s32[192]{0:T(256)S(1)} %get-tuple-element.28, pred[192]{0:T(512)(128)(4,1)S(1)} %get-tuple-element.31, pred[192]{0:T(512)(128)(4,1)S(1)} %get-tuple-element.30), kind=kOutput, calls=%fused_computation.38 | convolution fusion | flops 151756800 | bytes 1968000 | tf_op jit(solution)/shard_map/dot_general | solution.py:164
  (66 shorter events, 2.4 us)
Async XLA Ops:
  4.2 10.0 %copy-start.21 = (bf16[192,1024]{1,0:T(8,128)(2,1)S(1)}, bf16[192,1024]{1,0:T(8,128)(2,1)}, u32[]{:S(2)}) copy-start(bf16[192,1024]{1,0:T(8,128)(2,1)} %param.7) | copy-start | bytes 1179652
  4.2 11.6 %copy-start.22 = (bf16[192,1024]{1,0:T(8,128)(2,1)S(1)}, bf16[192,1024]{1,0:T(8,128)(2,1)}, u32[]{:S(2)}) copy-start(bf16[192,1024]{1,0:T(8,128)(2,1)} %param.6) | copy-start | bytes 1179652
  7.0 27.5 %all-to-all-start = ((bf16[8,48,1024]{2,1,0:T(8,128)(2,1)}), bf16[8,48,1024]{2,1,0:T(8,128)(2,1)S(1)}, u32[]{:S(2)}, u32[]{:S(2)}) async-start(bf16[8,48,1024]{2,1,0:T(8,128)(2,1)} %bitcast.3), calls=%async_computation | async-start | bytes 1572864 | tf_op jit(solution)/shard_map/all_to_all | solution.py:86
  14.3 12.1 %collective-permute-start = (bf16[192,1024]{1,0:T(8,128)(2,1)S(1)}, bf16[192,1024]{1,0:T(8,128)(2,1)S(1)}, u32[]{:S(2)}, u32[]{:S(2)}) collective-permute-start(bf16[192,1024]{1,0:T(8,128)(2,1)S(1)} %copy-done.21), channel_id=1, source_target_pairs={{0,2},{1,3},{2,0},{3,1},{4,6},{5,7},{6,4},{7,5},{8,10},{9,11},{10,... | collective-permute-start | bytes 1179656 | tf_op jit(solution)/shard_map/ppermute | solution.py:49
  15.8 17.5 %collective-permute-start.1 = (bf16[192,1024]{1,0:T(8,128)(2,1)S(1)}, bf16[192,1024]{1,0:T(8,128)(2,1)S(1)}, u32[]{:S(2)}, u32[]{:S(2)}) collective-permute-start(bf16[192,1024]{1,0:T(8,128)(2,1)S(1)} %copy-done.22), channel_id=1, source_target_pairs={{0,2},{1,3},{2,0},{3,1},{4,6},{5,7},{6,4},{7,5},{8,10},{9,11},{10,... | collective-permute-start | bytes 1179656 | tf_op jit(solution)/shard_map/ppermute | solution.py:91
  58.2 0.7 copy-start.23
  58.4 3.8 %collective-permute-start.2 = (bf16[384,2048]{1,0:T(8,128)(2,1)S(1)}, bf16[384,2048]{1,0:T(8,128)(2,1)}, u32[]{:S(2)}, u32[]{:S(2)}) collective-permute-start(bf16[384,2048]{1,0:T(8,128)(2,1)S(1)} %pad_maximum_fusion.6), channel_id=1, source_target_pairs={{0,1},{1,0},{2,3},{3,2},{4,5},{5,4},{6,7},{7,6},{8,9},{9,8},{10,11... | collective-permute-start | bytes 4718600 | tf_op jit(solution)/shard_map/ppermute | solution.py:62
  65.0 41.8 %all-to-all-start.2 = ((bf16[8,48,2048]{2,1,0:T(8,128)(2,1)}), bf16[8,48,2048]{2,1,0:T(8,128)(2,1)}, u32[]{:S(2)}, u32[]{:S(2)}) async-start(bf16[8,48,2048]{2,1,0:T(8,128)(2,1)} %bitcast.79), calls=%async_computation.2 | async-start | bytes 3145728 | tf_op jit(solution)/shard_map/all_to_all | solution.py:86
  74.7 1.0 copy-start.18
  81.8 1.9 copy-start.10
  81.8 2.1 %copy-start.11 = (f32[384,1024]{1,0:T(8,128)}, f32[384,1024]{1,0:T(8,128)S(1)}, u32[]{:S(2)}) copy-start(f32[384,1024]{1,0:T(8,128)S(1)} %get-tuple-element.37) | copy-start | bytes 4718596
  81.8 2.6 %copy-start.12 = (f32[384,1024]{1,0:T(8,128)}, f32[384,1024]{1,0:T(8,128)S(1)}, u32[]{:S(2)}) copy-start(f32[384,1024]{1,0:T(8,128)S(1)} %get-tuple-element.38) | copy-start | bytes 4718596
  81.8 3.2 %copy-start.13 = (f32[384,1024]{1,0:T(8,128)}, f32[384,1024]{1,0:T(8,128)S(1)}, u32[]{:S(2)}) copy-start(f32[384,1024]{1,0:T(8,128)S(1)} %get-tuple-element.39) | copy-start | bytes 4718596
  85.1 3.8 %collective-permute-start.3 = (bf16[384,2048]{1,0:T(8,128)(2,1)}, bf16[384,2048]{1,0:T(8,128)(2,1)}, u32[]{:S(2)}, u32[]{:S(2)}) collective-permute-start(bf16[384,2048]{1,0:T(8,128)(2,1)} %select_convert_fusion.1), channel_id=1, source_target_pairs={{0,1},{1,0},{2,3},{3,2},{4,5},{5,4},{6,7},{7,6},{8,9},{9,8},{10,11... | collective-permute-start | bytes 4718600 | tf_op jit(solution)/shard_map/ppermute | solution.py:134
  106.8 4.5 %collective-permute-start.5 = (bf16[384,2048]{1,0:T(8,128)(2,1)}, bf16[384,2048]{1,0:T(8,128)(2,1)}, u32[]{:S(2)}, u32[]{:S(2)}) collective-permute-start(bf16[384,2048]{1,0:T(8,128)(2,1)} %bitcast.10), channel_id=1, source_target_pairs={{0,1},{1,0},{2,3},{3,2},{4,5},{5,4},{6,7},{7,6},{8,9},{9,8},{10,11... | collective-permute-start | bytes 4718600 | tf_op jit(solution)/shard_map/ppermute | solution.py:62
  106.8 42.3 %all-to-all-start.3 = ((bf16[8,48,2048]{2,1,0:T(8,128)(2,1)}), bf16[8,48,2048]{2,1,0:T(8,128)(2,1)}, u32[]{:S(2)}, u32[]{:S(2)}) async-start(bf16[8,48,2048]{2,1,0:T(8,128)(2,1)} %bitcast.75), calls=%async_computation.3 | async-start | bytes 3145728 | tf_op jit(solution)/shard_map/all_to_all | solution.py:86
  113.6 0.9 copy-start.14
  113.6 1.1 copy-start.15
  113.6 2.2 %copy-start.19 = (f32[384,768]{1,0:T(8,128)S(1)}, f32[384,768]{1,0:T(8,128)}, u32[]{:S(2)}) copy-start(f32[384,768]{1,0:T(8,128)} %copy-done.18) | copy-start | bytes 3538948
  113.6 8.6 %slice-start = ((s8[6291456]{0:T(1024)(128)(4,1)}), s8[4194304]{0:T(1024)(128)(4,1)S(1)}, s32[]{:S(2)}) async-start(s8[6291456]{0:T(1024)(128)(4,1)} %bitcast.85), calls=%async_computation.6 | async-start | bytes 8388608
  113.7 1.2 copy-start.16
  113.8 1.5 copy-start.17
  115.8 6.5 %slice-start.1 = ((s8[6291456]{0:T(1024)(128)(4,1)}), s8[2097152]{0:T(1024)(128)(4,1)S(1)}, s32[]{:S(2)}) async-start(s8[6291456]{0:T(1024)(128)(4,1)} %bitcast.85), calls=%async_computation.7 | async-start | bytes 4194304
  122.3 2.7 %copy-start.20 = (bf16[384,768]{1,0:T(8,128)(2,1)}, bf16[384,768]{1,0:T(8,128)(2,1)S(1)}, u32[]{:S(2)}) copy-start(bf16[384,768]{1,0:T(8,128)(2,1)S(1)} %fusion.24) | copy-start | bytes 1769476
  126.0 1.9 copy-start
  126.1 2.1 %copy-start.2 = (f32[384,1024]{1,0:T(8,128)}, f32[384,1024]{1,0:T(8,128)S(1)}, u32[]{:S(2)}) copy-start(f32[384,1024]{1,0:T(8,128)S(1)} %get-tuple-element.33) | copy-start | bytes 4718596
  126.1 2.7 %copy-start.4 = (f32[384,1024]{1,0:T(8,128)}, f32[384,1024]{1,0:T(8,128)S(1)}, u32[]{:S(2)}) copy-start(f32[384,1024]{1,0:T(8,128)S(1)} %get-tuple-element.34) | copy-start | bytes 4718596
  126.1 3.2 %copy-start.6 = (f32[384,1024]{1,0:T(8,128)}, f32[384,1024]{1,0:T(8,128)S(1)}, u32[]{:S(2)}) copy-start(f32[384,1024]{1,0:T(8,128)S(1)} %get-tuple-element.35) | copy-start | bytes 4718596
  129.2 11.2 %collective-permute-start.6 = (bf16[384,2048]{1,0:T(8,128)(2,1)}, bf16[384,2048]{1,0:T(8,128)(2,1)}, u32[]{:S(2)}, u32[]{:S(2)}) collective-permute-start(bf16[384,2048]{1,0:T(8,128)(2,1)} %select_convert_fusion), channel_id=1, source_target_pairs={{0,1},{1,0},{2,3},{3,2},{4,5},{5,4},{6,7},{7,6},{8,9},{9,8},{10,11... | collective-permute-start | bytes 4718600 | tf_op jit(solution)/shard_map/ppermute | solution.py:134
  129.7 10.7 %copy-start.1 = (f32[384,1024]{1,0:T(8,128)S(1)}, f32[384,1024]{1,0:T(8,128)}, u32[]{:S(2)}) copy-start(f32[384,1024]{1,0:T(8,128)} %copy-done) | copy-start | bytes 4718596
  129.7 10.7 %copy-start.3 = (f32[384,1024]{1,0:T(8,128)S(1)}, f32[384,1024]{1,0:T(8,128)}, u32[]{:S(2)}) copy-start(f32[384,1024]{1,0:T(8,128)} %copy-done.2) | copy-start | bytes 4718596
  129.7 10.7 %copy-start.5 = (f32[384,1024]{1,0:T(8,128)S(1)}, f32[384,1024]{1,0:T(8,128)}, u32[]{:S(2)}) copy-start(f32[384,1024]{1,0:T(8,128)} %copy-done.4) | copy-start | bytes 4718596
  129.7 10.7 %copy-start.7 = (f32[384,1024]{1,0:T(8,128)S(1)}, f32[384,1024]{1,0:T(8,128)}, u32[]{:S(2)}) copy-start(f32[384,1024]{1,0:T(8,128)} %copy-done.6) | copy-start | bytes 4718596
  149.1 24.6 %all-to-all-start.5 = ((bf16[8,48,1024]{2,1,0:T(8,128)(2,1)}), bf16[8,48,1024]{2,1,0:T(8,128)(2,1)}, u32[]{:S(2)}, u32[]{:S(2)}) async-start(bf16[8,48,1024]{2,1,0:T(8,128)(2,1)} %bitcast.77), calls=%async_computation.5 | async-start | bytes 1572864 | tf_op jit(solution)/shard_map/all_to_all | solution.py:86
  157.4 1.2 copy-start.8
  159.6 29.5 %collective-permute-start.4 = (f32[192,1024]{1,0:T(8,128)}, f32[192,1024]{1,0:T(8,128)}, u32[]{:S(2)}, u32[]{:S(2)}) collective-permute-start(f32[192,1024]{1,0:T(8,128)} %slice_select_fusion), channel_id=1, source_target_pairs={{0,2},{1,3},{2,0},{3,1},{4,6},{5,7},{6,4},{7,5},{8,10},{9,11},{10,... | collective-permute-start | bytes 2359304 | tf_op jit(solution)/shard_map/ppermute | solution.py:142
  173.7 24.3 %all-to-all-start.4 = ((bf16[8,48,1024]{2,1,0:T(8,128)(2,1)}), bf16[8,48,1024]{2,1,0:T(8,128)(2,1)}, u32[]{:S(2)}, u32[]{:S(2)}) async-start(bf16[8,48,1024]{2,1,0:T(8,128)(2,1)} %bitcast.76), calls=%async_computation.4 | async-start | bytes 1572864 | tf_op jit(solution)/shard_map/all_to_all | solution.py:86
  185.8 3.3 %copy-start.9 = (f32[192,2048]{1,0:T(8,128)S(1)}, f32[192,2048]{1,0:T(8,128)}, u32[]{:S(2)}) copy-start(f32[192,2048]{1,0:T(8,128)} %copy-done.8) | copy-start | bytes 4718596
  187.5 18.5 %collective-permute-start.7 = (f32[192,1024]{1,0:T(8,128)S(1)}, f32[192,1024]{1,0:T(8,128)S(1)}, u32[]{:S(2)}, u32[]{:S(2)}) collective-permute-start(f32[192,1024]{1,0:T(8,128)S(1)} %fusion.54), channel_id=1, source_target_pairs={{0,2},{1,3},{2,0},{3,1},{4,6},{5,7},{6,4},{7,5},{8,10},{9,11},{10,... | collective-permute-start | bytes 2359304 | tf_op jit(solution)/shard_map/ppermute | solution.py:162

commit v5 on v4

--- a/solution.py
+++ b/solution.py
@@ -156,11 +156,12 @@
     sum_dx, (x_late, pre_late, grad_down) = group_sum(dx_loc, (x_rows, grad_pre, grad_down))
     dx_pieces = [sum_dx[:, p * slice_w:(p + 1) * slice_w] for p in range(EXP_DEV)]
     back_give = send(pick_by((half + 1) % EXP_DEV, dx_pieces))
-    grad_up = jnp.einsum("sd,sh->dh", x_late, pre_late, preferred_element_type=f32)
-    back_give, grad_up = lax.optimization_barrier((back_give, grad_up))
     dx_give = jnp.dot(dispatch_mat.T, back_give, preferred_element_type=f32)
     dx_came = lax.ppermute(dx_give, "exp", half_swap)
     back_keep = send(pick_by(half, dx_pieces))
+    dx_give, x_late, pre_late = lax.optimization_barrier((dx_give, x_late, pre_late))
+    grad_up = jnp.einsum("sd,sh->dh", x_late, pre_late, preferred_element_type=f32)
+    back_keep, grad_up = lax.optimization_barrier((back_keep, grad_up))
     grad_patches = (jnp.dot(dispatch_mat.T, back_keep, preferred_element_type=f32) + dx_came).astype(bf16)
 
     mixed_sub = None

time: 209 us -> 203 us (0.971)
  waiting for transfers between devices: 65.5 us -> 59.2 us
    ppermute x1, waiting for transfers between devices: 8.11 us -> 1.57 us  [on_device(): dx_came = lax.ppermute(dx_give, 'exp', half_swap)]
    unnamed x53 -> x55, local copies, waits for them, and re-layouts: 8.13 us -> 8.07 us
  transfers between devices with their start and end apart: 13 -> 13, of which waited for: 9 -> 9; matrix products, arithmetic and copies ran while one was open for 33% -> 34% of each run, Pallas kernels for 0% -> 0%
where the time goes in v5:
time: 203 us; the launch traced here: 202 us
  waiting for transfers between devices  59.2 us (29%)
  matrix products  52 us (26%)
  starting transfers between devices  30.4 us (15%)
  blocking collectives  23.7 us (12%)
  other arithmetic  23.5 us (12%)
  local copies, waits for them, and re-layouts  12.1 us (6%)
    all_to_all x5, waiting for transfers between devices, send(): lax.all_to_all(buf.reshape(sections, capacity, width), 'attn', split_axis...  38 us
    all_to_all x5, starting transfers between devices, send(): lax.all_to_all(buf.reshape(sections, capacity, width), 'attn', split_axis...  24.7 us
    all_to_all x1, blocking collectives, send(): lax.all_to_all(buf.reshape(sections, capacity, width), 'attn', split_axis...  23.7 us
    dot_general x1, matrix products, on_device(): jnp.einsum('sh,sd->hd', activation, d_rows, preferred_element_type=f32)  10.7 us
    ppermute x1, waiting for transfers between devices, core_subset(): other = lax.ppermute(local, 'exp', half_swap)  10 us
    unnamed x55, local copies, waits for them, and re-layouts  8.07 us
    convert_element_type x2, other arithmetic, group_sum(): return lax.optimization_barrier((summed.astype(bf16), hold))  7.64 us
    dot_general x1, matrix products, on_device(): jnp.einsum('sd,sh->dh', x_late, pre_late, preferred_element_type=f32)  6.61 us
  transfers between devices with their start and end apart: 13, of which 9 were waited for; matrix products, arithmetic and copies ran while one was open for 34% of the time, Pallas kernels for 0%

profile of v5, /device:TPU:0, one launch (start us, length us, event | category | flops | bytes accessed | tf_op | source)
XLA Modules:
  0.0 202.1 jit_solution(15540351808009263347)
XLA Ops:
  0.6 0.7 broadcast_compare_fusion
  1.3 0.8 copy.30
  2.6 0.9 reduce-window.6
  4.5 2.4 %convolution_convert_fusion = bf16[384,1024]{1,0:T(8,128)(2,1)} fusion(bf16[192,1024]{1,0:T(8,128)(2,1)} %param.6, s32[192]{0:T(256)S(1)} %get-tuple-element.33, s32[192]{0:T(256)S(1)} %get-tuple-element.32, pred[192]{0:T(512)(128)(4,1)S(1)} %get-tuple-element.35, pred[192]{0:T(512)(128)(4,1)S(1)} %get-tuple-element.34), kind=kOutput, calls=%fused_computation.34 | convolution fusion | flops 151756800 | bytes 1181568 | tf_op jit(solution)/shard_map/dot_general | solution.py:90
  7.0 7.3 %all-to-all-start = ((bf16[8,48,1024]{2,1,0:T(8,128)(2,1)}), bf16[8,48,1024]{2,1,0:T(8,128)(2,1)S(1)}, u32[]{:S(2)}, u32[]{:S(2)}) async-start(bf16[8,48,1024]{2,1,0:T(8,128)(2,1)} %bitcast.3), calls=%async_computation | async-start | bytes 1572864 | tf_op jit(solution)/shard_map/all_to_all | solution.py:86
  14.3 1.6 collective-permute-start
  15.8 0.5 collective-permute-start.1
  16.3 10.0 %collective-permute-done = bf16[192,1024]{1,0:T(8,128)(2,1)S(1)} collective-permute-done((bf16[192,1024]{1,0:T(8,128)(2,1)S(1)}, bf16[192,1024]{1,0:T(8,128)(2,1)S(1)}, u32[]{:S(2)}, u32[]{:S(2)}) %collective-permute-start) | collective-permute-done | bytes 393248 | tf_op jit(solution)/shard_map/ppermute | solution.py:49
  26.4 0.9 pad_maximum_fusion.7
  27.4 6.0 %collective-permute-done.1 = bf16[192,1024]{1,0:T(8,128)(2,1)S(1)} collective-permute-done((bf16[192,1024]{1,0:T(8,128)(2,1)S(1)}, bf16[192,1024]{1,0:T(8,128)(2,1)S(1)}, u32[]{:S(2)}, u32[]{:S(2)}) %collective-permute-start.1) | collective-permute-done | bytes 393248 | tf_op jit(solution)/shard_map/ppermute | solution.py:91
  33.3 0.6 convolution_convert_fusion.1
  33.9 0.5 all-to-all-done
  34.4 23.7 %all_to_all.30 = bf16[8,48,1024]{2,1,0:T(8,128)(2,1)S(1)} all-to-all(bf16[8,48,1024]{2,1,0:T(8,128)(2,1)S(1)} %bitcast.78), channel_id=1, replica_groups=mesh['attn'=8,'exp'=4] {'attn'}, dimensions={0} | all-to-all | bytes 1572864 | tf_op jit(solution)/shard_map/all_to_all | solution.py:86
  58.5 0.4 copy-done.24
  58.9 0.2 select_reduce_fusion
  59.2 3.0 %multiply_convert_fusion = bf16[384,2048]{1,0:T(8,128)(2,1)} fusion(bf16[192,2048]{1,0:T(8,128)(2,1)} %pad_maximum_fusion.7, f32[384]{0:T(512)S(1)} %add.78, s32[192]{0:T(256)S(1)} %get-tuple-element.33, s32[192]{0:T(256)S(1)} %get-tuple-element.32, pred[192]{0:T(512)(128)(4,1)S(1)} %get-tuple-element.35, pred[192]{0:T(512)(128)(4,1)S(1)} %get-tuple-element.34), kind=kOutput, calls=%fused_computation.22 | convolution fusion | flops 303931392 | bytes 2362752 | tf_op jit(solution)/shard_map/dot_general | solution.py:100
  62.2 2.2 %broadcast_select_fusion.3 = (bf16[384,2048]{1,0:T(8,128)(2,1)S(1)}, bf16[384,2048]{1,0:T(8,128)(2,1)S(1)}) fusion(bf16[384,2048]{1,0:T(8,128)(2,1)} %collective-permute-done.2, pred[]{:T(512)S(6)} %eq.122, bf16[384,1024]{1,0:T(8,128)(2,1)S(1)} %bitcast.74, bf16[384,1024]{1,0:T(8,128)(2,1)S(1)} %bitcast.72, pred[]{:T(512)S(6)} %eq.123), kind=kLoop, calls=%fused_computation.32 | loop fusion | flops 4718592 | bytes 6291458 | tf_op jit(solution)/shard_map/jit(_where)/select_n | solution.py:58
  64.4 0.3 fusion.64
  64.7 0.3 pad_maximum_fusion
  65.0 4.3 %all-to-all-start.2 = ((bf16[8,48,2048]{2,1,0:T(8,128)(2,1)}), bf16[8,48,2048]{2,1,0:T(8,128)(2,1)}, u32[]{:S(2)}, u32[]{:S(2)}) async-start(bf16[8,48,2048]{2,1,0:T(8,128)(2,1)} %bitcast.79), calls=%async_computation.2 | async-start | bytes 3145728 | tf_op jit(solution)/shard_map/all_to_all | solution.py:86
  69.4 5.4 %fusion.6 = f32[384,768]{1,0:T(8,128)S(1)} fusion(bf16[384,4096]{1,0:T(8,128)(2,1)S(1)} %pad_maximum_fusion, bf16[1,4096,768]{2,1,0:T(8,128)(2,1)} %param.10), kind=kOutput, calls=%fused_computation.6 | convolution fusion | flops 2415919104 | bytes 10616832 | tf_op jit(solution)/shard_map/dot_general | solution.py:112
  74.8 1.0 copy-done.18
  75.8 4.9 %fusion.17 = f32[384,4096]{1,0:T(8,128)S(1)} fusion(bf16[1,768,4096]{2,1,0:T(8,128)(2,1)} %param.11, f32[384,768]{1,0:T(8,128)S(1)} %fusion.6), kind=kOutput, calls=%fused_computation.11 | convolution fusion | flops 2421719040 | bytes 13762560 | tf_op jit(solution)/shard_map/dot_general | solution.py:119
  80.7 1.1 fusion.61
  81.9 1.9 select_convert_fusion.1
  84.0 0.5 copy-done.12
  84.5 0.6 copy-done.13
  85.1 3.7 %collective-permute-done.3 = bf16[384,2048]{1,0:T(8,128)(2,1)} collective-permute-done((bf16[384,2048]{1,0:T(8,128)(2,1)}, bf16[384,2048]{1,0:T(8,128)(2,1)}, u32[]{:S(2)}, u32[]{:S(2)}) %collective-permute-start.3) | collective-permute-done | bytes 1572896 | tf_op jit(solution)/shard_map/ppermute | solution.py:134
  88.8 5.3 %add_convert_fusion.1 = bf16[384,2048]{1,0:T(8,128)(2,1)} fusion(bf16[384,2048]{1,0:T(8,128)(2,1)} %collective-permute-done.3, f32[384,1024]{1,0:T(8,128)} %copy-done.11, f32[384,1024]{1,0:T(8,128)} %copy-done.12, f32[384,1024]{1,0:T(8,128)} %copy-done.13, f32[384,1024]{1,0:T(8,128)} %copy-done.10, pred[]{:T(512)S(6)} %eq.116), kind=kLoop, calls=%fused_computation.20 | loop fusion | flops 4718592 | bytes 9437185 | tf_op jit(solution)/shard_map/convert_element_type | solution.py:136
  94.2 12.7 %all-to-all-done.2 = bf16[8,48,2048]{2,1,0:T(8,128)(2,1)} async-done(((bf16[8,48,2048]{2,1,0:T(8,128)(2,1)}), bf16[8,48,2048]{2,1,0:T(8,128)(2,1)}, u32[]{:S(2)}, u32[]{:S(2)}) %all-to-all-start.2) | async-done | bytes 1572896 | tf_op jit(solution)/shard_map/all_to_all | solution.py:86
  106.8 4.5 %all-to-all-start.3 = ((bf16[8,48,2048]{2,1,0:T(8,128)(2,1)}), bf16[8,48,2048]{2,1,0:T(8,128)(2,1)}, u32[]{:S(2)}, u32[]{:S(2)}) async-start(bf16[8,48,2048]{2,1,0:T(8,128)(2,1)} %bitcast.75), calls=%async_computation.3 | async-start | bytes 3145728 | tf_op jit(solution)/shard_map/all_to_all | solution.py:86
  111.4 2.1 %broadcast_select_fusion.2 = (bf16[384,2048]{1,0:T(8,128)(2,1)S(1)}, bf16[384,2048]{1,0:T(8,128)(2,1)S(1)}) fusion(bf16[384,2048]{1,0:T(8,128)(2,1)} %collective-permute-done.5, bf16[384,2048]{1,0:T(8,128)(2,1)} %bitcast.10, pred[]{:T(512)S(6)} %eq.122, pred[]{:T(512)S(6)} %eq.123), kind=kLoop, calls=%fused_computation.31 | loop fusion | flops 1572864 | bytes 6291458 | tf_op jit(solution)/shard_map/jit(_where)/select_n | solution.py:58
  113.8 0.7 copy-done.14
  114.5 0.2 copy-done.15
  114.7 0.3 copy-done.16
  115.0 0.3 copy-done.17
  115.2 0.5 copy-done.19
  115.8 6.5 %fusion.24 = bf16[384,768]{1,0:T(8,128)(2,1)S(1)} fusion(bf16[1,768,4096]{2,1,0:T(8,128)(2,1)} %param.11, f32[384,768]{1,0:T(8,128)S(1)} %copy-done.19, bf16[384,1024]{1,0:T(8,128)(2,1)S(1)} %get-tuple-element.53, bf16[384,1024]{1,0:T(8,128)(2,1)S(1)} %get-tuple-element.51, bf16[384,1024]{1,0:T(8,128)(2,1)S(1)} %get-tuple-element.52, ...), kind=kOutput, calls=%fused_computation.36 | convolution fusion | flops 2434105344 | bytes 11206656 | tf_op jit(solution)/shard_map/sd,hd->sh/dot_general | solution.py:147
  122.3 2.6 %fusion.11 = f32[384,4096]{1,0:T(8,128)S(1)} fusion(bf16[384,768]{1,0:T(8,128)(2,1)S(1)} %fusion.24, bf16[1,4096,768]{2,1,0:T(8,128)(2,1)S(1)} %bitcast.86), kind=kOutput, calls=%fused_computation.9 | convolution fusion | flops 2419064832 | bytes 13172736 | tf_op jit(solution)/shard_map/sh,dh->sd/dot_general | solution.py:152
  124.9 1.1 fusion.60
  126.1 1.8 select_convert_fusion
  127.9 0.3 copy-done.2
  128.2 0.6 copy-done.4
  128.8 0.5 copy-done.6
  129.2 0.5 collective-permute-start.6
  129.8 10.7 %fusion.33 = f32[768,4096]{1,0:T(8,128)} fusion(bf16[384,1024]{1,0:T(8,128)(2,1)} %copy-done.17, bf16[384,1024]{1,0:T(8,128)(2,1)} %copy-done.15, bf16[384,1024]{1,0:T(8,128)(2,1)} %copy-done.16, bf16[384,1024]{1,0:T(8,128)(2,1)} %copy-done.14, f32[384,768]{1,0:T(8,128)} %copy-done.18), kind=kOutput, calls=%fused_computation.52 | convolution fusion | flops 2431156224 | bytes 16908288 | tf_op jit(solution)/shard_map/sh,sd->hd/dot_general | solution.py:155
  140.5 2.3 %add_convert_fusion = bf16[384,2048]{1,0:T(8,128)(2,1)S(1)} fusion(bf16[384,2048]{1,0:T(8,128)(2,1)} %collective-permute-done.6, f32[384,1024]{1,0:T(8,128)S(1)} %copy-done.3, f32[384,1024]{1,0:T(8,128)S(1)} %copy-done.5, f32[384,1024]{1,0:T(8,128)S(1)} %copy-done.7, f32[384,1024]{1,0:T(8,128)S(1)} %copy-done.1, pred[]{:T(512)S(6)} %eq.116), kind=kLoop, calls=%fused_computation.18 | loop fusion | flops 4718592 | bytes 9437185 | tf_op jit(solution)/shard_map/convert_element_type | solution.py:136
  142.8 1.3 broadcast_select_fusion.5
  144.1 5.0 %all-to-all-done.3 = bf16[8,48,2048]{2,1,0:T(8,128)(2,1)} async-done(((bf16[8,48,2048]{2,1,0:T(8,128)(2,1)}), bf16[8,48,2048]{2,1,0:T(8,128)(2,1)}, u32[]{:S(2)}, u32[]{:S(2)}) %all-to-all-start.3) | async-done | bytes 1572896 | tf_op jit(solution)/shard_map/all_to_all | solution.py:86
  149.1 4.2 %all-to-all-start.5 = ((bf16[8,48,1024]{2,1,0:T(8,128)(2,1)}), bf16[8,48,1024]{2,1,0:T(8,128)(2,1)}, u32[]{:S(2)}, u32[]{:S(2)}) async-start(bf16[8,48,1024]{2,1,0:T(8,128)(2,1)} %bitcast.77), calls=%async_computation.5 | async-start | bytes 1572864 | tf_op jit(solution)/shard_map/all_to_all | solution.py:86
  153.3 2.0 %convolution_multiply_fusion.1 = f32[192,2048]{1,0:T(8,128)S(1)} fusion(bf16[384,2048]{1,0:T(8,128)(2,1)} %bitcast.12, f32[192]{0:T(256)S(1)} %bitcast.83, s32[192]{0:T(256)S(1)} %get-tuple-element.32, pred[192]{0:T(512)(128)(4,1)S(1)} %get-tuple-element.34), kind=kOutput, calls=%fused_computation.25 | convolution fusion | flops 302530560 | bytes 3147456 | tf_op jit(solution)/shard_map/dot_general | solution.py:169
  155.4 2.0 %fusion.20 = f32[192,2048]{1,0:T(8,128)S(1)} fusion(f32[192,2048]{1,0:T(8,128)S(1)} %convolution_multiply_fusion.1, bf16[384,2048]{1,0:T(8,128)(2,1)} %bitcast.12, f32[192]{0:T(256)S(1)} %bitcast.81, s32[192]{0:T(256)S(1)} %get-tuple-element.33, pred[192]{0:T(512)(128)(4,1)S(1)} %get-tuple-element.35), kind=kOutput, calls=%fused_computation.24 | convolution fusion | flops 302923776 | bytes 4720320 | tf_op jit(solution)/shard_map/dot_general | solution.py:169
  157.4 1.1 copy-done.8
  158.6 1.0 slice_select_fusion
  159.6 1.5 collective-permute-start.4
  161.1 12.6 %all-to-all-done.5 = bf16[8,48,1024]{2,1,0:T(8,128)(2,1)} async-done(((bf16[8,48,1024]{2,1,0:T(8,128)(2,1)}), bf16[8,48,1024]{2,1,0:T(8,128)(2,1)}, u32[]{:S(2)}, u32[]{:S(2)}) %all-to-all-start.5) | async-done | bytes 786464 | tf_op jit(solution)/shard_map/all_to_all | solution.py:86
  173.7 4.4 %all-to-all-start.4 = ((bf16[8,48,1024]{2,1,0:T(8,128)(2,1)}), bf16[8,48,1024]{2,1,0:T(8,128)(2,1)}, u32[]{:S(2)}, u32[]{:S(2)}) async-start(bf16[8,48,1024]{2,1,0:T(8,128)(2,1)} %bitcast.76), calls=%async_computation.4 | async-start | bytes 1572864 | tf_op jit(solution)/shard_map/all_to_all | solution.py:86
  178.1 2.6 %fusion.55 = f32[192,1024]{1,0:T(8,128)} fusion(bf16[384,1024]{1,0:T(8,128)(2,1)} %bitcast.16, s32[192]{0:T(256)S(1)} %get-tuple-element.33, s32[192]{0:T(256)S(1)} %get-tuple-element.32, pred[192]{0:T(512)(128)(4,1)S(1)} %get-tuple-element.35, pred[192]{0:T(512)(128)(4,1)S(1)} %get-tuple-element.34), kind=kOutput, calls=%fused_computation.93 | convolution fusion | flops 151363584 | bytes 1574784 | tf_op jit(solution)/shard_map/dot_general | solution.py:159
  180.7 1.5 collective-permute-start.7
  182.2 2.0 %add_convert_fusion.2 = bf16[192,1024]{1,0:T(8,128)(2,1)} fusion(f32[192,1024]{1,0:T(8,128)} %collective-permute-done.4, f32[192,2048]{1,0:T(8,128)S(1)} %copy-done.9, pred[]{:T(512)S(6)} %eq.101), kind=kLoop, calls=%fused_computation.46 | loop fusion | flops 589824 | bytes 2752513 | tf_op jit(solution)/shard_map/convert_element_type | solution.py:142
  184.3 6.6 %fusion.67 = f32[4096,768]{1,0:T(8,128)} fusion(bf16[384,4096]{1,0:T(8,128)(2,1)S(1)} %pad_maximum_fusion, bf16[384,768]{1,0:T(8,128)(2,1)S(1)} %copy-done.21), kind=kOutput, calls=%fused_computation.101 | convolution fusion | flops 2415919104 | bytes 16318464 | tf_op jit(solution)/shard_map/sd,sh->dh/dot_general | solution.py:163
  190.9 7.1 %all-to-all-done.4 = bf16[8,48,1024]{2,1,0:T(8,128)(2,1)} async-done(((bf16[8,48,1024]{2,1,0:T(8,128)(2,1)}), bf16[8,48,1024]{2,1,0:T(8,128)(2,1)}, u32[]{:S(2)}, u32[]{:S(2)}) %all-to-all-start.4) | async-done | bytes 786464 | tf_op jit(solution)/shard_map/all_to_all | solution.py:86
  198.0 1.6 collective-permute-done.7
  199.5 2.6 %fusion.27 = bf16[192,1024]{1,0:T(8,128)(2,1)} fusion(f32[192,1024]{1,0:T(8,128)} %collective-permute-done.7, bf16[384,1024]{1,0:T(8,128)(2,1)} %bitcast.14, s32[192]{0:T(256)S(1)} %get-tuple-element.33, s32[192]{0:T(256)S(1)} %get-tuple-element.32, pred[192]{0:T(512)(128)(4,1)S(1)} %get-tuple-element.35, pred[192]{0:T(512)(128)(4,1)S(1)} %get-tuple-element.34), kind=kOutput, calls=%fused_computation.38 | convolution fusion | flops 151756800 | bytes 1968000 | tf_op jit(solution)/shard_map/dot_general | solution.py:165
  (68 shorter events, 2.4 us)
Async XLA Ops:
  4.2 10.0 %copy-start.22 = (bf16[192,1024]{1,0:T(8,128)(2,1)S(1)}, bf16[192,1024]{1,0:T(8,128)(2,1)}, u32[]{:S(2)}) copy-start(bf16[192,1024]{1,0:T(8,128)(2,1)} %param.7) | copy-start | bytes 1179652
  4.2 11.6 %copy-start.23 = (bf16[192,1024]{1,0:T(8,128)(2,1)S(1)}, bf16[192,1024]{1,0:T(8,128)(2,1)}, u32[]{:S(2)}) copy-start(bf16[192,1024]{1,0:T(8,128)(2,1)} %param.6) | copy-start | bytes 1179652
  7.0 27.5 %all-to-all-start = ((bf16[8,48,1024]{2,1,0:T(8,128)(2,1)}), bf16[8,48,1024]{2,1,0:T(8,128)(2,1)S(1)}, u32[]{:S(2)}, u32[]{:S(2)}) async-start(bf16[8,48,1024]{2,1,0:T(8,128)(2,1)} %bitcast.3), calls=%async_computation | async-start | bytes 1572864 | tf_op jit(solution)/shard_map/all_to_all | solution.py:86
  14.3 12.1 %collective-permute-start = (bf16[192,1024]{1,0:T(8,128)(2,1)S(1)}, bf16[192,1024]{1,0:T(8,128)(2,1)S(1)}, u32[]{:S(2)}, u32[]{:S(2)}) collective-permute-start(bf16[192,1024]{1,0:T(8,128)(2,1)S(1)} %copy-done.22), channel_id=1, source_target_pairs={{0,2},{1,3},{2,0},{3,1},{4,6},{5,7},{6,4},{7,5},{8,10},{9,11},{10,... | collective-permute-start | bytes 1179656 | tf_op jit(solution)/shard_map/ppermute | solution.py:49
  15.8 17.5 %collective-permute-start.1 = (bf16[192,1024]{1,0:T(8,128)(2,1)S(1)}, bf16[192,1024]{1,0:T(8,128)(2,1)S(1)}, u32[]{:S(2)}, u32[]{:S(2)}) collective-permute-start(bf16[192,1024]{1,0:T(8,128)(2,1)S(1)} %copy-done.23), channel_id=1, source_target_pairs={{0,2},{1,3},{2,0},{3,1},{4,6},{5,7},{6,4},{7,5},{8,10},{9,11},{10,... | collective-permute-start | bytes 1179656 | tf_op jit(solution)/shard_map/ppermute | solution.py:91
  58.2 0.7 copy-start.24
  58.4 3.8 %collective-permute-start.2 = (bf16[384,2048]{1,0:T(8,128)(2,1)S(1)}, bf16[384,2048]{1,0:T(8,128)(2,1)}, u32[]{:S(2)}, u32[]{:S(2)}) collective-permute-start(bf16[384,2048]{1,0:T(8,128)(2,1)S(1)} %pad_maximum_fusion.6), channel_id=1, source_target_pairs={{0,1},{1,0},{2,3},{3,2},{4,5},{5,4},{6,7},{7,6},{8,9},{9,8},{10,11... | collective-permute-start | bytes 4718600 | tf_op jit(solution)/shard_map/ppermute | solution.py:62
  65.0 41.8 %all-to-all-start.2 = ((bf16[8,48,2048]{2,1,0:T(8,128)(2,1)}), bf16[8,48,2048]{2,1,0:T(8,128)(2,1)}, u32[]{:S(2)}, u32[]{:S(2)}) async-start(bf16[8,48,2048]{2,1,0:T(8,128)(2,1)} %bitcast.79), calls=%async_computation.2 | async-start | bytes 3145728 | tf_op jit(solution)/shard_map/all_to_all | solution.py:86
  74.7 1.0 copy-start.18
  81.8 1.9 copy-start.10
  81.8 2.1 %copy-start.11 = (f32[384,1024]{1,0:T(8,128)}, f32[384,1024]{1,0:T(8,128)S(1)}, u32[]{:S(2)}) copy-start(f32[384,1024]{1,0:T(8,128)S(1)} %get-tuple-element.41) | copy-start | bytes 4718596
  81.8 2.6 %copy-start.12 = (f32[384,1024]{1,0:T(8,128)}, f32[384,1024]{1,0:T(8,128)S(1)}, u32[]{:S(2)}) copy-start(f32[384,1024]{1,0:T(8,128)S(1)} %get-tuple-element.42) | copy-start | bytes 4718596
  81.9 3.2 %copy-start.13 = (f32[384,1024]{1,0:T(8,128)}, f32[384,1024]{1,0:T(8,128)S(1)}, u32[]{:S(2)}) copy-start(f32[384,1024]{1,0:T(8,128)S(1)} %get-tuple-element.43) | copy-start | bytes 4718596
  85.1 3.8 %collective-permute-start.3 = (bf16[384,2048]{1,0:T(8,128)(2,1)}, bf16[384,2048]{1,0:T(8,128)(2,1)}, u32[]{:S(2)}, u32[]{:S(2)}) collective-permute-start(bf16[384,2048]{1,0:T(8,128)(2,1)} %select_convert_fusion.1), channel_id=1, source_target_pairs={{0,1},{1,0},{2,3},{3,2},{4,5},{5,4},{6,7},{7,6},{8,9},{9,8},{10,11... | collective-permute-start | bytes 4718600 | tf_op jit(solution)/shard_map/ppermute | solution.py:134
  106.8 4.5 %collective-permute-start.5 = (bf16[384,2048]{1,0:T(8,128)(2,1)}, bf16[384,2048]{1,0:T(8,128)(2,1)}, u32[]{:S(2)}, u32[]{:S(2)}) collective-permute-start(bf16[384,2048]{1,0:T(8,128)(2,1)} %bitcast.10), channel_id=1, source_target_pairs={{0,1},{1,0},{2,3},{3,2},{4,5},{5,4},{6,7},{7,6},{8,9},{9,8},{10,11... | collective-permute-start | bytes 4718600 | tf_op jit(solution)/shard_map/ppermute | solution.py:62
  106.8 42.3 %all-to-all-start.3 = ((bf16[8,48,2048]{2,1,0:T(8,128)(2,1)}), bf16[8,48,2048]{2,1,0:T(8,128)(2,1)}, u32[]{:S(2)}, u32[]{:S(2)}) async-start(bf16[8,48,2048]{2,1,0:T(8,128)(2,1)} %bitcast.75), calls=%async_computation.3 | async-start | bytes 3145728 | tf_op jit(solution)/shard_map/all_to_all | solution.py:86
  113.6 0.9 copy-start.14
  113.6 1.1 copy-start.15
  113.6 2.2 %copy-start.19 = (f32[384,768]{1,0:T(8,128)S(1)}, f32[384,768]{1,0:T(8,128)}, u32[]{:S(2)}) copy-start(f32[384,768]{1,0:T(8,128)} %copy-done.18) | copy-start | bytes 3538948
  113.6 8.6 %slice-start = ((s8[6291456]{0:T(1024)(128)(4,1)}), s8[4194304]{0:T(1024)(128)(4,1)S(1)}, s32[]{:S(2)}) async-start(s8[6291456]{0:T(1024)(128)(4,1)} %bitcast.85), calls=%async_computation.6 | async-start | bytes 8388608
  113.7 1.2 copy-start.16
  113.8 1.5 copy-start.17
  115.8 6.5 %slice-start.1 = ((s8[6291456]{0:T(1024)(128)(4,1)}), s8[2097152]{0:T(1024)(128)(4,1)S(1)}, s32[]{:S(2)}) async-start(s8[6291456]{0:T(1024)(128)(4,1)} %bitcast.85), calls=%async_computation.7 | async-start | bytes 4194304
  122.3 2.7 %copy-start.20 = (bf16[384,768]{1,0:T(8,128)(2,1)}, bf16[384,768]{1,0:T(8,128)(2,1)S(1)}, u32[]{:S(2)}) copy-start(bf16[384,768]{1,0:T(8,128)(2,1)S(1)} %fusion.24) | copy-start | bytes 1769476
  126.0 1.9 copy-start
  126.1 2.2 %copy-start.2 = (f32[384,1024]{1,0:T(8,128)}, f32[384,1024]{1,0:T(8,128)S(1)}, u32[]{:S(2)}) copy-start(f32[384,1024]{1,0:T(8,128)S(1)} %get-tuple-element.37) | copy-start | bytes 4718596
  126.1 2.7 %copy-start.4 = (f32[384,1024]{1,0:T(8,128)}, f32[384,1024]{1,0:T(8,128)S(1)}, u32[]{:S(2)}) copy-start(f32[384,1024]{1,0:T(8,128)S(1)} %get-tuple-element.38) | copy-start | bytes 4718596
  126.1 3.2 %copy-start.6 = (f32[384,1024]{1,0:T(8,128)}, f32[384,1024]{1,0:T(8,128)S(1)}, u32[]{:S(2)}) copy-start(f32[384,1024]{1,0:T(8,128)S(1)} %get-tuple-element.39) | copy-start | bytes 4718596
  129.2 11.2 %collective-permute-start.6 = (bf16[384,2048]{1,0:T(8,128)(2,1)}, bf16[384,2048]{1,0:T(8,128)(2,1)}, u32[]{:S(2)}, u32[]{:S(2)}) collective-permute-start(bf16[384,2048]{1,0:T(8,128)(2,1)} %select_convert_fusion), channel_id=1, source_target_pairs={{0,1},{1,0},{2,3},{3,2},{4,5},{5,4},{6,7},{7,6},{8,9},{9,8},{10,11... | collective-permute-start | bytes 4718600 | tf_op jit(solution)/shard_map/ppermute | solution.py:134
  129.7 10.7 %copy-start.1 = (f32[384,1024]{1,0:T(8,128)S(1)}, f32[384,1024]{1,0:T(8,128)}, u32[]{:S(2)}) copy-start(f32[384,1024]{1,0:T(8,128)} %copy-done) | copy-start | bytes 4718596
  129.7 10.7 %copy-start.3 = (f32[384,1024]{1,0:T(8,128)S(1)}, f32[384,1024]{1,0:T(8,128)}, u32[]{:S(2)}) copy-start(f32[384,1024]{1,0:T(8,128)} %copy-done.2) | copy-start | bytes 4718596
  129.7 10.7 %copy-start.5 = (f32[384,1024]{1,0:T(8,128)S(1)}, f32[384,1024]{1,0:T(8,128)}, u32[]{:S(2)}) copy-start(f32[384,1024]{1,0:T(8,128)} %copy-done.4) | copy-start | bytes 4718596
  129.8 10.7 %copy-start.7 = (f32[384,1024]{1,0:T(8,128)S(1)}, f32[384,1024]{1,0:T(8,128)}, u32[]{:S(2)}) copy-start(f32[384,1024]{1,0:T(8,128)} %copy-done.6) | copy-start | bytes 4718596
  149.1 24.6 %all-to-all-start.5 = ((bf16[8,48,1024]{2,1,0:T(8,128)(2,1)}), bf16[8,48,1024]{2,1,0:T(8,128)(2,1)}, u32[]{:S(2)}, u32[]{:S(2)}) async-start(bf16[8,48,1024]{2,1,0:T(8,128)(2,1)} %bitcast.77), calls=%async_computation.5 | async-start | bytes 1572864 | tf_op jit(solution)/shard_map/all_to_all | solution.py:86
  157.4 1.1 copy-start.8
  159.6 22.7 %collective-permute-start.4 = (f32[192,1024]{1,0:T(8,128)}, f32[192,1024]{1,0:T(8,128)}, u32[]{:S(2)}, u32[]{:S(2)}) collective-permute-start(f32[192,1024]{1,0:T(8,128)} %slice_select_fusion), channel_id=1, source_target_pairs={{0,2},{1,3},{2,0},{3,1},{4,6},{5,7},{6,4},{7,5},{8,10},{9,11},{10,... | collective-permute-start | bytes 2359304 | tf_op jit(solution)/shard_map/ppermute | solution.py:142
  173.7 24.3 %all-to-all-start.4 = ((bf16[8,48,1024]{2,1,0:T(8,128)(2,1)}), bf16[8,48,1024]{2,1,0:T(8,128)(2,1)}, u32[]{:S(2)}, u32[]{:S(2)}) async-start(bf16[8,48,1024]{2,1,0:T(8,128)(2,1)} %bitcast.76), calls=%async_computation.4 | async-start | bytes 1572864 | tf_op jit(solution)/shard_map/all_to_all | solution.py:86
  178.1 4.1 %copy-start.9 = (f32[192,2048]{1,0:T(8,128)S(1)}, f32[192,2048]{1,0:T(8,128)}, u32[]{:S(2)}) copy-start(f32[192,2048]{1,0:T(8,128)} %copy-done.8) | copy-start | bytes 4718596
  180.7 3.5 %copy-start.21 = (bf16[384,768]{1,0:T(8,128)(2,1)S(1)}, bf16[384,768]{1,0:T(8,128)(2,1)}, u32[]{:S(2)}) copy-start(bf16[384,768]{1,0:T(8,128)(2,1)} %copy-done.20) | copy-start | bytes 1769476
  180.7 18.8 %collective-permute-start.7 = (f32[192,1024]{1,0:T(8,128)}, f32[192,1024]{1,0:T(8,128)}, u32[]{:S(2)}, u32[]{:S(2)}) collective-permute-start(f32[192,1024]{1,0:T(8,128)} %fusion.55), channel_id=1, source_target_pairs={{0,2},{1,3},{2,0},{3,1},{4,6},{5,7},{6,4},{7,5},{8,10},{9,11},{10,... | collective-permute-start | bytes 2359304 | tf_op jit(solution)/shard_map/ppermute | solution.py:160

commit v6 on v5

--- a/solution.py
+++ b/solution.py
@@ -93,13 +93,18 @@
     sub_dy = core_subset(grad_out)
     sub_dy, other_buf = lax.optimization_barrier((sub_dy, other_buf))
     got_other = send(other_buf)
-    first = half == 0
-    got_x = jnp.concatenate(
-        [jnp.where(first, got_own, got_other), jnp.where(first, got_other, got_own)], axis=1
-    )
     dy_buf = jnp.dot(dispatch_mat, sub_dy, preferred_element_type=f32)
     d_buf = (gate_slot[:, None] * dy_buf).astype(bf16)
-    x_rows = to_experts(got_x)
+    own_all = [got_own] + [lax.ppermute(got_own, "exp", core_shift(s)) for s in range(1, cores)]
+    other_all = [got_other] + [lax.ppermute(got_other, "exp", core_shift(s)) for s in range(1, cores)]
+    x_pieces = []
+    for p in range(EXP_DEV):
+        for q in range(cores):
+            shift = (core - q) % cores
+            x_pieces.append(
+                jnp.where(p == half, pick_by(shift, own_all), pick_by(shift, other_all))
+            )
+    x_rows = jnp.concatenate(x_pieces, axis=1)
     d_buf, x_rows = lax.optimization_barrier((d_buf, x_rows))
     got_d = send(d_buf)
 

time: 203 us -> 201 us (level)
  blocking collectives: 23.7 us -> 0 us
  waiting for transfers between devices: 59.2 us -> 78.6 us
  starting transfers between devices: 30.4 us -> 36.2 us
    all_to_all x1 -> x0, blocking collectives: 23.7 us -> none  [send(): lax.all_to_all(buf.reshape(sections, capacity, width), 'attn', split_axis...]
    all_to_all x5 -> x6, waiting for transfers between devices: 38 us -> 56.4 us  [send(): lax.all_to_all(buf.reshape(sections, capacity, width), 'attn', split_axis...]
    all_to_all x5 -> x6, starting transfers between devices: 24.7 us -> 30.4 us  [send(): lax.all_to_all(buf.reshape(sections, capacity, width), 'attn', split_axis...]
    select_n x4 -> x3, other arithmetic: 6.56 us -> 4.38 us  [pick_by(): picked = jnp.where(index == i, value, picked)]
  transfers between devices with their start and end apart: 13 -> 15, of which waited for: 9 -> 10; matrix products, arithmetic and copies ran while one was open for 34% -> 34% of each run, Pallas kernels for 0% -> 0%
where the time goes in v6:
time: 201 us
  waiting for transfers between devices  78.6 us (39%)
  matrix products  51.7 us (26%)
  starting transfers between devices  36.2 us (18%)
  other arithmetic  21.6 us (11%)
  local copies, waits for them, and re-layouts  11.3 us (6%)
    all_to_all x6, waiting for transfers between devices, send(): lax.all_to_all(buf.reshape(sections, capacity, width), 'attn', split_axis...  56.4 us
    all_to_all x6, starting transfers between devices, send(): lax.all_to_all(buf.reshape(sections, capacity, width), 'attn', split_axis...  30.4 us
    dot_general x1, matrix products, on_device(): jnp.einsum('sh,sd->hd', activation, d_rows, preferred_element_type=f32)  10.7 us
    ppermute x1, waiting for transfers between devices, core_subset(): other = lax.ppermute(local, 'exp', half_swap)  10 us
    unnamed x55, local copies, waits for them, and re-layouts  7.63 us
    convert_element_type x2, other arithmetic, group_sum(): return lax.optimization_barrier((summed.astype(bf16), hold))  7.63 us
    ppermute x1, waiting for transfers between devices, on_device(): x_other = lax.ppermute(patches, 'exp', half_swap)  6.82 us
    dot_general x1, matrix products, on_device(): jnp.einsum('sd,sh->dh', x_late, pre_late, preferred_element_type=f32)  6.61 us
  transfers between devices with their start and end apart: 15, of which 10 were waited for; matrix products, arithmetic and copies ran while one was open for 34% of the time, Pallas kernels for 0%

profile of v6, /device:TPU:0, one launch (start us, length us, event | category | flops | bytes accessed | tf_op | source)
XLA Modules:
  0.0 200.6 jit_solution(14633678441705815296)
XLA Ops:
  0.6 0.7 broadcast_compare_fusion
  1.3 0.8 copy.30
  2.6 0.9 reduce-window.6
  3.5 0.2 slice_reduce_fusion.4
  4.5 2.4 %convolution_convert_fusion = bf16[384,1024]{1,0:T(8,128)(2,1)} fusion(bf16[192,1024]{1,0:T(8,128)(2,1)} %param.6, s32[192]{0:T(256)S(1)} %get-tuple-element.33, s32[192]{0:T(256)S(1)} %get-tuple-element.32, pred[192]{0:T(512)(128)(4,1)S(1)} %get-tuple-element.35, pred[192]{0:T(512)(128)(4,1)S(1)} %get-tuple-element.34), kind=kOutput, calls=%fused_computation.31 | convolution fusion | flops 151756800 | bytes 1181568 | tf_op jit(solution)/shard_map/dot_general | solution.py:90
  7.0 7.3 %all-to-all-start = ((bf16[8,48,1024]{2,1,0:T(8,128)(2,1)}), bf16[8,48,1024]{2,1,0:T(8,128)(2,1)S(1)}, u32[]{:S(2)}, u32[]{:S(2)}) async-start(bf16[8,48,1024]{2,1,0:T(8,128)(2,1)} %bitcast.3), calls=%async_computation | async-start | bytes 1572864 | tf_op jit(solution)/shard_map/all_to_all | solution.py:86
  14.3 1.6 collective-permute-start
  15.8 0.5 collective-permute-start.1
  16.3 10.0 %collective-permute-done = bf16[192,1024]{1,0:T(8,128)(2,1)S(1)} collective-permute-done((bf16[192,1024]{1,0:T(8,128)(2,1)S(1)}, bf16[192,1024]{1,0:T(8,128)(2,1)S(1)}, u32[]{:S(2)}, u32[]{:S(2)}) %collective-permute-start) | collective-permute-done | bytes 393248 | tf_op jit(solution)/shard_map/ppermute | solution.py:49
  26.5 6.8 %collective-permute-done.1 = bf16[192,1024]{1,0:T(8,128)(2,1)S(1)} collective-permute-done((bf16[192,1024]{1,0:T(8,128)(2,1)S(1)}, bf16[192,1024]{1,0:T(8,128)(2,1)S(1)}, u32[]{:S(2)}, u32[]{:S(2)}) %collective-permute-start.1) | collective-permute-done | bytes 393248 | tf_op jit(solution)/shard_map/ppermute | solution.py:91
  33.3 1.4 convolution_convert_fusion.1
  34.8 5.7 %all-to-all-start.1 = ((bf16[8,48,1024]{2,1,0:T(8,128)(2,1)}), bf16[8,48,1024]{2,1,0:T(8,128)(2,1)S(1)}, u32[]{:S(2)}, u32[]{:S(2)}) async-start(bf16[8,48,1024]{2,1,0:T(8,128)(2,1)} %bitcast.5), calls=%async_computation.1 | async-start | bytes 1572864 | tf_op jit(solution)/shard_map/all_to_all | solution.py:86
  40.4 18.8 %all-to-all-done.1 = bf16[8,48,1024]{2,1,0:T(8,128)(2,1)S(1)} async-done(((bf16[8,48,1024]{2,1,0:T(8,128)(2,1)}), bf16[8,48,1024]{2,1,0:T(8,128)(2,1)S(1)}, u32[]{:S(2)}, u32[]{:S(2)}) %all-to-all-start.1) | async-done | bytes 786464 | tf_op jit(solution)/shard_map/all_to_all | solution.py:86
  59.2 0.2 select_reduce_fusion
  59.4 1.9 multiply_convert_fusion
  61.4 0.2 collective-permute-done.3
  61.6 1.4 broadcast_select_fusion.11
  63.0 0.3 pad_maximum_fusion
  63.3 4.3 %all-to-all-start.2 = ((bf16[8,48,2048]{2,1,0:T(8,128)(2,1)}), bf16[8,48,2048]{2,1,0:T(8,128)(2,1)}, u32[]{:S(2)}, u32[]{:S(2)}) async-start(bf16[8,48,2048]{2,1,0:T(8,128)(2,1)} %bitcast.84), calls=%async_computation.2 | async-start | bytes 3145728 | tf_op jit(solution)/shard_map/all_to_all | solution.py:86
  67.6 5.4 %fusion.6 = f32[384,768]{1,0:T(8,128)S(1)} fusion(bf16[384,4096]{1,0:T(8,128)(2,1)S(1)} %pad_maximum_fusion, bf16[1,4096,768]{2,1,0:T(8,128)(2,1)} %param.10), kind=kOutput, calls=%fused_computation.6 | convolution fusion | flops 2415919104 | bytes 10616832 | tf_op jit(solution)/shard_map/dot_general | solution.py:117
  73.0 1.0 copy-done.18
  74.0 4.9 %fusion.17 = f32[384,4096]{1,0:T(8,128)S(1)} fusion(bf16[1,768,4096]{2,1,0:T(8,128)(2,1)} %param.11, f32[384,768]{1,0:T(8,128)S(1)} %fusion.6), kind=kOutput, calls=%fused_computation.11 | convolution fusion | flops 2421719040 | bytes 13762560 | tf_op jit(solution)/shard_map/dot_general | solution.py:124
  78.9 1.1 fusion.61
  80.1 1.9 select_convert_fusion.1
  82.2 0.5 copy-done.12
  82.7 0.6 copy-done.13
  83.3 0.3 collective-permute-start.4
  83.6 3.5 %collective-permute-done.4 = bf16[384,2048]{1,0:T(8,128)(2,1)} collective-permute-done((bf16[384,2048]{1,0:T(8,128)(2,1)}, bf16[384,2048]{1,0:T(8,128)(2,1)}, u32[]{:S(2)}, u32[]{:S(2)}) %collective-permute-start.4) | collective-permute-done | bytes 1572896 | tf_op jit(solution)/shard_map/ppermute | solution.py:139
  87.1 5.3 %add_convert_fusion.1 = bf16[384,2048]{1,0:T(8,128)(2,1)} fusion(bf16[384,2048]{1,0:T(8,128)(2,1)} %collective-permute-done.4, f32[384,1024]{1,0:T(8,128)} %copy-done.11, f32[384,1024]{1,0:T(8,128)} %copy-done.12, f32[384,1024]{1,0:T(8,128)} %copy-done.13, f32[384,1024]{1,0:T(8,128)} %copy-done.10, pred[]{:T(512)S(6)} %eq.127), kind=kLoop, calls=%fused_computation.20 | loop fusion | flops 4718592 | bytes 9437185 | tf_op jit(solution)/shard_map/convert_element_type | solution.py:141
  92.4 12.9 %all-to-all-done.2 = bf16[8,48,2048]{2,1,0:T(8,128)(2,1)} async-done(((bf16[8,48,2048]{2,1,0:T(8,128)(2,1)}), bf16[8,48,2048]{2,1,0:T(8,128)(2,1)}, u32[]{:S(2)}, u32[]{:S(2)}) %all-to-all-start.2) | async-done | bytes 1572896 | tf_op jit(solution)/shard_map/all_to_all | solution.py:86
  105.3 4.5 %all-to-all-start.3 = ((bf16[8,48,2048]{2,1,0:T(8,128)(2,1)}), bf16[8,48,2048]{2,1,0:T(8,128)(2,1)}, u32[]{:S(2)}, u32[]{:S(2)}) async-start(bf16[8,48,2048]{2,1,0:T(8,128)(2,1)} %bitcast.79), calls=%async_computation.3 | async-start | bytes 3145728 | tf_op jit(solution)/shard_map/all_to_all | solution.py:86
  109.8 2.1 %broadcast_select_fusion.1 = (bf16[384,2048]{1,0:T(8,128)(2,1)S(1)}, bf16[384,2048]{1,0:T(8,128)(2,1)S(1)}) fusion(bf16[384,2048]{1,0:T(8,128)(2,1)} %collective-permute-done.6, bf16[384,2048]{1,0:T(8,128)(2,1)} %bitcast.10, pred[]{:T(512)S(6)} %eq.133, pred[]{:T(512)S(6)} %eq.134), kind=kLoop, calls=%fused_computation.29 | loop fusion | flops 1572864 | bytes 6291458 | tf_op jit(solution)/shard_map/jit(_where)/select_n | solution.py:58
  112.2 0.7 copy-done.14
  112.9 0.2 copy-done.15
  113.2 0.2 copy-done.16
  113.4 0.3 copy-done.17
  113.7 0.5 copy-done.19
  114.2 6.5 %fusion.24 = bf16[384,768]{1,0:T(8,128)(2,1)S(1)} fusion(bf16[1,768,4096]{2,1,0:T(8,128)(2,1)} %param.11, f32[384,768]{1,0:T(8,128)S(1)} %copy-done.19, bf16[384,1024]{1,0:T(8,128)(2,1)S(1)} %get-tuple-element.55, bf16[384,1024]{1,0:T(8,128)(2,1)S(1)} %get-tuple-element.53, bf16[384,1024]{1,0:T(8,128)(2,1)S(1)} %get-tuple-element.54, ...), kind=kOutput, calls=%fused_computation.33 | convolution fusion | flops 2434105344 | bytes 11206656 | tf_op jit(solution)/shard_map/sd,hd->sh/dot_general | solution.py:152
  120.7 2.6 %fusion.11 = f32[384,4096]{1,0:T(8,128)S(1)} fusion(bf16[384,768]{1,0:T(8,128)(2,1)S(1)} %fusion.24, bf16[1,4096,768]{2,1,0:T(8,128)(2,1)S(1)} %bitcast.91), kind=kOutput, calls=%fused_computation.9 | convolution fusion | flops 2419064832 | bytes 13172736 | tf_op jit(solution)/shard_map/sh,dh->sd/dot_general | solution.py:157
  123.4 1.1 fusion.60
  124.6 1.9 select_convert_fusion
  126.4 0.3 copy-done.2
  126.7 0.5 copy-done.4
  127.2 0.5 copy-done.6
  127.7 0.5 collective-permute-start.7
  128.2 10.7 %fusion.33 = f32[768,4096]{1,0:T(8,128)} fusion(bf16[384,1024]{1,0:T(8,128)(2,1)} %copy-done.17, bf16[384,1024]{1,0:T(8,128)(2,1)} %copy-done.15, bf16[384,1024]{1,0:T(8,128)(2,1)} %copy-done.16, bf16[384,1024]{1,0:T(8,128)(2,1)} %copy-done.14, f32[384,768]{1,0:T(8,128)} %copy-done.18), kind=kOutput, calls=%fused_computation.55 | convolution fusion | flops 2431156224 | bytes 16908288 | tf_op jit(solution)/shard_map/sh,sd->hd/dot_general | solution.py:160
  139.0 2.3 %add_convert_fusion = bf16[384,2048]{1,0:T(8,128)(2,1)S(1)} fusion(bf16[384,2048]{1,0:T(8,128)(2,1)} %collective-permute-done.7, f32[384,1024]{1,0:T(8,128)S(1)} %copy-done.3, f32[384,1024]{1,0:T(8,128)S(1)} %copy-done.5, f32[384,1024]{1,0:T(8,128)S(1)} %copy-done.7, f32[384,1024]{1,0:T(8,128)S(1)} %copy-done.1, pred[]{:T(512)S(6)} %eq.127), kind=kLoop, calls=%fused_computation.18 | loop fusion | flops 4718592 | bytes 9437185 | tf_op jit(solution)/shard_map/convert_element_type | solution.py:141
  141.3 1.3 broadcast_select_fusion.3
  142.5 5.0 %all-to-all-done.3 = bf16[8,48,2048]{2,1,0:T(8,128)(2,1)} async-done(((bf16[8,48,2048]{2,1,0:T(8,128)(2,1)}), bf16[8,48,2048]{2,1,0:T(8,128)(2,1)}, u32[]{:S(2)}, u32[]{:S(2)}) %all-to-all-start.3) | async-done | bytes 1572896 | tf_op jit(solution)/shard_map/all_to_all | solution.py:86
  147.6 4.2 %all-to-all-start.5 = ((bf16[8,48,1024]{2,1,0:T(8,128)(2,1)}), bf16[8,48,1024]{2,1,0:T(8,128)(2,1)}, u32[]{:S(2)}, u32[]{:S(2)}) async-start(bf16[8,48,1024]{2,1,0:T(8,128)(2,1)} %bitcast.81), calls=%async_computation.5 | async-start | bytes 1572864 | tf_op jit(solution)/shard_map/all_to_all | solution.py:86
  151.8 2.0 %convolution_multiply_fusion.1 = f32[192,2048]{1,0:T(8,128)S(1)} fusion(bf16[384,2048]{1,0:T(8,128)(2,1)} %bitcast.12, f32[192]{0:T(256)S(1)} %bitcast.88, s32[192]{0:T(256)S(1)} %get-tuple-element.32, pred[192]{0:T(512)(128)(4,1)S(1)} %get-tuple-element.34), kind=kOutput, calls=%fused_computation.25 | convolution fusion | flops 302530560 | bytes 3147456 | tf_op jit(solution)/shard_map/dot_general | solution.py:174
  153.9 2.0 %fusion.20 = f32[192,2048]{1,0:T(8,128)S(1)} fusion(f32[192,2048]{1,0:T(8,128)S(1)} %convolution_multiply_fusion.1, bf16[384,2048]{1,0:T(8,128)(2,1)} %bitcast.12, f32[192]{0:T(256)S(1)} %bitcast.86, s32[192]{0:T(256)S(1)} %get-tuple-element.33, pred[192]{0:T(512)(128)(4,1)S(1)} %get-tuple-element.35), kind=kOutput, calls=%fused_computation.24 | convolution fusion | flops 302923776 | bytes 4720320 | tf_op jit(solution)/shard_map/dot_general | solution.py:174
  155.9 1.1 copy-done.8
  157.0 1.0 slice_select_fusion
  158.1 1.5 collective-permute-start.5
  159.6 12.6 %all-to-all-done.5 = bf16[8,48,1024]{2,1,0:T(8,128)(2,1)} async-done(((bf16[8,48,1024]{2,1,0:T(8,128)(2,1)}), bf16[8,48,1024]{2,1,0:T(8,128)(2,1)}, u32[]{:S(2)}, u32[]{:S(2)}) %all-to-all-start.5) | async-done | bytes 786464 | tf_op jit(solution)/shard_map/all_to_all | solution.py:86
  172.2 4.4 %all-to-all-start.4 = ((bf16[8,48,1024]{2,1,0:T(8,128)(2,1)}), bf16[8,48,1024]{2,1,0:T(8,128)(2,1)}, u32[]{:S(2)}, u32[]{:S(2)}) async-start(bf16[8,48,1024]{2,1,0:T(8,128)(2,1)} %bitcast.80), calls=%async_computation.4 | async-start | bytes 1572864 | tf_op jit(solution)/shard_map/all_to_all | solution.py:86
  176.6 2.6 %fusion.55 = f32[192,1024]{1,0:T(8,128)} fusion(bf16[384,1024]{1,0:T(8,128)(2,1)} %bitcast.16, s32[192]{0:T(256)S(1)} %get-tuple-element.33, s32[192]{0:T(256)S(1)} %get-tuple-element.32, pred[192]{0:T(512)(128)(4,1)S(1)} %get-tuple-element.35, pred[192]{0:T(512)(128)(4,1)S(1)} %get-tuple-element.34), kind=kOutput, calls=%fused_computation.96 | convolution fusion | flops 151363584 | bytes 1574784 | tf_op jit(solution)/shard_map/dot_general | solution.py:164
  179.2 1.5 collective-permute-start.8
  180.7 2.0 %add_convert_fusion.2 = bf16[192,1024]{1,0:T(8,128)(2,1)} fusion(f32[192,1024]{1,0:T(8,128)} %collective-permute-done.5, f32[192,2048]{1,0:T(8,128)S(1)} %copy-done.9, pred[]{:T(512)S(6)} %eq.112), kind=kLoop, calls=%fused_computation.43 | loop fusion | flops 589824 | bytes 2752513 | tf_op jit(solution)/shard_map/convert_element_type | solution.py:147
  182.8 6.6 %fusion.65 = f32[4096,768]{1,0:T(8,128)} fusion(bf16[384,4096]{1,0:T(8,128)(2,1)S(1)} %pad_maximum_fusion, bf16[384,768]{1,0:T(8,128)(2,1)S(1)} %copy-done.21), kind=kOutput, calls=%fused_computation.102 | convolution fusion | flops 2415919104 | bytes 16318464 | tf_op jit(solution)/shard_map/sd,sh->dh/dot_general | solution.py:168
  189.4 7.1 %all-to-all-done.4 = bf16[8,48,1024]{2,1,0:T(8,128)(2,1)} async-done(((bf16[8,48,1024]{2,1,0:T(8,128)(2,1)}), bf16[8,48,1024]{2,1,0:T(8,128)(2,1)}, u32[]{:S(2)}, u32[]{:S(2)}) %all-to-all-start.4) | async-done | bytes 786464 | tf_op jit(solution)/shard_map/all_to_all | solution.py:86
  196.5 1.6 collective-permute-done.8
  198.0 2.6 %fusion.27 = bf16[192,1024]{1,0:T(8,128)(2,1)} fusion(f32[192,1024]{1,0:T(8,128)} %collective-permute-done.8, bf16[384,1024]{1,0:T(8,128)(2,1)} %bitcast.14, s32[192]{0:T(256)S(1)} %get-tuple-element.33, s32[192]{0:T(256)S(1)} %get-tuple-element.32, pred[192]{0:T(512)(128)(4,1)S(1)} %get-tuple-element.35, pred[192]{0:T(512)(128)(4,1)S(1)} %get-tuple-element.34), kind=kOutput, calls=%fused_computation.35 | convolution fusion | flops 151756800 | bytes 1968000 | tf_op jit(solution)/shard_map/dot_general | solution.py:170
  (68 shorter events, 1.9 us)
Async XLA Ops:
  4.2 10.0 %copy-start.22 = (bf16[192,1024]{1,0:T(8,128)(2,1)S(1)}, bf16[192,1024]{1,0:T(8,128)(2,1)}, u32[]{:S(2)}) copy-start(bf16[192,1024]{1,0:T(8,128)(2,1)} %param.7) | copy-start | bytes 1179652
  4.2 11.6 %copy-start.23 = (bf16[192,1024]{1,0:T(8,128)(2,1)S(1)}, bf16[192,1024]{1,0:T(8,128)(2,1)}, u32[]{:S(2)}) copy-start(bf16[192,1024]{1,0:T(8,128)(2,1)} %param.6) | copy-start | bytes 1179652
  7.0 27.8 %all-to-all-start = ((bf16[8,48,1024]{2,1,0:T(8,128)(2,1)}), bf16[8,48,1024]{2,1,0:T(8,128)(2,1)S(1)}, u32[]{:S(2)}, u32[]{:S(2)}) async-start(bf16[8,48,1024]{2,1,0:T(8,128)(2,1)} %bitcast.3), calls=%async_computation | async-start | bytes 1572864 | tf_op jit(solution)/shard_map/all_to_all | solution.py:86
  14.3 12.1 %collective-permute-start = (bf16[192,1024]{1,0:T(8,128)(2,1)S(1)}, bf16[192,1024]{1,0:T(8,128)(2,1)S(1)}, u32[]{:S(2)}, u32[]{:S(2)}) collective-permute-start(bf16[192,1024]{1,0:T(8,128)(2,1)S(1)} %copy-done.22), channel_id=1, source_target_pairs={{0,2},{1,3},{2,0},{3,1},{4,6},{5,7},{6,4},{7,5},{8,10},{9,11},{10,... | collective-permute-start | bytes 1179656 | tf_op jit(solution)/shard_map/ppermute | solution.py:49
  15.8 17.5 %collective-permute-start.1 = (bf16[192,1024]{1,0:T(8,128)(2,1)S(1)}, bf16[192,1024]{1,0:T(8,128)(2,1)S(1)}, u32[]{:S(2)}, u32[]{:S(2)}) collective-permute-start(bf16[192,1024]{1,0:T(8,128)(2,1)S(1)} %copy-done.23), channel_id=1, source_target_pairs={{0,2},{1,3},{2,0},{3,1},{4,6},{5,7},{6,4},{7,5},{8,10},{9,11},{10,... | collective-permute-start | bytes 1179656 | tf_op jit(solution)/shard_map/ppermute | solution.py:91
  26.5 32.7 %copy-start.24 = (f32[192,2]{0,1:T(2,128)S(1)}, f32[192,2]{0,1:T(2,128)}, u32[]{:S(2)}) copy-start(f32[192,2]{0,1:T(2,128)} %param.9) | copy-start | bytes 4612
  34.8 24.4 %all-to-all-start.1 = ((bf16[8,48,1024]{2,1,0:T(8,128)(2,1)}), bf16[8,48,1024]{2,1,0:T(8,128)(2,1)S(1)}, u32[]{:S(2)}, u32[]{:S(2)}) async-start(bf16[8,48,1024]{2,1,0:T(8,128)(2,1)} %bitcast.5), calls=%async_computation.1 | async-start | bytes 1572864 | tf_op jit(solution)/shard_map/all_to_all | solution.py:86
  40.4 20.9 %collective-permute-start.2 = (bf16[384,1024]{1,0:T(8,128)(2,1)S(1)}, bf16[384,1024]{1,0:T(8,128)(2,1)S(1)}, u32[]{:S(2)}, u32[]{:S(2)}) collective-permute-start(bf16[384,1024]{1,0:T(8,128)(2,1)S(1)} %bitcast.82), channel_id=1, source_target_pairs={{0,1},{1,0},{2,3},{3,2},{4,5},{5,4},{6,7},{7,6},{8,9},{9,8},{10,11... | collective-permute-start | bytes 2359304 | tf_op jit(solution)/shard_map/ppermute | solution.py:98
  59.2 2.4 %collective-permute-start.3 = (bf16[384,1024]{1,0:T(8,128)(2,1)S(1)}, bf16[384,1024]{1,0:T(8,128)(2,1)}, u32[]{:S(2)}, u32[]{:S(2)}) collective-permute-start(bf16[384,1024]{1,0:T(8,128)(2,1)S(1)} %bitcast.83), channel_id=1, source_target_pairs={{0,1},{1,0},{2,3},{3,2},{4,5},{5,4},{6,7},{7,6},{8,9},{9,8},{10,11... | collective-permute-start | bytes 2359304 | tf_op jit(solution)/shard_map/ppermute | solution.py:99
  63.3 42.0 %all-to-all-start.2 = ((bf16[8,48,2048]{2,1,0:T(8,128)(2,1)}), bf16[8,48,2048]{2,1,0:T(8,128)(2,1)}, u32[]{:S(2)}, u32[]{:S(2)}) async-start(bf16[8,48,2048]{2,1,0:T(8,128)(2,1)} %bitcast.84), calls=%async_computation.2 | async-start | bytes 3145728 | tf_op jit(solution)/shard_map/all_to_all | solution.py:86
  73.0 1.0 copy-start.18
  80.0 1.9 copy-start.10
  80.1 2.1 %copy-start.11 = (f32[384,1024]{1,0:T(8,128)}, f32[384,1024]{1,0:T(8,128)S(1)}, u32[]{:S(2)}) copy-start(f32[384,1024]{1,0:T(8,128)S(1)} %get-tuple-element.41) | copy-start | bytes 4718596
  80.1 2.6 %copy-start.12 = (f32[384,1024]{1,0:T(8,128)}, f32[384,1024]{1,0:T(8,128)S(1)}, u32[]{:S(2)}) copy-start(f32[384,1024]{1,0:T(8,128)S(1)} %get-tuple-element.42) | copy-start | bytes 4718596
  80.1 3.2 %copy-start.13 = (f32[384,1024]{1,0:T(8,128)}, f32[384,1024]{1,0:T(8,128)S(1)}, u32[]{:S(2)}) copy-start(f32[384,1024]{1,0:T(8,128)S(1)} %get-tuple-element.43) | copy-start | bytes 4718596
  83.3 3.8 %collective-permute-start.4 = (bf16[384,2048]{1,0:T(8,128)(2,1)}, bf16[384,2048]{1,0:T(8,128)(2,1)}, u32[]{:S(2)}, u32[]{:S(2)}) collective-permute-start(bf16[384,2048]{1,0:T(8,128)(2,1)} %select_convert_fusion.1), channel_id=1, source_target_pairs={{0,1},{1,0},{2,3},{3,2},{4,5},{5,4},{6,7},{7,6},{8,9},{9,8},{10,11... | collective-permute-start | bytes 4718600 | tf_op jit(solution)/shard_map/ppermute | solution.py:139
  105.3 4.5 %collective-permute-start.6 = (bf16[384,2048]{1,0:T(8,128)(2,1)}, bf16[384,2048]{1,0:T(8,128)(2,1)}, u32[]{:S(2)}, u32[]{:S(2)}) collective-permute-start(bf16[384,2048]{1,0:T(8,128)(2,1)} %bitcast.10), channel_id=1, source_target_pairs={{0,1},{1,0},{2,3},{3,2},{4,5},{5,4},{6,7},{7,6},{8,9},{9,8},{10,11... | collective-permute-start | bytes 4718600 | tf_op jit(solution)/shard_map/ppermute | solution.py:62
  105.3 42.3 %all-to-all-start.3 = ((bf16[8,48,2048]{2,1,0:T(8,128)(2,1)}), bf16[8,48,2048]{2,1,0:T(8,128)(2,1)}, u32[]{:S(2)}, u32[]{:S(2)}) async-start(bf16[8,48,2048]{2,1,0:T(8,128)(2,1)} %bitcast.79), calls=%async_computation.3 | async-start | bytes 3145728 | tf_op jit(solution)/shard_map/all_to_all | solution.py:86
  112.0 0.9 copy-start.14
  112.1 1.1 copy-start.15
  112.1 2.2 %copy-start.19 = (f32[384,768]{1,0:T(8,128)S(1)}, f32[384,768]{1,0:T(8,128)}, u32[]{:S(2)}) copy-start(f32[384,768]{1,0:T(8,128)} %copy-done.18) | copy-start | bytes 3538948
  112.1 8.6 %slice-start = ((s8[6291456]{0:T(1024)(128)(4,1)}), s8[4194304]{0:T(1024)(128)(4,1)S(1)}, s32[]{:S(2)}) async-start(s8[6291456]{0:T(1024)(128)(4,1)} %bitcast.90), calls=%async_computation.6 | async-start | bytes 8388608
  112.2 1.2 copy-start.16
  112.2 1.5 copy-start.17
  114.2 6.5 %slice-start.1 = ((s8[6291456]{0:T(1024)(128)(4,1)}), s8[2097152]{0:T(1024)(128)(4,1)S(1)}, s32[]{:S(2)}) async-start(s8[6291456]{0:T(1024)(128)(4,1)} %bitcast.90), calls=%async_computation.7 | async-start | bytes 4194304
  120.7 2.7 %copy-start.20 = (bf16[384,768]{1,0:T(8,128)(2,1)}, bf16[384,768]{1,0:T(8,128)(2,1)S(1)}, u32[]{:S(2)}) copy-start(bf16[384,768]{1,0:T(8,128)(2,1)S(1)} %fusion.24) | copy-start | bytes 1769476
  124.5 1.9 copy-start
  124.5 2.2 %copy-start.2 = (f32[384,1024]{1,0:T(8,128)}, f32[384,1024]{1,0:T(8,128)S(1)}, u32[]{:S(2)}) copy-start(f32[384,1024]{1,0:T(8,128)S(1)} %get-tuple-element.37) | copy-start | bytes 4718596
  124.5 2.7 %copy-start.4 = (f32[384,1024]{1,0:T(8,128)}, f32[384,1024]{1,0:T(8,128)S(1)}, u32[]{:S(2)}) copy-start(f32[384,1024]{1,0:T(8,128)S(1)} %get-tuple-element.38) | copy-start | bytes 4718596
  124.6 3.1 %copy-start.6 = (f32[384,1024]{1,0:T(8,128)}, f32[384,1024]{1,0:T(8,128)S(1)}, u32[]{:S(2)}) copy-start(f32[384,1024]{1,0:T(8,128)S(1)} %get-tuple-element.39) | copy-start | bytes 4718596
  127.7 11.2 %collective-permute-start.7 = (bf16[384,2048]{1,0:T(8,128)(2,1)}, bf16[384,2048]{1,0:T(8,128)(2,1)}, u32[]{:S(2)}, u32[]{:S(2)}) collective-permute-start(bf16[384,2048]{1,0:T(8,128)(2,1)} %select_convert_fusion), channel_id=1, source_target_pairs={{0,1},{1,0},{2,3},{3,2},{4,5},{5,4},{6,7},{7,6},{8,9},{9,8},{10,11... | collective-permute-start | bytes 4718600 | tf_op jit(solution)/shard_map/ppermute | solution.py:139
  128.2 10.7 %copy-start.1 = (f32[384,1024]{1,0:T(8,128)S(1)}, f32[384,1024]{1,0:T(8,128)}, u32[]{:S(2)}) copy-start(f32[384,1024]{1,0:T(8,128)} %copy-done) | copy-start | bytes 4718596
  128.2 10.7 %copy-start.3 = (f32[384,1024]{1,0:T(8,128)S(1)}, f32[384,1024]{1,0:T(8,128)}, u32[]{:S(2)}) copy-start(f32[384,1024]{1,0:T(8,128)} %copy-done.2) | copy-start | bytes 4718596
  128.2 10.7 %copy-start.5 = (f32[384,1024]{1,0:T(8,128)S(1)}, f32[384,1024]{1,0:T(8,128)}, u32[]{:S(2)}) copy-start(f32[384,1024]{1,0:T(8,128)} %copy-done.4) | copy-start | bytes 4718596
  128.2 10.7 %copy-start.7 = (f32[384,1024]{1,0:T(8,128)S(1)}, f32[384,1024]{1,0:T(8,128)}, u32[]{:S(2)}) copy-start(f32[384,1024]{1,0:T(8,128)} %copy-done.6) | copy-start | bytes 4718596
  147.6 24.6 %all-to-all-start.5 = ((bf16[8,48,1024]{2,1,0:T(8,128)(2,1)}), bf16[8,48,1024]{2,1,0:T(8,128)(2,1)}, u32[]{:S(2)}, u32[]{:S(2)}) async-start(bf16[8,48,1024]{2,1,0:T(8,128)(2,1)} %bitcast.81), calls=%async_computation.5 | async-start | bytes 1572864 | tf_op jit(solution)/shard_map/all_to_all | solution.py:86
  155.9 1.1 copy-start.8
  158.1 22.7 %collective-permute-start.5 = (f32[192,1024]{1,0:T(8,128)}, f32[192,1024]{1,0:T(8,128)}, u32[]{:S(2)}, u32[]{:S(2)}) collective-permute-start(f32[192,1024]{1,0:T(8,128)} %slice_select_fusion), channel_id=1, source_target_pairs={{0,2},{1,3},{2,0},{3,1},{4,6},{5,7},{6,4},{7,5},{8,10},{9,11},{10,... | collective-permute-start | bytes 2359304 | tf_op jit(solution)/shard_map/ppermute | solution.py:147
  172.2 24.3 %all-to-all-start.4 = ((bf16[8,48,1024]{2,1,0:T(8,128)(2,1)}), bf16[8,48,1024]{2,1,0:T(8,128)(2,1)}, u32[]{:S(2)}, u32[]{:S(2)}) async-start(bf16[8,48,1024]{2,1,0:T(8,128)(2,1)} %bitcast.80), calls=%async_computation.4 | async-start | bytes 1572864 | tf_op jit(solution)/shard_map/all_to_all | solution.py:86
  176.6 4.1 %copy-start.9 = (f32[192,2048]{1,0:T(8,128)S(1)}, f32[192,2048]{1,0:T(8,128)}, u32[]{:S(2)}) copy-start(f32[192,2048]{1,0:T(8,128)} %copy-done.8) | copy-start | bytes 4718596
  179.2 3.5 %copy-start.21 = (bf16[384,768]{1,0:T(8,128)(2,1)S(1)}, bf16[384,768]{1,0:T(8,128)(2,1)}, u32[]{:S(2)}) copy-start(bf16[384,768]{1,0:T(8,128)(2,1)} %copy-done.20) | copy-start | bytes 1769476
  179.2 18.8 %collective-permute-start.8 = (f32[192,1024]{1,0:T(8,128)}, f32[192,1024]{1,0:T(8,128)}, u32[]{:S(2)}, u32[]{:S(2)}) collective-permute-start(f32[192,1024]{1,0:T(8,128)} %fusion.55), channel_id=1, source_target_pairs={{0,2},{1,3},{2,0},{3,1},{4,6},{5,7},{6,4},{7,5},{8,10},{9,11},{10,... | collective-permute-start | bytes 2359304 | tf_op jit(solution)/shard_map/ppermute | solution.py:165

commit v7 on v6

--- a/solution.py
+++ b/solution.py
@@ -80,6 +80,14 @@
         jnp.sum(jnp.where(pick, gates[:, k][None, :], 0.0), axis=1) for k, pick in enumerate(picks)
     )
     dispatch_mat = dispatch.astype(bf16)
+    picks_other = [
+        (local_slot[:, k][None, :] == slot_iota) & ~owned[:, k][None, :]
+        for k in range(route_ids.shape[1])
+    ]
+    dispatch_other = picks_other[0]
+    for extra in picks_other[1:]:
+        dispatch_other = dispatch_other | extra
+    dispatch_other_mat = dispatch_other.astype(bf16)
 
     def send(buf):
         width = buf.shape[-1]
@@ -140,14 +148,16 @@
             summed = summed + got.astype(f32)
         return lax.optimization_barrier((summed.astype(bf16), hold))
 
-    def finish(sub):
-        pieces = [sub[:, p * slice_w:(p + 1) * slice_w] for p in range(EXP_DEV)]
+    def to_sections(summed, hold=()):
+        pieces = [summed[:, p * slice_w:(p + 1) * slice_w] for p in range(EXP_DEV)]
         keep = pick_by(half, pieces)
-        give = pick_by((half + 1) % EXP_DEV, pieces)
-        return (keep + lax.ppermute(give, "exp", half_swap)).astype(bf16)
+        give = lax.ppermute(pick_by((half + 1) % EXP_DEV, pieces), "exp", half_swap)
+        payload, hold = lax.optimization_barrier((jnp.concatenate([keep, give], axis=1), hold))
+        back = send(payload)
+        return back[:, :slice_w], back[:, slice_w:], hold
 
     sum_out, got_d = group_sum(out_loc, got_d)
-    back_out = send(sum_out)
+    out_keep, out_give, _ = to_sections(sum_out)
     d_rows = to_experts(got_d)
     grad_act = jnp.einsum("sd,hd->sh", d_rows, down_mat, preferred_element_type=f32)
     grad_pre = (grad_act * gelu_slope).astype(bf16)
@@ -157,24 +167,24 @@
         dx_g = jnp.einsum("sh,dh->sd", grad_pre[:, part], w_up[g], preferred_element_type=f32)
         dx_g = dx_g.astype(bf16).astype(f32)
         dx_loc = dx_g if dx_loc is None else dx_loc + dx_g
-    grad_down = jnp.einsum("sh,sd->hd", activation, d_rows, preferred_element_type=f32)
-    sum_dx, (x_late, pre_late, grad_down) = group_sum(dx_loc, (x_rows, grad_pre, grad_down))
-    dx_pieces = [sum_dx[:, p * slice_w:(p + 1) * slice_w] for p in range(EXP_DEV)]
-    back_give = send(pick_by((half + 1) % EXP_DEV, dx_pieces))
-    dx_give = jnp.dot(dispatch_mat.T, back_give, preferred_element_type=f32)
-    dx_came = lax.ppermute(dx_give, "exp", half_swap)
-    back_keep = send(pick_by(half, dx_pieces))
-    dx_give, x_late, pre_late = lax.optimization_barrier((dx_give, x_late, pre_late))
+    sum_dx, late = group_sum(dx_loc, (activation, d_rows, x_rows, grad_pre))
+    dx_keep, dx_give, late = to_sections(sum_dx, late)
+    act_late, d_late, x_late, pre_late = late
+    grad_down = jnp.einsum("sh,sd->hd", act_late, d_late, preferred_element_type=f32)
     grad_up = jnp.einsum("sd,sh->dh", x_late, pre_late, preferred_element_type=f32)
-    back_keep, grad_up = lax.optimization_barrier((back_keep, grad_up))
-    grad_patches = (jnp.dot(dispatch_mat.T, back_keep, preferred_element_type=f32) + dx_came).astype(bf16)
-
-    mixed_sub = None
-    for k, pick in enumerate(picks):
-        picked = jnp.dot(pick.astype(bf16).T, back_out, preferred_element_type=f32)
+
+    mixed = None
+    for k in range(len(picks)):
+        picked = jnp.dot(picks[k].astype(bf16).T, out_keep, preferred_element_type=f32)
+        picked = picked + jnp.dot(picks_other[k].astype(bf16).T, out_give, preferred_element_type=f32)
         term = gates[:, k][:, None] * picked
-        mixed_sub = term if mixed_sub is None else mixed_sub + term
-    mixed = finish(mixed_sub)
+        mixed = term if mixed is None else mixed + term
+    mixed = mixed.astype(bf16)
+    dx_keep, dx_give, grad_up, grad_down = lax.optimization_barrier((dx_keep, dx_give, grad_up, grad_down))
+    grad_patches = (
+        jnp.dot(dispatch_mat.T, dx_keep, preferred_element_type=f32)
+        + jnp.dot(dispatch_other_mat.T, dx_give, preferred_element_type=f32)
+    ).astype(bf16)
     grad_up = jnp.transpose(grad_up.reshape(model_width, n_loc, hid_loc), (1, 0, 2))
     grad_down = grad_down.reshape(n_loc, hid_loc, model_width)
     return (mixed, grad_patches, grad_up, grad_down)

time: 201 us -> 215 us (1.070)
  waiting for transfers between devices: 78.6 us -> 95.8 us
  starting transfers between devices: 36.2 us -> 31.8 us
  other arithmetic: 21.6 us -> 24.9 us
  matrix products: 51.7 us -> 48.6 us
    ppermute x2, waiting for transfers between devices: 1.57 us -> 18.3 us  [to_sections(): give = lax.ppermute(pick_by((half + 1) % EXP_DEV, pieces), 'exp', half_swap)]
    concatenate x0 -> x3, other arithmetic: none -> 5.88 us  [the longest x1 3.31 us: to_experts(): jnp.concatenate([ordered[q][:, p * slice_w:(p + 1) * slice_w] for p in ra...]
    dot_general x5 -> x7, matrix products: 19.9 us -> 15.3 us  [the longest x1 6.6 us: on_device(): jnp.einsum('sh,sd->hd', act_late, d_late, preferred_element_type=f32)]
    all_to_all x6 -> x5, starting transfers between devices: 30.4 us -> 26.2 us  [send(): lax.all_to_all(buf.reshape(sections, capacity, width), 'attn', split_axis...]
    unnamed x55 -> x57, local copies, waits for them, and re-layouts: 7.63 us -> 6.75 us
    all_to_all x6 -> x5, waiting for transfers between devices: 56.4 us -> 56.3 us  [send(): lax.all_to_all(buf.reshape(sections, capacity, width), 'attn', split_axis...]
  transfers between devices with their start and end apart: 15 -> 14, of which waited for: 10 -> 11; matrix products, arithmetic and copies ran while one was open for 34% -> 32% of each run, Pallas kernels for 0% -> 0%
where the time goes in v7:
time: 215 us; the launch traced here: 214 us
  waiting for transfers between devices  95.8 us (45%)
  matrix products  48.6 us (23%)
  starting transfers between devices  31.8 us (15%)
  other arithmetic  24.9 us (12%)
  local copies, waits for them, and re-layouts  11.9 us (6%)
    all_to_all x5, waiting for transfers between devices, send(): lax.all_to_all(buf.reshape(sections, capacity, width), 'attn', split_axis...  56.3 us
    all_to_all x5, starting transfers between devices, send(): lax.all_to_all(buf.reshape(sections, capacity, width), 'attn', split_axis...  26.2 us
    ppermute x2, waiting for transfers between devices, to_sections(): give = lax.ppermute(pick_by((half + 1) % EXP_DEV, pieces), 'exp', half_swap)  18.3 us
    ppermute x1, waiting for transfers between devices, core_subset(): other = lax.ppermute(local, 'exp', half_swap)  10 us
    convert_element_type x2, other arithmetic, group_sum(): return lax.optimization_barrier((summed.astype(bf16), hold))  7.58 us
    dot_general x1, matrix products, on_device(): jnp.einsum('sd,hd->sh', d_rows, down_mat, preferred_element_type=f32)  7.05 us
    ppermute x1, waiting for transfers between devices, on_device(): x_other = lax.ppermute(patches, 'exp', half_swap)  6.82 us
    unnamed x57, local copies, waits for them, and re-layouts  6.75 us
  transfers between devices with their start and end apart: 14, of which 11 were waited for; matrix products, arithmetic and copies ran while one was open for 32% of the time, Pallas kernels for 0%

profile of v7, /device:TPU:0, one launch (start us, length us, event | category | flops | bytes accessed | tf_op | source)
XLA Modules:
  0.0 214.2 jit_solution(16845899336674831549)
XLA Ops:
  0.6 0.7 broadcast_compare_fusion
  1.3 0.8 copy.30
  2.6 0.9 reduce-window.6
  4.5 2.4 %convolution_convert_fusion = bf16[384,1024]{1,0:T(8,128)(2,1)} fusion(bf16[192,1024]{1,0:T(8,128)(2,1)} %param.6, s32[192]{0:T(256)S(1)} %get-tuple-element.45, s32[192]{0:T(256)S(1)} %get-tuple-element.44, pred[192]{0:T(512)(128)(4,1)S(1)} %get-tuple-element.47, pred[192]{0:T(512)(128)(4,1)S(1)} %get-tuple-element.46), kind=kOutput, calls=%fused_computation.30 | convolution fusion | flops 151756800 | bytes 1181568 | tf_op jit(solution)/shard_map/dot_general | solution.py:98
  7.0 7.3 %all-to-all-start = ((bf16[8,48,1024]{2,1,0:T(8,128)(2,1)}), bf16[8,48,1024]{2,1,0:T(8,128)(2,1)S(1)}, u32[]{:S(2)}, u32[]{:S(2)}) async-start(bf16[8,48,1024]{2,1,0:T(8,128)(2,1)} %bitcast.3), calls=%async_computation | async-start | bytes 1572864 | tf_op jit(solution)/shard_map/all_to_all | solution.py:94
  14.3 1.6 collective-permute-start
  15.8 0.5 collective-permute-start.1
  16.3 10.0 %collective-permute-done = bf16[192,1024]{1,0:T(8,128)(2,1)S(1)} collective-permute-done((bf16[192,1024]{1,0:T(8,128)(2,1)S(1)}, bf16[192,1024]{1,0:T(8,128)(2,1)S(1)}, u32[]{:S(2)}, u32[]{:S(2)}) %collective-permute-start) | collective-permute-done | bytes 393248 | tf_op jit(solution)/shard_map/ppermute | solution.py:49
  26.5 6.8 %collective-permute-done.1 = bf16[192,1024]{1,0:T(8,128)(2,1)S(1)} collective-permute-done((bf16[192,1024]{1,0:T(8,128)(2,1)S(1)}, bf16[192,1024]{1,0:T(8,128)(2,1)S(1)}, u32[]{:S(2)}, u32[]{:S(2)}) %collective-permute-start.1) | collective-permute-done | bytes 393248 | tf_op jit(solution)/shard_map/ppermute | solution.py:99
  33.3 1.4 convolution_convert_fusion.1
  34.8 5.7 %all-to-all-start.1 = ((bf16[8,48,1024]{2,1,0:T(8,128)(2,1)}), bf16[8,48,1024]{2,1,0:T(8,128)(2,1)S(1)}, u32[]{:S(2)}, u32[]{:S(2)}) async-start(bf16[8,48,1024]{2,1,0:T(8,128)(2,1)} %bitcast.5), calls=%async_computation.1 | async-start | bytes 1572864 | tf_op jit(solution)/shard_map/all_to_all | solution.py:94
  40.4 18.7 %all-to-all-done.1 = bf16[8,48,1024]{2,1,0:T(8,128)(2,1)S(1)} async-done(((bf16[8,48,1024]{2,1,0:T(8,128)(2,1)}), bf16[8,48,1024]{2,1,0:T(8,128)(2,1)S(1)}, u32[]{:S(2)}, u32[]{:S(2)}) %all-to-all-start.1) | async-done | bytes 786464 | tf_op jit(solution)/shard_map/all_to_all | solution.py:94
  59.2 0.2 select_reduce_fusion
  59.4 1.9 multiply_convert_fusion
  61.3 0.2 collective-permute-done.3
  61.6 1.4 broadcast_select_fusion.9
  63.0 0.3 pad_maximum_fusion
  63.3 4.5 %all-to-all-start.2 = ((bf16[8,48,2048]{2,1,0:T(8,128)(2,1)}), bf16[8,48,2048]{2,1,0:T(8,128)(2,1)}, u32[]{:S(2)}, u32[]{:S(2)}) async-start(bf16[8,48,2048]{2,1,0:T(8,128)(2,1)} %bitcast.86), calls=%async_computation.2 | async-start | bytes 3145728 | tf_op jit(solution)/shard_map/all_to_all | solution.py:94
  67.8 6.5 %multiply_convert_fusion.1 = (bf16[384,768]{1,0:T(8,128)(2,1)S(1)}, f32[384,768]{1,0:T(8,128)}) fusion(bf16[384,4096]{1,0:T(8,128)(2,1)S(1)} %pad_maximum_fusion, bf16[1,4096,768]{2,1,0:T(8,128)(2,1)} %param.10), kind=kOutput, calls=%fused_computation.46 | convolution fusion | flops 2418573312 | bytes 11206656 | tf_op jit(solution)/shard_map/dot_general | solution.py:125
  74.2 0.8 copy-done.17
  75.1 4.8 %fusion.17 = f32[384,4096]{1,0:T(8,128)S(1)} fusion(bf16[384,768]{1,0:T(8,128)(2,1)S(1)} %get-tuple-element.38, bf16[1,768,4096]{2,1,0:T(8,128)(2,1)} %param.11), kind=kOutput, calls=%fused_computation.11 | convolution fusion | flops 2419064832 | bytes 13172736 | tf_op jit(solution)/shard_map/dot_general | solution.py:132
  79.8 1.1 fusion.80
  81.0 1.9 select_convert_fusion.1
  83.1 0.6 copy-done.10
  83.7 0.5 copy-done.11
  84.1 0.3 collective-permute-start.4
  84.4 3.5 %collective-permute-done.4 = bf16[384,2048]{1,0:T(8,128)(2,1)} collective-permute-done((bf16[384,2048]{1,0:T(8,128)(2,1)}, bf16[384,2048]{1,0:T(8,128)(2,1)}, u32[]{:S(2)}, u32[]{:S(2)}) %collective-permute-start.4) | collective-permute-done | bytes 1572896 | tf_op jit(solution)/shard_map/ppermute | solution.py:147
  87.9 5.3 %add_convert_fusion.1 = bf16[384,2048]{1,0:T(8,128)(2,1)} fusion(bf16[384,2048]{1,0:T(8,128)(2,1)} %collective-permute-done.4, f32[384,1024]{1,0:T(8,128)} %copy-done.9, f32[384,1024]{1,0:T(8,128)} %copy-done.10, f32[384,1024]{1,0:T(8,128)} %copy-done.11, f32[384,1024]{1,0:T(8,128)} %copy-done.8, pred[]{:T(512)S(6)} %eq.141), kind=kLoop, calls=%fused_computation.20 | loop fusion | flops 4718592 | bytes 9437185 | tf_op jit(solution)/shard_map/convert_element_type | solution.py:149
  93.2 12.1 %all-to-all-done.2 = bf16[8,48,2048]{2,1,0:T(8,128)(2,1)} async-done(((bf16[8,48,2048]{2,1,0:T(8,128)(2,1)}), bf16[8,48,2048]{2,1,0:T(8,128)(2,1)}, u32[]{:S(2)}, u32[]{:S(2)}) %all-to-all-start.2) | async-done | bytes 1572896 | tf_op jit(solution)/shard_map/all_to_all | solution.py:94
  105.3 1.6 broadcast_select_fusion.11
  106.9 1.6 collective-permute-start.5
  108.5 0.5 collective-permute-done.6
  109.0 2.1 broadcast_select_fusion.1
  111.5 0.7 copy-done.13
  112.2 0.3 copy-done.14
  112.5 7.1 %fusion.23 = bf16[384,768]{1,0:T(8,128)(2,1)S(1)} fusion(bf16[1,768,4096]{2,1,0:T(8,128)(2,1)S(1)} %bitcast.81, f32[384,768]{1,0:T(8,128)} %get-tuple-element.77, bf16[384,1024]{1,0:T(8,128)(2,1)S(1)} %get-tuple-element.69, bf16[384,1024]{1,0:T(8,128)(2,1)S(1)} %get-tuple-element.67, bf16[384,1024]{1,0:T(8,128)(2,1)S(1)} %get-tuple-element.68, ...), kind=kOutput, calls=%fused_computation.32 | convolution fusion | flops 2434105344 | bytes 11206656 | tf_op jit(solution)/shard_map/sd,hd->sh/dot_general | solution.py:162
  119.6 2.6 %fusion.11 = f32[384,4096]{1,0:T(8,128)S(1)} fusion(bf16[384,768]{1,0:T(8,128)(2,1)S(1)} %fusion.23, bf16[1,4096,768]{2,1,0:T(8,128)(2,1)S(1)} %bitcast.93), kind=kOutput, calls=%fused_computation.9 | convolution fusion | flops 2419064832 | bytes 13172736 | tf_op jit(solution)/shard_map/sh,dh->sd/dot_general | solution.py:167
  122.2 1.1 fusion.79
  123.4 1.9 select_convert_fusion
  125.3 0.2 copy-done.2
  125.5 0.5 copy-done.4
  126.0 0.5 copy-done.6
  126.7 0.3 collective-permute-done.5
  127.0 1.3 pad_maximum_fusion.6
  128.2 4.5 %all-to-all-start.3 = ((bf16[8,48,2048]{2,1,0:T(8,128)(2,1)}), bf16[8,48,2048]{2,1,0:T(8,128)(2,1)}, u32[]{:S(2)}, u32[]{:S(2)}) async-start(bf16[8,48,2048]{2,1,0:T(8,128)(2,1)} %bitcast.82), calls=%async_computation.3 | async-start | bytes 3145728 | tf_op jit(solution)/shard_map/all_to_all | solution.py:94
  132.8 3.3 %pad_maximum_fusion.3 = bf16[384,4096]{1,0:T(8,128)(2,1)} fusion(bf16[384,1024]{1,0:T(8,128)(2,1)} %copy-done.16, bf16[384,1024]{1,0:T(8,128)(2,1)} %copy-done.14, bf16[384,1024]{1,0:T(8,128)(2,1)} %copy-done.15, bf16[384,1024]{1,0:T(8,128)(2,1)} %copy-done.13), kind=kLoop, calls=%fused_computation.15 | loop fusion | flops 12582912 | bytes 6291456 | tf_op jit(solution)/shard_map/concatenate | solution.py:64
  136.1 1.1 copy-done.5
  137.2 0.5 copy-done.7
  137.7 2.3 %add_convert_fusion = bf16[384,2048]{1,0:T(8,128)(2,1)S(1)} fusion(bf16[384,2048]{1,0:T(8,128)(2,1)} %collective-permute-done.7, f32[384,1024]{1,0:T(8,128)S(1)} %copy-done.3, f32[384,1024]{1,0:T(8,128)S(1)} %copy-done.5, f32[384,1024]{1,0:T(8,128)S(1)} %copy-done.7, f32[384,1024]{1,0:T(8,128)S(1)} %copy-done.1, pred[]{:T(512)S(6)} %eq.141), kind=kLoop, calls=%fused_computation.18 | loop fusion | flops 4718592 | bytes 9437185 | tf_op jit(solution)/shard_map/convert_element_type | solution.py:149
  140.1 1.6 collective-permute-start.8
  141.7 18.0 %collective-permute-done.8 = bf16[384,1024]{1,0:T(8,128)(2,1)S(1)} collective-permute-done((bf16[384,1024]{1,0:T(8,128)(2,1)S(1)}, bf16[384,1024]{1,0:T(8,128)(2,1)S(1)}, u32[]{:S(2)}, u32[]{:S(2)}) %collective-permute-start.8) | collective-permute-done | bytes 786464 | tf_op jit(solution)/shard_map/ppermute | solution.py:154
  159.7 1.3 pad_maximum_fusion.7
  161.0 9.1 %all-to-all-done.3 = bf16[8,48,2048]{2,1,0:T(8,128)(2,1)} async-done(((bf16[8,48,2048]{2,1,0:T(8,128)(2,1)}), bf16[8,48,2048]{2,1,0:T(8,128)(2,1)}, u32[]{:S(2)}, u32[]{:S(2)}) %all-to-all-start.3) | async-done | bytes 1572896 | tf_op jit(solution)/shard_map/all_to_all | solution.py:94
  170.1 4.3 %all-to-all-start.4 = ((bf16[8,48,2048]{2,1,0:T(8,128)(2,1)}), bf16[8,48,2048]{2,1,0:T(8,128)(2,1)}, u32[]{:S(2)}, u32[]{:S(2)}) async-start(bf16[8,48,2048]{2,1,0:T(8,128)(2,1)} %bitcast.83), calls=%async_computation.4 | async-start | bytes 3145728 | tf_op jit(solution)/shard_map/all_to_all | solution.py:94
  174.4 1.5 fusion.38
  176.0 1.5 fusion.40
  177.5 1.6 fusion.28
  179.1 2.4 %fusion.29 = bf16[192,1024]{1,0:T(8,128)(2,1)} fusion(f32[192,1024]{1,0:T(8,128)S(1)} %fusion.28, f32[192,1024]{1,0:T(8,128)S(1)} %fusion.40, bf16[384,2048]{1,0:T(8,128)(2,1)} %bitcast.12, f32[192]{0:T(256)S(1)} %bitcast.88, s32[192]{0:T(256)S(1)} %get-tuple-element.44, pred[192]{0:T(512)(128)(4,1)S(1)} %not.16), kind=kOutput, calls=%fused_computation.39 | convolution fusion | flops 151928832 | bytes 2754240 | tf_op jit(solution)/shard_map/dot_general | solution.py:179
  181.5 6.6 %fusion.85 = f32[4096,768]{1,0:T(8,128)} fusion(bf16[384,4096]{1,0:T(8,128)(2,1)S(1)} %pad_maximum_fusion, bf16[384,768]{1,0:T(8,128)(2,1)S(1)} %copy-done.20), kind=kOutput, calls=%fused_computation.122 | convolution fusion | flops 2415919104 | bytes 16318464 | tf_op jit(solution)/shard_map/sd,sh->dh/dot_general | solution.py:174
  188.1 6.6 %fusion.86 = f32[768,4096]{1,0:T(8,128)} fusion(bf16[384,768]{1,0:T(8,128)(2,1)S(1)} %copy-done.18, bf16[384,4096]{1,0:T(8,128)(2,1)S(1)} %copy-done.12), kind=kOutput, calls=%fused_computation.123 | convolution fusion | flops 2415919104 | bytes 16318464 | tf_op jit(solution)/shard_map/sh,sd->hd/dot_general | solution.py:173
  194.7 16.4 %all-to-all-done.4 = bf16[8,48,2048]{2,1,0:T(8,128)(2,1)} async-done(((bf16[8,48,2048]{2,1,0:T(8,128)(2,1)}), bf16[8,48,2048]{2,1,0:T(8,128)(2,1)}, u32[]{:S(2)}, u32[]{:S(2)}) %all-to-all-start.4) | async-done | bytes 1572896 | tf_op jit(solution)/shard_map/all_to_all | solution.py:94
  211.1 1.5 fusion.81
  212.6 0.4 fusion.74
  213.0 1.2 fusion.30
  (76 shorter events, 2.4 us)
Async XLA Ops:
  4.2 10.0 %copy-start.21 = (bf16[192,1024]{1,0:T(8,128)(2,1)S(1)}, bf16[192,1024]{1,0:T(8,128)(2,1)}, u32[]{:S(2)}) copy-start(bf16[192,1024]{1,0:T(8,128)(2,1)} %param.7) | copy-start | bytes 1179652
  4.2 11.6 %copy-start.22 = (bf16[192,1024]{1,0:T(8,128)(2,1)S(1)}, bf16[192,1024]{1,0:T(8,128)(2,1)}, u32[]{:S(2)}) copy-start(bf16[192,1024]{1,0:T(8,128)(2,1)} %param.6) | copy-start | bytes 1179652
  7.0 27.8 %all-to-all-start = ((bf16[8,48,1024]{2,1,0:T(8,128)(2,1)}), bf16[8,48,1024]{2,1,0:T(8,128)(2,1)S(1)}, u32[]{:S(2)}, u32[]{:S(2)}) async-start(bf16[8,48,1024]{2,1,0:T(8,128)(2,1)} %bitcast.3), calls=%async_computation | async-start | bytes 1572864 | tf_op jit(solution)/shard_map/all_to_all | solution.py:94
  14.3 12.1 %collective-permute-start = (bf16[192,1024]{1,0:T(8,128)(2,1)S(1)}, bf16[192,1024]{1,0:T(8,128)(2,1)S(1)}, u32[]{:S(2)}, u32[]{:S(2)}) collective-permute-start(bf16[192,1024]{1,0:T(8,128)(2,1)S(1)} %copy-done.21), channel_id=1, source_target_pairs={{0,2},{1,3},{2,0},{3,1},{4,6},{5,7},{6,4},{7,5},{8,10},{9,11},{10,... | collective-permute-start | bytes 1179656 | tf_op jit(solution)/shard_map/ppermute | solution.py:49
  15.8 17.5 %collective-permute-start.1 = (bf16[192,1024]{1,0:T(8,128)(2,1)S(1)}, bf16[192,1024]{1,0:T(8,128)(2,1)S(1)}, u32[]{:S(2)}, u32[]{:S(2)}) collective-permute-start(bf16[192,1024]{1,0:T(8,128)(2,1)S(1)} %copy-done.22), channel_id=1, source_target_pairs={{0,2},{1,3},{2,0},{3,1},{4,6},{5,7},{6,4},{7,5},{8,10},{9,11},{10,... | collective-permute-start | bytes 1179656 | tf_op jit(solution)/shard_map/ppermute | solution.py:99
  26.5 32.7 %copy-start.23 = (f32[192,2]{0,1:T(2,128)S(1)}, f32[192,2]{0,1:T(2,128)}, u32[]{:S(2)}) copy-start(f32[192,2]{0,1:T(2,128)} %param.9) | copy-start | bytes 4612
  34.8 24.4 %all-to-all-start.1 = ((bf16[8,48,1024]{2,1,0:T(8,128)(2,1)}), bf16[8,48,1024]{2,1,0:T(8,128)(2,1)S(1)}, u32[]{:S(2)}, u32[]{:S(2)}) async-start(bf16[8,48,1024]{2,1,0:T(8,128)(2,1)} %bitcast.5), calls=%async_computation.1 | async-start | bytes 1572864 | tf_op jit(solution)/shard_map/all_to_all | solution.py:94
  40.4 20.9 %collective-permute-start.2 = (bf16[384,1024]{1,0:T(8,128)(2,1)S(1)}, bf16[384,1024]{1,0:T(8,128)(2,1)S(1)}, u32[]{:S(2)}, u32[]{:S(2)}) collective-permute-start(bf16[384,1024]{1,0:T(8,128)(2,1)S(1)} %bitcast.84), channel_id=1, source_target_pairs={{0,1},{1,0},{2,3},{3,2},{4,5},{5,4},{6,7},{7,6},{8,9},{9,8},{10,11... | collective-permute-start | bytes 2359304 | tf_op jit(solution)/shard_map/ppermute | solution.py:106
  59.2 2.4 %collective-permute-start.3 = (bf16[384,1024]{1,0:T(8,128)(2,1)S(1)}, bf16[384,1024]{1,0:T(8,128)(2,1)}, u32[]{:S(2)}, u32[]{:S(2)}) collective-permute-start(bf16[384,1024]{1,0:T(8,128)(2,1)S(1)} %bitcast.85), channel_id=1, source_target_pairs={{0,1},{1,0},{2,3},{3,2},{4,5},{5,4},{6,7},{7,6},{8,9},{9,8},{10,11... | collective-permute-start | bytes 2359304 | tf_op jit(solution)/shard_map/ppermute | solution.py:107
  63.3 42.0 %all-to-all-start.2 = ((bf16[8,48,2048]{2,1,0:T(8,128)(2,1)}), bf16[8,48,2048]{2,1,0:T(8,128)(2,1)}, u32[]{:S(2)}, u32[]{:S(2)}) async-start(bf16[8,48,2048]{2,1,0:T(8,128)(2,1)} %bitcast.86), calls=%async_computation.2 | async-start | bytes 3145728 | tf_op jit(solution)/shard_map/all_to_all | solution.py:94
  74.2 0.8 copy-start.17
  81.0 1.9 copy-start.8
  81.0 2.1 copy-start.9
  81.0 2.7 %copy-start.10 = (f32[384,1024]{1,0:T(8,128)}, f32[384,1024]{1,0:T(8,128)S(1)}, u32[]{:S(2)}) copy-start(f32[384,1024]{1,0:T(8,128)S(1)} %get-tuple-element.54) | copy-start | bytes 4718596
  81.0 3.2 %copy-start.11 = (f32[384,1024]{1,0:T(8,128)}, f32[384,1024]{1,0:T(8,128)S(1)}, u32[]{:S(2)}) copy-start(f32[384,1024]{1,0:T(8,128)S(1)} %get-tuple-element.55) | copy-start | bytes 4718596
  84.1 3.8 %collective-permute-start.4 = (bf16[384,2048]{1,0:T(8,128)(2,1)}, bf16[384,2048]{1,0:T(8,128)(2,1)}, u32[]{:S(2)}, u32[]{:S(2)}) collective-permute-start(bf16[384,2048]{1,0:T(8,128)(2,1)} %select_convert_fusion.1), channel_id=1, source_target_pairs={{0,1},{1,0},{2,3},{3,2},{4,5},{5,4},{6,7},{7,6},{8,9},{9,8},{10,11... | collective-permute-start | bytes 4718600 | tf_op jit(solution)/shard_map/ppermute | solution.py:147
  105.3 3.8 %collective-permute-start.6 = (bf16[384,2048]{1,0:T(8,128)(2,1)}, bf16[384,2048]{1,0:T(8,128)(2,1)}, u32[]{:S(2)}, u32[]{:S(2)}) collective-permute-start(bf16[384,2048]{1,0:T(8,128)(2,1)} %bitcast.10), channel_id=1, source_target_pairs={{0,1},{1,0},{2,3},{3,2},{4,5},{5,4},{6,7},{7,6},{8,9},{9,8},{10,11... | collective-permute-start | bytes 4718600 | tf_op jit(solution)/shard_map/ppermute | solution.py:62
  105.3 7.1 %slice-start = ((s8[6291456]{0:T(1024)(128)(4,1)}), s8[4194304]{0:T(1024)(128)(4,1)S(1)}, s32[]{:S(2)}) async-start(s8[6291456]{0:T(1024)(128)(4,1)} %bitcast.80), calls=%async_computation.5 | async-start | bytes 8388608
  106.9 5.5 %slice-start.1 = ((s8[6291456]{0:T(1024)(128)(4,1)}), s8[2097152]{0:T(1024)(128)(4,1)S(1)}, s32[]{:S(2)}) async-start(s8[6291456]{0:T(1024)(128)(4,1)} %bitcast.80), calls=%async_computation.6 | async-start | bytes 4194304
  106.9 20.0 %collective-permute-start.5 = (bf16[384,1024]{1,0:T(8,128)(2,1)S(1)}, bf16[384,1024]{1,0:T(8,128)(2,1)S(1)}, u32[]{:S(2)}, u32[]{:S(2)}) collective-permute-start(bf16[384,1024]{1,0:T(8,128)(2,1)S(1)} %get-tuple-element.71), channel_id=1, source_target_pairs={{0,2},{1,3},{2,0},{3,1},{4,6},{5,7},{6,4},{7,5},{8,10},{9,11},{10,... | collective-permute-start | bytes 2359304 | tf_op jit(solution)/shard_map/ppermute | solution.py:154
  111.3 0.9 copy-start.13
  111.3 1.2 copy-start.14
  111.3 8.2 %slice-start.2 = ((s8[6291456]{0:T(1024)(128)(4,1)}), s8[4194304]{0:T(1024)(128)(4,1)S(1)}, s32[]{:S(2)}) async-start(s8[6291456]{0:T(1024)(128)(4,1)} %bitcast.92), calls=%async_computation.7 | async-start | bytes 8388608
  111.5 8.1 %copy-start.15 = (bf16[384,1024]{1,0:T(8,128)(2,1)}, bf16[384,1024]{1,0:T(8,128)(2,1)S(1)}, u32[]{:S(2)}) copy-start(bf16[384,1024]{1,0:T(8,128)(2,1)S(1)} %get-tuple-element.68) | copy-start | bytes 2359300
  111.5 8.1 %copy-start.16 = (bf16[384,1024]{1,0:T(8,128)(2,1)}, bf16[384,1024]{1,0:T(8,128)(2,1)S(1)}, u32[]{:S(2)}) copy-start(bf16[384,1024]{1,0:T(8,128)(2,1)S(1)} %get-tuple-element.69) | copy-start | bytes 2359300
  112.4 7.1 %slice-start.3 = ((s8[6291456]{0:T(1024)(128)(4,1)}), s8[2097152]{0:T(1024)(128)(4,1)S(1)}, s32[]{:S(2)}) async-start(s8[6291456]{0:T(1024)(128)(4,1)} %bitcast.92), calls=%async_computation.8 | async-start | bytes 4194304
  119.6 2.6 %copy-start.19 = (bf16[384,768]{1,0:T(8,128)(2,1)}, bf16[384,768]{1,0:T(8,128)(2,1)S(1)}, u32[]{:S(2)}) copy-start(bf16[384,768]{1,0:T(8,128)(2,1)S(1)} %fusion.23) | copy-start | bytes 1769476
  123.3 1.9 copy-start
  123.4 2.1 copy-start.2
  123.4 2.7 %copy-start.4 = (f32[384,1024]{1,0:T(8,128)}, f32[384,1024]{1,0:T(8,128)S(1)}, u32[]{:S(2)}) copy-start(f32[384,1024]{1,0:T(8,128)S(1)} %get-tuple-element.50) | copy-start | bytes 4718596
  123.4 3.2 %copy-start.6 = (f32[384,1024]{1,0:T(8,128)}, f32[384,1024]{1,0:T(8,128)S(1)}, u32[]{:S(2)}) copy-start(f32[384,1024]{1,0:T(8,128)S(1)} %get-tuple-element.51) | copy-start | bytes 4718596
  126.5 9.6 %collective-permute-start.7 = (bf16[384,2048]{1,0:T(8,128)(2,1)}, bf16[384,2048]{1,0:T(8,128)(2,1)}, u32[]{:S(2)}, u32[]{:S(2)}) collective-permute-start(bf16[384,2048]{1,0:T(8,128)(2,1)} %select_convert_fusion), channel_id=1, source_target_pairs={{0,1},{1,0},{2,3},{3,2},{4,5},{5,4},{6,7},{7,6},{8,9},{9,8},{10,11... | collective-permute-start | bytes 4718600 | tf_op jit(solution)/shard_map/ppermute | solution.py:147
  128.2 41.8 %all-to-all-start.3 = ((bf16[8,48,2048]{2,1,0:T(8,128)(2,1)}), bf16[8,48,2048]{2,1,0:T(8,128)(2,1)}, u32[]{:S(2)}, u32[]{:S(2)}) async-start(bf16[8,48,2048]{2,1,0:T(8,128)(2,1)} %bitcast.82), calls=%async_computation.3 | async-start | bytes 3145728 | tf_op jit(solution)/shard_map/all_to_all | solution.py:94
  132.8 3.4 %copy-start.1 = (f32[384,1024]{1,0:T(8,128)S(1)}, f32[384,1024]{1,0:T(8,128)}, u32[]{:S(2)}) copy-start(f32[384,1024]{1,0:T(8,128)} %copy-done) | copy-start | bytes 4718596
  132.8 3.4 %copy-start.3 = (f32[384,1024]{1,0:T(8,128)S(1)}, f32[384,1024]{1,0:T(8,128)}, u32[]{:S(2)}) copy-start(f32[384,1024]{1,0:T(8,128)} %copy-done.2) | copy-start | bytes 4718596
  132.8 4.4 %copy-start.5 = (f32[384,1024]{1,0:T(8,128)S(1)}, f32[384,1024]{1,0:T(8,128)}, u32[]{:S(2)}) copy-start(f32[384,1024]{1,0:T(8,128)} %copy-done.4) | copy-start | bytes 4718596
  132.8 4.9 %copy-start.7 = (f32[384,1024]{1,0:T(8,128)S(1)}, f32[384,1024]{1,0:T(8,128)}, u32[]{:S(2)}) copy-start(f32[384,1024]{1,0:T(8,128)} %copy-done.6) | copy-start | bytes 4718596
  140.1 19.6 %collective-permute-start.8 = (bf16[384,1024]{1,0:T(8,128)(2,1)S(1)}, bf16[384,1024]{1,0:T(8,128)(2,1)S(1)}, u32[]{:S(2)}, u32[]{:S(2)}) collective-permute-start(bf16[384,1024]{1,0:T(8,128)(2,1)S(1)} %get-tuple-element.65), channel_id=1, source_target_pairs={{0,2},{1,3},{2,0},{3,1},{4,6},{5,7},{6,4},{7,5},{8,10},{9,11},{10,... | collective-permute-start | bytes 2359304 | tf_op jit(solution)/shard_map/ppermute | solution.py:154
  170.1 41.0 %all-to-all-start.4 = ((bf16[8,48,2048]{2,1,0:T(8,128)(2,1)}), bf16[8,48,2048]{2,1,0:T(8,128)(2,1)}, u32[]{:S(2)}, u32[]{:S(2)}) async-start(bf16[8,48,2048]{2,1,0:T(8,128)(2,1)} %bitcast.83), calls=%async_computation.4 | async-start | bytes 3145728 | tf_op jit(solution)/shard_map/all_to_all | solution.py:94
  179.1 2.4 %copy-start.20 = (bf16[384,768]{1,0:T(8,128)(2,1)S(1)}, bf16[384,768]{1,0:T(8,128)(2,1)}, u32[]{:S(2)}) copy-start(bf16[384,768]{1,0:T(8,128)(2,1)} %copy-done.19) | copy-start | bytes 1769476
  181.5 6.6 %copy-start.12 = (bf16[384,4096]{1,0:T(8,128)(2,1)S(1)}, bf16[384,4096]{1,0:T(8,128)(2,1)}, u32[]{:S(2)}) copy-start(bf16[384,4096]{1,0:T(8,128)(2,1)} %pad_maximum_fusion.3) | copy-start | bytes 9437188
  181.5 6.6 %copy-start.18 = (bf16[384,768]{1,0:T(8,128)(2,1)S(1)}, bf16[384,768]{1,0:T(8,128)(2,1)}, u32[]{:S(2)}) copy-start(bf16[384,768]{1,0:T(8,128)(2,1)} %copy-done.17) | copy-start | bytes 1769476

commit v8 on v6

--- a/solution.py
+++ b/solution.py
@@ -45,13 +45,6 @@
 
     half_swap = [(i, (i + cores) % n_exp) for i in range(n_exp)]
 
-    def core_subset(local):
-        other = lax.ppermute(local, "exp", half_swap)
-        first = half == 0
-        return jnp.concatenate(
-            [jnp.where(first, local, other), jnp.where(first, other, local)], axis=1
-        )
-
     def pick_by(index, values):
         picked = values[0]
         for i, value in enumerate(values[1:], start=1):
@@ -88,9 +81,13 @@
         ).reshape(slots, width)
 
     got_own = send(jnp.dot(dispatch_mat, patches, preferred_element_type=f32).astype(bf16))
-    x_other = lax.ppermute(patches, "exp", half_swap)
+    both_other = lax.ppermute(jnp.concatenate([patches, grad_out], axis=1), "exp", half_swap)
+    x_other = both_other[:, :slice_w]
+    dy_other = both_other[:, slice_w:]
     other_buf = jnp.dot(dispatch_mat, x_other, preferred_element_type=f32).astype(bf16)
-    sub_dy = core_subset(grad_out)
+    sub_dy = jnp.concatenate(
+        [jnp.where(half == 0, grad_out, dy_other), jnp.where(half == 0, dy_other, grad_out)], axis=1
+    )
     sub_dy, other_buf = lax.optimization_barrier((sub_dy, other_buf))
     got_other = send(other_buf)
     dy_buf = jnp.dot(dispatch_mat, sub_dy, preferred_element_type=f32)

time: 201 us -> 201 us (level)
  waiting for transfers between devices: 78.6 us -> 83.5 us
  starting transfers between devices: 36.2 us -> 31.8 us
    all_to_all x6, waiting for transfers between devices: 56.4 us -> 70.5 us  [send(): lax.all_to_all(buf.reshape(sections, capacity, width), 'attn', split_axis...]
    ppermute x2 -> x1, waiting for transfers between devices: 16.8 us -> 7.74 us  [on_device(): lax.ppermute(jnp.concatenate([patches, grad_out], axis=1), 'exp', half_swap)]
    all_to_all x6, starting transfers between devices: 30.4 us -> 26.8 us  [send(): lax.all_to_all(buf.reshape(sections, capacity, width), 'attn', split_axis...]
    unnamed x55 -> x57, local copies, waits for them, and re-layouts: 7.63 us -> 6.96 us
  transfers between devices with their start and end apart: 15 -> 14, of which waited for: 10 -> 10; matrix products, arithmetic and copies ran while one was open for 34% -> 36% of each run, Pallas kernels for 0% -> 0%
where the time goes in v8:
time: 201 us; the launch traced here: 200 us
  waiting for transfers between devices  83.5 us (42%)
  matrix products  50.7 us (25%)
  starting transfers between devices  31.8 us (16%)
  other arithmetic  22.2 us (11%)
  local copies, waits for them, and re-layouts  10.6 us (5%)
    all_to_all x6, waiting for transfers between devices, send(): lax.all_to_all(buf.reshape(sections, capacity, width), 'attn', split_axis...  70.5 us
    all_to_all x6, starting transfers between devices, send(): lax.all_to_all(buf.reshape(sections, capacity, width), 'attn', split_axis...  26.8 us
    dot_general x1, matrix products, on_device(): jnp.einsum('sh,sd->hd', activation, d_rows, preferred_element_type=f32)  10.7 us
    ppermute x1, waiting for transfers between devices, on_device(): lax.ppermute(jnp.concatenate([patches, grad_out], axis=1), 'exp', half_swap)  7.74 us
    convert_element_type x2, other arithmetic, group_sum(): return lax.optimization_barrier((summed.astype(bf16), hold))  7.63 us
    unnamed x57, local copies, waits for them, and re-layouts  6.96 us
    dot_general x1, matrix products, on_device(): jnp.einsum('sd,sh->dh', x_late, pre_late, preferred_element_type=f32)  6.62 us
    dot_general x1, matrix products, on_device(): jnp.einsum('sd,hd->sh', d_rows, down_mat, preferred_element_type=f32)  6.46 us
  transfers between devices with their start and end apart: 14, of which 10 were waited for; matrix products, arithmetic and copies ran while one was open for 36% of the time, Pallas kernels for 0%

profile of v8, /device:TPU:0, one launch (start us, length us, event | category | flops | bytes accessed | tf_op | source)
XLA Modules:
  0.0 199.9 jit_solution(11489993882321299164)
XLA Ops:
  0.7 1.2 pad_maximum_fusion.6
  1.9 3.0 %collective-permute-start = (bf16[192,2048]{1,0:T(8,128)(2,1)S(1)}, bf16[192,2048]{1,0:T(8,128)(2,1)S(1)}, u32[]{:S(2)}, u32[]{:S(2)}) collective-permute-start(bf16[192,2048]{1,0:T(8,128)(2,1)S(1)} %pad_maximum_fusion.6), channel_id=1, source_target_pairs={{0,2},{1,3},{2,0},{3,1},{4,6},{5,7},{6,4},{7,5},{8,10},{9,11},{10,... | collective-permute-start | bytes 2359304 | tf_op jit(solution)/shard_map/ppermute | solution.py:84
  5.5 0.9 reduce-window.6
  6.4 0.2 slice_reduce_fusion.4
  6.7 0.2 slice_reduce_fusion.3
  7.4 1.4 convolution_convert_fusion
  8.9 5.8 %all-to-all-start = ((bf16[8,48,1024]{2,1,0:T(8,128)(2,1)}), bf16[8,48,1024]{2,1,0:T(8,128)(2,1)S(1)}, u32[]{:S(2)}, u32[]{:S(2)}) async-start(bf16[8,48,1024]{2,1,0:T(8,128)(2,1)} %bitcast.3), calls=%async_computation | async-start | bytes 1572864 | tf_op jit(solution)/shard_map/all_to_all | solution.py:79
  14.7 7.7 %collective-permute-done = bf16[192,2048]{1,0:T(8,128)(2,1)S(1)} collective-permute-done((bf16[192,2048]{1,0:T(8,128)(2,1)S(1)}, bf16[192,2048]{1,0:T(8,128)(2,1)S(1)}, u32[]{:S(2)}, u32[]{:S(2)}) %collective-permute-start) | collective-permute-done | bytes 786464 | tf_op jit(solution)/shard_map/ppermute | solution.py:84
  22.6 1.4 convolution_convert_fusion.1
  24.0 10.6 %all-to-all-done = bf16[8,48,1024]{2,1,0:T(8,128)(2,1)S(1)} async-done(((bf16[8,48,1024]{2,1,0:T(8,128)(2,1)}), bf16[8,48,1024]{2,1,0:T(8,128)(2,1)S(1)}, u32[]{:S(2)}, u32[]{:S(2)}) %all-to-all-start) | async-done | bytes 786464 | tf_op jit(solution)/shard_map/all_to_all | solution.py:79
  34.7 3.5 %all-to-all-start.1 = ((bf16[8,48,1024]{2,1,0:T(8,128)(2,1)}), bf16[8,48,1024]{2,1,0:T(8,128)(2,1)S(1)}, u32[]{:S(2)}, u32[]{:S(2)}) async-start(bf16[8,48,1024]{2,1,0:T(8,128)(2,1)} %bitcast.5), calls=%async_computation.1 | async-start | bytes 1572864 | tf_op jit(solution)/shard_map/all_to_all | solution.py:79
  38.3 20.2 %all-to-all-done.1 = bf16[8,48,1024]{2,1,0:T(8,128)(2,1)S(1)} async-done(((bf16[8,48,1024]{2,1,0:T(8,128)(2,1)}), bf16[8,48,1024]{2,1,0:T(8,128)(2,1)S(1)}, u32[]{:S(2)}, u32[]{:S(2)}) %all-to-all-start.1) | async-done | bytes 786464 | tf_op jit(solution)/shard_map/all_to_all | solution.py:79
  58.5 0.2 select_reduce_fusion
  58.8 1.9 multiply_convert_fusion
  60.7 0.2 collective-permute-done.2
  60.9 1.4 broadcast_select_fusion.11
  62.3 0.3 pad_maximum_fusion
  62.6 4.3 %all-to-all-start.2 = ((bf16[8,48,2048]{2,1,0:T(8,128)(2,1)}), bf16[8,48,2048]{2,1,0:T(8,128)(2,1)}, u32[]{:S(2)}, u32[]{:S(2)}) async-start(bf16[8,48,2048]{2,1,0:T(8,128)(2,1)} %bitcast.83), calls=%async_computation.2 | async-start | bytes 3145728 | tf_op jit(solution)/shard_map/all_to_all | solution.py:79
  66.9 5.4 %fusion.6 = f32[384,768]{1,0:T(8,128)S(1)} fusion(bf16[384,4096]{1,0:T(8,128)(2,1)S(1)} %pad_maximum_fusion, bf16[1,4096,768]{2,1,0:T(8,128)(2,1)} %param.10), kind=kOutput, calls=%fused_computation.6 | convolution fusion | flops 2415919104 | bytes 10616832 | tf_op jit(solution)/shard_map/dot_general | solution.py:114
  72.3 1.0 copy-done.20
  73.4 4.9 %fusion.17 = f32[384,4096]{1,0:T(8,128)S(1)} fusion(bf16[1,768,4096]{2,1,0:T(8,128)(2,1)} %param.11, f32[384,768]{1,0:T(8,128)S(1)} %fusion.6), kind=kOutput, calls=%fused_computation.11 | convolution fusion | flops 2421719040 | bytes 13762560 | tf_op jit(solution)/shard_map/dot_general | solution.py:121
  78.3 1.1 fusion.62
  79.4 1.9 select_convert_fusion.1
  81.3 0.2 copy-done.11
  81.5 0.5 copy-done.12
  82.1 0.6 copy-done.13
  82.7 0.3 collective-permute-start.3
  82.9 3.5 %collective-permute-done.3 = bf16[384,2048]{1,0:T(8,128)(2,1)} collective-permute-done((bf16[384,2048]{1,0:T(8,128)(2,1)}, bf16[384,2048]{1,0:T(8,128)(2,1)}, u32[]{:S(2)}, u32[]{:S(2)}) %collective-permute-start.3) | collective-permute-done | bytes 1572896 | tf_op jit(solution)/shard_map/ppermute | solution.py:136
  86.4 5.3 %add_convert_fusion.1 = bf16[384,2048]{1,0:T(8,128)(2,1)} fusion(bf16[384,2048]{1,0:T(8,128)(2,1)} %collective-permute-done.3, f32[384,1024]{1,0:T(8,128)} %copy-done.11, f32[384,1024]{1,0:T(8,128)} %copy-done.12, f32[384,1024]{1,0:T(8,128)} %copy-done.13, f32[384,1024]{1,0:T(8,128)} %copy-done.10, pred[]{:T(512)S(6)} %eq.128), kind=kLoop, calls=%fused_computation.20 | loop fusion | flops 4718592 | bytes 9437185 | tf_op jit(solution)/shard_map/convert_element_type | solution.py:138
  91.7 12.9 %all-to-all-done.2 = bf16[8,48,2048]{2,1,0:T(8,128)(2,1)} async-done(((bf16[8,48,2048]{2,1,0:T(8,128)(2,1)}), bf16[8,48,2048]{2,1,0:T(8,128)(2,1)}, u32[]{:S(2)}, u32[]{:S(2)}) %all-to-all-start.2) | async-done | bytes 1572896 | tf_op jit(solution)/shard_map/all_to_all | solution.py:79
  104.7 4.5 %all-to-all-start.3 = ((bf16[8,48,2048]{2,1,0:T(8,128)(2,1)}), bf16[8,48,2048]{2,1,0:T(8,128)(2,1)}, u32[]{:S(2)}, u32[]{:S(2)}) async-start(bf16[8,48,2048]{2,1,0:T(8,128)(2,1)} %bitcast.78), calls=%async_computation.3 | async-start | bytes 3145728 | tf_op jit(solution)/shard_map/all_to_all | solution.py:79
  109.2 2.1 %broadcast_select_fusion.1 = (bf16[384,2048]{1,0:T(8,128)(2,1)S(1)}, bf16[384,2048]{1,0:T(8,128)(2,1)S(1)}) fusion(bf16[384,2048]{1,0:T(8,128)(2,1)} %collective-permute-done.5, bf16[384,2048]{1,0:T(8,128)(2,1)} %bitcast.10, pred[]{:T(512)S(6)} %eq.134, pred[]{:T(512)S(6)} %eq.135), kind=kLoop, calls=%fused_computation.29 | loop fusion | flops 1572864 | bytes 6291458 | tf_op jit(solution)/shard_map/jit(_where)/select_n | solution.py:51
  111.6 0.7 copy-done.14
  112.3 0.2 copy-done.15
  112.5 0.2 copy-done.16
  112.8 0.3 copy-done.17
  113.1 0.5 copy-done.21
  113.6 6.5 %fusion.24 = bf16[384,768]{1,0:T(8,128)(2,1)S(1)} fusion(bf16[1,768,4096]{2,1,0:T(8,128)(2,1)} %param.11, f32[384,768]{1,0:T(8,128)S(1)} %copy-done.21, bf16[384,1024]{1,0:T(8,128)(2,1)S(1)} %get-tuple-element.55, bf16[384,1024]{1,0:T(8,128)(2,1)S(1)} %get-tuple-element.53, bf16[384,1024]{1,0:T(8,128)(2,1)S(1)} %get-tuple-element.54, ...), kind=kOutput, calls=%fused_computation.33 | convolution fusion | flops 2434105344 | bytes 11206656 | tf_op jit(solution)/shard_map/sd,hd->sh/dot_general | solution.py:149
  120.1 2.6 %fusion.11 = f32[384,4096]{1,0:T(8,128)S(1)} fusion(bf16[384,768]{1,0:T(8,128)(2,1)S(1)} %fusion.24, bf16[1,4096,768]{2,1,0:T(8,128)(2,1)S(1)} %bitcast.90), kind=kOutput, calls=%fused_computation.9 | convolution fusion | flops 2419064832 | bytes 13172736 | tf_op jit(solution)/shard_map/sh,dh->sd/dot_general | solution.py:154
  122.8 1.1 fusion.61
  123.9 1.9 select_convert_fusion
  125.8 0.3 copy-done.2
  126.0 0.5 copy-done.4
  126.6 0.5 copy-done.6
  127.0 0.5 collective-permute-start.6
  127.6 10.7 %fusion.33 = f32[768,4096]{1,0:T(8,128)} fusion(bf16[384,1024]{1,0:T(8,128)(2,1)} %copy-done.17, bf16[384,1024]{1,0:T(8,128)(2,1)} %copy-done.15, bf16[384,1024]{1,0:T(8,128)(2,1)} %copy-done.16, bf16[384,1024]{1,0:T(8,128)(2,1)} %copy-done.14, f32[384,768]{1,0:T(8,128)} %copy-done.20), kind=kOutput, calls=%fused_computation.56 | convolution fusion | flops 2431156224 | bytes 16908288 | tf_op jit(solution)/shard_map/sh,sd->hd/dot_general | solution.py:157
  138.3 2.3 %add_convert_fusion = bf16[384,2048]{1,0:T(8,128)(2,1)S(1)} fusion(bf16[384,2048]{1,0:T(8,128)(2,1)} %collective-permute-done.6, f32[384,1024]{1,0:T(8,128)S(1)} %copy-done.3, f32[384,1024]{1,0:T(8,128)S(1)} %copy-done.5, f32[384,1024]{1,0:T(8,128)S(1)} %copy-done.7, f32[384,1024]{1,0:T(8,128)S(1)} %copy-done.1, pred[]{:T(512)S(6)} %eq.128), kind=kLoop, calls=%fused_computation.18 | loop fusion | flops 4718592 | bytes 9437185 | tf_op jit(solution)/shard_map/convert_element_type | solution.py:138
  140.6 1.3 broadcast_select_fusion.3
  141.9 5.0 %all-to-all-done.3 = bf16[8,48,2048]{2,1,0:T(8,128)(2,1)} async-done(((bf16[8,48,2048]{2,1,0:T(8,128)(2,1)}), bf16[8,48,2048]{2,1,0:T(8,128)(2,1)}, u32[]{:S(2)}, u32[]{:S(2)}) %all-to-all-start.3) | async-done | bytes 1572896 | tf_op jit(solution)/shard_map/all_to_all | solution.py:79
  146.9 4.2 %all-to-all-start.5 = ((bf16[8,48,1024]{2,1,0:T(8,128)(2,1)}), bf16[8,48,1024]{2,1,0:T(8,128)(2,1)}, u32[]{:S(2)}, u32[]{:S(2)}) async-start(bf16[8,48,1024]{2,1,0:T(8,128)(2,1)} %bitcast.80), calls=%async_computation.5 | async-start | bytes 1572864 | tf_op jit(solution)/shard_map/all_to_all | solution.py:79
  151.2 2.0 %convolution_multiply_fusion.1 = f32[192,2048]{1,0:T(8,128)S(1)} fusion(bf16[384,2048]{1,0:T(8,128)(2,1)} %bitcast.12, f32[192]{0:T(256)S(1)} %bitcast.87, s32[192]{0:T(256)S(1)} %get-tuple-element.32, pred[192]{0:T(512)(128)(4,1)S(1)} %get-tuple-element.34), kind=kOutput, calls=%fused_computation.25 | convolution fusion | flops 302530560 | bytes 3147456 | tf_op jit(solution)/shard_map/dot_general | solution.py:171
  153.2 2.0 %fusion.20 = f32[192,2048]{1,0:T(8,128)S(1)} fusion(f32[192,2048]{1,0:T(8,128)S(1)} %convolution_multiply_fusion.1, bf16[384,2048]{1,0:T(8,128)(2,1)} %bitcast.12, f32[192]{0:T(256)S(1)} %bitcast.85, s32[192]{0:T(256)S(1)} %get-tuple-element.33, pred[192]{0:T(512)(128)(4,1)S(1)} %get-tuple-element.35), kind=kOutput, calls=%fused_computation.24 | convolution fusion | flops 302923776 | bytes 4720320 | tf_op jit(solution)/shard_map/dot_general | solution.py:171
  155.3 1.1 copy-done.8
  156.4 1.0 slice_select_fusion
  157.4 0.5 collective-permute-start.4
  158.0 13.6 %all-to-all-done.5 = bf16[8,48,1024]{2,1,0:T(8,128)(2,1)} async-done(((bf16[8,48,1024]{2,1,0:T(8,128)(2,1)}), bf16[8,48,1024]{2,1,0:T(8,128)(2,1)}, u32[]{:S(2)}, u32[]{:S(2)}) %all-to-all-start.5) | async-done | bytes 786464 | tf_op jit(solution)/shard_map/all_to_all | solution.py:79
  171.5 4.4 %all-to-all-start.4 = ((bf16[8,48,1024]{2,1,0:T(8,128)(2,1)}), bf16[8,48,1024]{2,1,0:T(8,128)(2,1)}, u32[]{:S(2)}, u32[]{:S(2)}) async-start(bf16[8,48,1024]{2,1,0:T(8,128)(2,1)} %bitcast.79), calls=%async_computation.4 | async-start | bytes 1572864 | tf_op jit(solution)/shard_map/all_to_all | solution.py:79
  176.0 2.6 %fusion.56 = f32[192,1024]{1,0:T(8,128)} fusion(bf16[384,1024]{1,0:T(8,128)(2,1)} %bitcast.16, s32[192]{0:T(256)S(1)} %get-tuple-element.33, s32[192]{0:T(256)S(1)} %get-tuple-element.32, pred[192]{0:T(512)(128)(4,1)S(1)} %get-tuple-element.35, pred[192]{0:T(512)(128)(4,1)S(1)} %get-tuple-element.34), kind=kOutput, calls=%fused_computation.98 | convolution fusion | flops 151363584 | bytes 1574784 | tf_op jit(solution)/shard_map/dot_general | solution.py:161
  178.6 0.5 collective-permute-start.7
  179.1 2.0 %add_convert_fusion.2 = bf16[192,1024]{1,0:T(8,128)(2,1)} fusion(f32[192,1024]{1,0:T(8,128)} %collective-permute-done.4, f32[192,2048]{1,0:T(8,128)S(1)} %copy-done.9, pred[]{:T(512)S(6)} %eq.113), kind=kLoop, calls=%fused_computation.44 | loop fusion | flops 589824 | bytes 2752513 | tf_op jit(solution)/shard_map/convert_element_type | solution.py:144
  181.1 6.6 %fusion.66 = f32[4096,768]{1,0:T(8,128)} fusion(bf16[384,4096]{1,0:T(8,128)(2,1)S(1)} %pad_maximum_fusion, bf16[384,768]{1,0:T(8,128)(2,1)S(1)} %copy-done.23), kind=kOutput, calls=%fused_computation.104 | convolution fusion | flops 2415919104 | bytes 16318464 | tf_op jit(solution)/shard_map/sd,sh->dh/dot_general | solution.py:165
  187.8 8.0 %all-to-all-done.4 = bf16[8,48,1024]{2,1,0:T(8,128)(2,1)} async-done(((bf16[8,48,1024]{2,1,0:T(8,128)(2,1)}), bf16[8,48,1024]{2,1,0:T(8,128)(2,1)}, u32[]{:S(2)}, u32[]{:S(2)}) %all-to-all-start.4) | async-done | bytes 786464 | tf_op jit(solution)/shard_map/all_to_all | solution.py:79
  195.8 1.6 collective-permute-done.7
  197.4 2.6 %fusion.27 = bf16[192,1024]{1,0:T(8,128)(2,1)} fusion(f32[192,1024]{1,0:T(8,128)} %collective-permute-done.7, bf16[384,1024]{1,0:T(8,128)(2,1)} %bitcast.14, s32[192]{0:T(256)S(1)} %get-tuple-element.33, s32[192]{0:T(256)S(1)} %get-tuple-element.32, pred[192]{0:T(512)(128)(4,1)S(1)} %get-tuple-element.35, pred[192]{0:T(512)(128)(4,1)S(1)} %get-tuple-element.34), kind=kOutput, calls=%fused_computation.35 | convolution fusion | flops 151756800 | bytes 1968000 | tf_op jit(solution)/shard_map/dot_general | solution.py:167
  (69 shorter events, 1.7 us)
Async XLA Ops:
  0.6 6.8 %copy-start.18 = (bf16[192,1024]{1,0:T(8,128)(2,1)S(1)}, bf16[192,1024]{1,0:T(8,128)(2,1)}, u32[]{:S(2)}) copy-start(bf16[192,1024]{1,0:T(8,128)(2,1)} %param.6) | copy-start | bytes 1179652
  0.6 4.2 %copy-start.24 = (s32[192,2]{0,1:T(2,128)S(1)}, s32[192,2]{0,1:T(2,128)}, u32[]{:S(2)}) copy-start(s32[192,2]{0,1:T(2,128)} %param.8) | copy-start | bytes 4612
  1.9 20.5 %collective-permute-start = (bf16[192,2048]{1,0:T(8,128)(2,1)S(1)}, bf16[192,2048]{1,0:T(8,128)(2,1)S(1)}, u32[]{:S(2)}, u32[]{:S(2)}) collective-permute-start(bf16[192,2048]{1,0:T(8,128)(2,1)S(1)} %pad_maximum_fusion.6), channel_id=1, source_target_pairs={{0,2},{1,3},{2,0},{3,1},{4,6},{5,7},{6,4},{7,5},{8,10},{9,11},{10,... | collective-permute-start | bytes 2359304 | tf_op jit(solution)/shard_map/ppermute | solution.py:84
  7.1 15.3 %copy-start.19 = (bf16[192,1024]{1,0:T(8,128)(2,1)S(1)}, bf16[192,1024]{1,0:T(8,128)(2,1)}, u32[]{:S(2)}) copy-start(bf16[192,1024]{1,0:T(8,128)(2,1)} %param.7) | copy-start | bytes 1179652
  8.9 25.8 %all-to-all-start = ((bf16[8,48,1024]{2,1,0:T(8,128)(2,1)}), bf16[8,48,1024]{2,1,0:T(8,128)(2,1)S(1)}, u32[]{:S(2)}, u32[]{:S(2)}) async-start(bf16[8,48,1024]{2,1,0:T(8,128)(2,1)} %bitcast.3), calls=%async_computation | async-start | bytes 1572864 | tf_op jit(solution)/shard_map/all_to_all | solution.py:79
  22.6 36.0 %copy-start.25 = (f32[192,2]{0,1:T(2,128)S(1)}, f32[192,2]{0,1:T(2,128)}, u32[]{:S(2)}) copy-start(f32[192,2]{0,1:T(2,128)} %param.9) | copy-start | bytes 4612
  34.7 23.9 %all-to-all-start.1 = ((bf16[8,48,1024]{2,1,0:T(8,128)(2,1)}), bf16[8,48,1024]{2,1,0:T(8,128)(2,1)S(1)}, u32[]{:S(2)}, u32[]{:S(2)}) async-start(bf16[8,48,1024]{2,1,0:T(8,128)(2,1)} %bitcast.5), calls=%async_computation.1 | async-start | bytes 1572864 | tf_op jit(solution)/shard_map/all_to_all | solution.py:79
  38.2 22.5 %collective-permute-start.1 = (bf16[384,1024]{1,0:T(8,128)(2,1)S(1)}, bf16[384,1024]{1,0:T(8,128)(2,1)S(1)}, u32[]{:S(2)}, u32[]{:S(2)}) collective-permute-start(bf16[384,1024]{1,0:T(8,128)(2,1)S(1)} %bitcast.81), channel_id=1, source_target_pairs={{0,1},{1,0},{2,3},{3,2},{4,5},{5,4},{6,7},{7,6},{8,9},{9,8},{10,11... | collective-permute-start | bytes 2359304 | tf_op jit(solution)/shard_map/ppermute | solution.py:95
  58.5 2.4 %collective-permute-start.2 = (bf16[384,1024]{1,0:T(8,128)(2,1)S(1)}, bf16[384,1024]{1,0:T(8,128)(2,1)}, u32[]{:S(2)}, u32[]{:S(2)}) collective-permute-start(bf16[384,1024]{1,0:T(8,128)(2,1)S(1)} %bitcast.82), channel_id=1, source_target_pairs={{0,1},{1,0},{2,3},{3,2},{4,5},{5,4},{6,7},{7,6},{8,9},{9,8},{10,11... | collective-permute-start | bytes 2359304 | tf_op jit(solution)/shard_map/ppermute | solution.py:96
  62.6 42.0 %all-to-all-start.2 = ((bf16[8,48,2048]{2,1,0:T(8,128)(2,1)}), bf16[8,48,2048]{2,1,0:T(8,128)(2,1)}, u32[]{:S(2)}, u32[]{:S(2)}) async-start(bf16[8,48,2048]{2,1,0:T(8,128)(2,1)} %bitcast.83), calls=%async_computation.2 | async-start | bytes 3145728 | tf_op jit(solution)/shard_map/all_to_all | solution.py:79
  72.3 1.0 copy-start.20
  79.4 1.9 copy-start.10
  79.4 2.1 %copy-start.11 = (f32[384,1024]{1,0:T(8,128)}, f32[384,1024]{1,0:T(8,128)S(1)}, u32[]{:S(2)}) copy-start(f32[384,1024]{1,0:T(8,128)S(1)} %get-tuple-element.41) | copy-start | bytes 4718596
  79.4 2.6 %copy-start.12 = (f32[384,1024]{1,0:T(8,128)}, f32[384,1024]{1,0:T(8,128)S(1)}, u32[]{:S(2)}) copy-start(f32[384,1024]{1,0:T(8,128)S(1)} %get-tuple-element.42) | copy-start | bytes 4718596
  79.4 3.2 %copy-start.13 = (f32[384,1024]{1,0:T(8,128)}, f32[384,1024]{1,0:T(8,128)S(1)}, u32[]{:S(2)}) copy-start(f32[384,1024]{1,0:T(8,128)S(1)} %get-tuple-element.43) | copy-start | bytes 4718596
  82.7 3.8 %collective-permute-start.3 = (bf16[384,2048]{1,0:T(8,128)(2,1)}, bf16[384,2048]{1,0:T(8,128)(2,1)}, u32[]{:S(2)}, u32[]{:S(2)}) collective-permute-start(bf16[384,2048]{1,0:T(8,128)(2,1)} %select_convert_fusion.1), channel_id=1, source_target_pairs={{0,1},{1,0},{2,3},{3,2},{4,5},{5,4},{6,7},{7,6},{8,9},{9,8},{10,11... | collective-permute-start | bytes 4718600 | tf_op jit(solution)/shard_map/ppermute | solution.py:136
  104.7 4.5 %collective-permute-start.5 = (bf16[384,2048]{1,0:T(8,128)(2,1)}, bf16[384,2048]{1,0:T(8,128)(2,1)}, u32[]{:S(2)}, u32[]{:S(2)}) collective-permute-start(bf16[384,2048]{1,0:T(8,128)(2,1)} %bitcast.10), channel_id=1, source_target_pairs={{0,1},{1,0},{2,3},{3,2},{4,5},{5,4},{6,7},{7,6},{8,9},{9,8},{10,11... | collective-permute-start | bytes 4718600 | tf_op jit(solution)/shard_map/ppermute | solution.py:55
  104.7 42.3 %all-to-all-start.3 = ((bf16[8,48,2048]{2,1,0:T(8,128)(2,1)}), bf16[8,48,2048]{2,1,0:T(8,128)(2,1)}, u32[]{:S(2)}, u32[]{:S(2)}) async-start(bf16[8,48,2048]{2,1,0:T(8,128)(2,1)} %bitcast.78), calls=%async_computation.3 | async-start | bytes 3145728 | tf_op jit(solution)/shard_map/all_to_all | solution.py:79
  111.4 0.9 copy-start.14
  111.4 1.1 copy-start.15
  111.4 2.2 %copy-start.21 = (f32[384,768]{1,0:T(8,128)S(1)}, f32[384,768]{1,0:T(8,128)}, u32[]{:S(2)}) copy-start(f32[384,768]{1,0:T(8,128)} %copy-done.20) | copy-start | bytes 3538948
  111.4 8.6 %slice-start = ((s8[6291456]{0:T(1024)(128)(4,1)}), s8[4194304]{0:T(1024)(128)(4,1)S(1)}, s32[]{:S(2)}) async-start(s8[6291456]{0:T(1024)(128)(4,1)} %bitcast.89), calls=%async_computation.6 | async-start | bytes 8388608
  111.6 1.2 copy-start.16
  111.6 1.5 copy-start.17
  113.6 6.5 %slice-start.1 = ((s8[6291456]{0:T(1024)(128)(4,1)}), s8[2097152]{0:T(1024)(128)(4,1)S(1)}, s32[]{:S(2)}) async-start(s8[6291456]{0:T(1024)(128)(4,1)} %bitcast.89), calls=%async_computation.7 | async-start | bytes 4194304
  120.1 2.7 %copy-start.22 = (bf16[384,768]{1,0:T(8,128)(2,1)}, bf16[384,768]{1,0:T(8,128)(2,1)S(1)}, u32[]{:S(2)}) copy-start(bf16[384,768]{1,0:T(8,128)(2,1)S(1)} %fusion.24) | copy-start | bytes 1769476
  123.9 1.9 copy-start
  123.9 2.2 %copy-start.2 = (f32[384,1024]{1,0:T(8,128)}, f32[384,1024]{1,0:T(8,128)S(1)}, u32[]{:S(2)}) copy-start(f32[384,1024]{1,0:T(8,128)S(1)} %get-tuple-element.37) | copy-start | bytes 4718596
  123.9 2.7 %copy-start.4 = (f32[384,1024]{1,0:T(8,128)}, f32[384,1024]{1,0:T(8,128)S(1)}, u32[]{:S(2)}) copy-start(f32[384,1024]{1,0:T(8,128)S(1)} %get-tuple-element.38) | copy-start | bytes 4718596
  123.9 3.1 %copy-start.6 = (f32[384,1024]{1,0:T(8,128)}, f32[384,1024]{1,0:T(8,128)S(1)}, u32[]{:S(2)}) copy-start(f32[384,1024]{1,0:T(8,128)S(1)} %get-tuple-element.39) | copy-start | bytes 4718596
  127.0 11.2 %collective-permute-start.6 = (bf16[384,2048]{1,0:T(8,128)(2,1)}, bf16[384,2048]{1,0:T(8,128)(2,1)}, u32[]{:S(2)}, u32[]{:S(2)}) collective-permute-start(bf16[384,2048]{1,0:T(8,128)(2,1)} %select_convert_fusion), channel_id=1, source_target_pairs={{0,1},{1,0},{2,3},{3,2},{4,5},{5,4},{6,7},{7,6},{8,9},{9,8},{10,11... | collective-permute-start | bytes 4718600 | tf_op jit(solution)/shard_map/ppermute | solution.py:136
  127.5 10.7 %copy-start.1 = (f32[384,1024]{1,0:T(8,128)S(1)}, f32[384,1024]{1,0:T(8,128)}, u32[]{:S(2)}) copy-start(f32[384,1024]{1,0:T(8,128)} %copy-done) | copy-start | bytes 4718596
  127.6 10.7 %copy-start.3 = (f32[384,1024]{1,0:T(8,128)S(1)}, f32[384,1024]{1,0:T(8,128)}, u32[]{:S(2)}) copy-start(f32[384,1024]{1,0:T(8,128)} %copy-done.2) | copy-start | bytes 4718596
  127.6 10.7 %copy-start.5 = (f32[384,1024]{1,0:T(8,128)S(1)}, f32[384,1024]{1,0:T(8,128)}, u32[]{:S(2)}) copy-start(f32[384,1024]{1,0:T(8,128)} %copy-done.4) | copy-start | bytes 4718596
  127.6 10.7 %copy-start.7 = (f32[384,1024]{1,0:T(8,128)S(1)}, f32[384,1024]{1,0:T(8,128)}, u32[]{:S(2)}) copy-start(f32[384,1024]{1,0:T(8,128)} %copy-done.6) | copy-start | bytes 4718596
  146.9 24.6 %all-to-all-start.5 = ((bf16[8,48,1024]{2,1,0:T(8,128)(2,1)}), bf16[8,48,1024]{2,1,0:T(8,128)(2,1)}, u32[]{:S(2)}, u32[]{:S(2)}) async-start(bf16[8,48,1024]{2,1,0:T(8,128)(2,1)} %bitcast.80), calls=%async_computation.5 | async-start | bytes 1572864 | tf_op jit(solution)/shard_map/all_to_all | solution.py:79
  155.3 1.1 copy-start.8
  157.4 21.7 %collective-permute-start.4 = (f32[192,1024]{1,0:T(8,128)}, f32[192,1024]{1,0:T(8,128)}, u32[]{:S(2)}, u32[]{:S(2)}) collective-permute-start(f32[192,1024]{1,0:T(8,128)} %slice_select_fusion), channel_id=1, source_target_pairs={{0,2},{1,3},{2,0},{3,1},{4,6},{5,7},{6,4},{7,5},{8,10},{9,11},{10,... | collective-permute-start | bytes 2359304 | tf_op jit(solution)/shard_map/ppermute | solution.py:144
  171.5 24.3 %all-to-all-start.4 = ((bf16[8,48,1024]{2,1,0:T(8,128)(2,1)}), bf16[8,48,1024]{2,1,0:T(8,128)(2,1)}, u32[]{:S(2)}, u32[]{:S(2)}) async-start(bf16[8,48,1024]{2,1,0:T(8,128)(2,1)} %bitcast.79), calls=%async_computation.4 | async-start | bytes 1572864 | tf_op jit(solution)/shard_map/all_to_all | solution.py:79
  176.0 3.1 %copy-start.9 = (f32[192,2048]{1,0:T(8,128)S(1)}, f32[192,2048]{1,0:T(8,128)}, u32[]{:S(2)}) copy-start(f32[192,2048]{1,0:T(8,128)} %copy-done.8) | copy-start | bytes 4718596
  178.6 2.6 %copy-start.23 = (bf16[384,768]{1,0:T(8,128)(2,1)S(1)}, bf16[384,768]{1,0:T(8,128)(2,1)}, u32[]{:S(2)}) copy-start(bf16[384,768]{1,0:T(8,128)(2,1)} %copy-done.22) | copy-start | bytes 1769476
  178.6 18.8 %collective-permute-start.7 = (f32[192,1024]{1,0:T(8,128)}, f32[192,1024]{1,0:T(8,128)}, u32[]{:S(2)}, u32[]{:S(2)}) collective-permute-start(f32[192,1024]{1,0:T(8,128)} %fusion.56), channel_id=1, source_target_pairs={{0,2},{1,3},{2,0},{3,1},{4,6},{5,7},{6,4},{7,5},{8,10},{9,11},{10,... | collective-permute-start | bytes 2359304 | tf_op jit(solution)/shard_map/ppermute | solution.py:162

commit v9 on v8

--- a/solution.py
+++ b/solution.py
@@ -88,10 +88,10 @@
     sub_dy = jnp.concatenate(
         [jnp.where(half == 0, grad_out, dy_other), jnp.where(half == 0, dy_other, grad_out)], axis=1
     )
-    sub_dy, other_buf = lax.optimization_barrier((sub_dy, other_buf))
-    got_other = send(other_buf)
     dy_buf = jnp.dot(dispatch_mat, sub_dy, preferred_element_type=f32)
     d_buf = (gate_slot[:, None] * dy_buf).astype(bf16)
+    d_buf, other_buf = lax.optimization_barrier((d_buf, other_buf))
+    got_other = send(other_buf)
     own_all = [got_own] + [lax.ppermute(got_own, "exp", core_shift(s)) for s in range(1, cores)]
     other_all = [got_other] + [lax.ppermute(got_other, "exp", core_shift(s)) for s in range(1, cores)]
     x_pieces = []

time: 201 us -> 200 us (level)
    ppermute x1, waiting for transfers between devices: 0.24 us -> 2.28 us  [on_device(): lax.ppermute(got_other, 'exp', core_shift(s))]
where the time goes in v9:
time: 200 us; the launch traced here: 199 us
  waiting for transfers between devices  83.4 us (42%)
  matrix products  50.7 us (25%)
  starting transfers between devices  31.8 us (16%)
  other arithmetic  21.1 us (11%)
  local copies, waits for them, and re-layouts  10.7 us (5%)
    all_to_all x6, waiting for transfers between devices, send(): lax.all_to_all(buf.reshape(sections, capacity, width), 'attn', split_axis...  68.7 us
    all_to_all x6, starting transfers between devices, send(): lax.all_to_all(buf.reshape(sections, capacity, width), 'attn', split_axis...  27 us
    dot_general x1, matrix products, on_device(): jnp.einsum('sh,sd->hd', activation, d_rows, preferred_element_type=f32)  10.7 us
    convert_element_type x2, other arithmetic, group_sum(): return lax.optimization_barrier((summed.astype(bf16), hold))  7.63 us
    ppermute x1, waiting for transfers between devices, on_device(): lax.ppermute(jnp.concatenate([patches, grad_out], axis=1), 'exp', half_swap)  7.27 us
    unnamed x57, local copies, waits for them, and re-layouts  6.96 us
    dot_general x1, matrix products, on_device(): jnp.einsum('sd,sh->dh', x_late, pre_late, preferred_element_type=f32)  6.62 us
    dot_general x1, matrix products, on_device(): jnp.einsum('sd,hd->sh', d_rows, down_mat, preferred_element_type=f32)  6.46 us
  transfers between devices with their start and end apart: 14, of which 10 were waited for; matrix products, arithmetic and copies ran while one was open for 36% of the time, Pallas kernels for 0%

profile of v9, /device:TPU:0, one launch (start us, length us, event | category | flops | bytes accessed | tf_op | source)
XLA Modules:
  0.0 198.8 jit_solution(506708035016621312)
XLA Ops:
  0.7 1.2 pad_maximum_fusion.6
  1.9 3.0 %collective-permute-start = (bf16[192,2048]{1,0:T(8,128)(2,1)S(1)}, bf16[192,2048]{1,0:T(8,128)(2,1)S(1)}, u32[]{:S(2)}, u32[]{:S(2)}) collective-permute-start(bf16[192,2048]{1,0:T(8,128)(2,1)S(1)} %pad_maximum_fusion.6), channel_id=1, source_target_pairs={{0,2},{1,3},{2,0},{3,1},{4,6},{5,7},{6,4},{7,5},{8,10},{9,11},{10,... | collective-permute-start | bytes 2359304 | tf_op jit(solution)/shard_map/ppermute | solution.py:84
  5.5 0.9 reduce-window.6
  6.4 0.2 slice_reduce_fusion.4
  6.7 0.2 slice_reduce_fusion.2
  7.2 0.2 slice_reduce_fusion
  7.5 1.4 convolution_convert_fusion
  8.9 6.0 %all-to-all-start = ((bf16[8,48,1024]{2,1,0:T(8,128)(2,1)}), bf16[8,48,1024]{2,1,0:T(8,128)(2,1)S(1)}, u32[]{:S(2)}, u32[]{:S(2)}) async-start(bf16[8,48,1024]{2,1,0:T(8,128)(2,1)} %bitcast.3), calls=%async_computation | async-start | bytes 1572864 | tf_op jit(solution)/shard_map/all_to_all | solution.py:79
  14.9 0.2 select_reduce_fusion
  15.2 7.3 %collective-permute-done = bf16[192,2048]{1,0:T(8,128)(2,1)S(1)} collective-permute-done((bf16[192,2048]{1,0:T(8,128)(2,1)S(1)}, bf16[192,2048]{1,0:T(8,128)(2,1)S(1)}, u32[]{:S(2)}, u32[]{:S(2)}) %collective-permute-start) | collective-permute-done | bytes 786464 | tf_op jit(solution)/shard_map/ppermute | solution.py:84
  22.4 1.4 convolution_convert_fusion.1
  23.9 1.9 multiply_convert_fusion
  25.8 9.0 %all-to-all-done = bf16[8,48,1024]{2,1,0:T(8,128)(2,1)S(1)} async-done(((bf16[8,48,1024]{2,1,0:T(8,128)(2,1)}), bf16[8,48,1024]{2,1,0:T(8,128)(2,1)S(1)}, u32[]{:S(2)}, u32[]{:S(2)}) %all-to-all-start) | async-done | bytes 786464 | tf_op jit(solution)/shard_map/all_to_all | solution.py:79
  34.8 3.5 %all-to-all-start.1 = ((bf16[8,48,1024]{2,1,0:T(8,128)(2,1)}), bf16[8,48,1024]{2,1,0:T(8,128)(2,1)S(1)}, u32[]{:S(2)}, u32[]{:S(2)}) async-start(bf16[8,48,1024]{2,1,0:T(8,128)(2,1)} %bitcast.5), calls=%async_computation.1 | async-start | bytes 1572864 | tf_op jit(solution)/shard_map/all_to_all | solution.py:79
  38.5 20.2 %all-to-all-done.1 = bf16[8,48,1024]{2,1,0:T(8,128)(2,1)S(1)} async-done(((bf16[8,48,1024]{2,1,0:T(8,128)(2,1)}), bf16[8,48,1024]{2,1,0:T(8,128)(2,1)S(1)}, u32[]{:S(2)}, u32[]{:S(2)}) %all-to-all-start.1) | async-done | bytes 786464 | tf_op jit(solution)/shard_map/all_to_all | solution.py:79
  58.7 2.3 %collective-permute-done.2 = bf16[384,1024]{1,0:T(8,128)(2,1)S(1)} collective-permute-done((bf16[384,1024]{1,0:T(8,128)(2,1)S(1)}, bf16[384,1024]{1,0:T(8,128)(2,1)S(1)}, u32[]{:S(2)}, u32[]{:S(2)}) %collective-permute-start.2) | collective-permute-done | bytes 786464 | tf_op jit(solution)/shard_map/ppermute | solution.py:96
  61.0 0.4 broadcast_select_fusion.11
  61.4 0.3 pad_maximum_fusion
  61.7 4.3 %all-to-all-start.2 = ((bf16[8,48,2048]{2,1,0:T(8,128)(2,1)}), bf16[8,48,2048]{2,1,0:T(8,128)(2,1)}, u32[]{:S(2)}, u32[]{:S(2)}) async-start(bf16[8,48,2048]{2,1,0:T(8,128)(2,1)} %bitcast.82), calls=%async_computation.2 | async-start | bytes 3145728 | tf_op jit(solution)/shard_map/all_to_all | solution.py:79
  66.0 5.4 %fusion.6 = f32[384,768]{1,0:T(8,128)S(1)} fusion(bf16[384,4096]{1,0:T(8,128)(2,1)S(1)} %pad_maximum_fusion, bf16[1,4096,768]{2,1,0:T(8,128)(2,1)} %param.10), kind=kOutput, calls=%fused_computation.6 | convolution fusion | flops 2415919104 | bytes 10616832 | tf_op jit(solution)/shard_map/dot_general | solution.py:114
  71.4 1.0 copy-done.20
  72.4 4.9 %fusion.17 = f32[384,4096]{1,0:T(8,128)S(1)} fusion(bf16[1,768,4096]{2,1,0:T(8,128)(2,1)} %param.11, f32[384,768]{1,0:T(8,128)S(1)} %fusion.6), kind=kOutput, calls=%fused_computation.11 | convolution fusion | flops 2421719040 | bytes 13762560 | tf_op jit(solution)/shard_map/dot_general | solution.py:121
  77.3 1.1 fusion.66
  78.5 1.9 select_convert_fusion.1
  80.4 0.2 copy-done.11
  80.6 0.5 copy-done.12
  81.1 0.6 copy-done.13
  81.8 3.6 %collective-permute-done.3 = bf16[384,2048]{1,0:T(8,128)(2,1)} collective-permute-done((bf16[384,2048]{1,0:T(8,128)(2,1)}, bf16[384,2048]{1,0:T(8,128)(2,1)}, u32[]{:S(2)}, u32[]{:S(2)}) %collective-permute-start.3) | collective-permute-done | bytes 1572896 | tf_op jit(solution)/shard_map/ppermute | solution.py:136
  85.4 5.3 %add_convert_fusion.1 = bf16[384,2048]{1,0:T(8,128)(2,1)} fusion(bf16[384,2048]{1,0:T(8,128)(2,1)} %collective-permute-done.3, f32[384,1024]{1,0:T(8,128)} %copy-done.11, f32[384,1024]{1,0:T(8,128)} %copy-done.12, f32[384,1024]{1,0:T(8,128)} %copy-done.13, f32[384,1024]{1,0:T(8,128)} %copy-done.10, pred[]{:T(512)S(6)} %eq.128), kind=kLoop, calls=%fused_computation.20 | loop fusion | flops 4718592 | bytes 9437185 | tf_op jit(solution)/shard_map/convert_element_type | solution.py:138
  90.8 12.8 %all-to-all-done.2 = bf16[8,48,2048]{2,1,0:T(8,128)(2,1)} async-done(((bf16[8,48,2048]{2,1,0:T(8,128)(2,1)}), bf16[8,48,2048]{2,1,0:T(8,128)(2,1)}, u32[]{:S(2)}, u32[]{:S(2)}) %all-to-all-start.2) | async-done | bytes 1572896 | tf_op jit(solution)/shard_map/all_to_all | solution.py:79
  103.6 4.5 %all-to-all-start.3 = ((bf16[8,48,2048]{2,1,0:T(8,128)(2,1)}), bf16[8,48,2048]{2,1,0:T(8,128)(2,1)}, u32[]{:S(2)}, u32[]{:S(2)}) async-start(bf16[8,48,2048]{2,1,0:T(8,128)(2,1)} %bitcast.77), calls=%async_computation.3 | async-start | bytes 3145728 | tf_op jit(solution)/shard_map/all_to_all | solution.py:79
  108.1 2.1 %broadcast_select_fusion.1 = (bf16[384,2048]{1,0:T(8,128)(2,1)S(1)}, bf16[384,2048]{1,0:T(8,128)(2,1)S(1)}) fusion(bf16[384,2048]{1,0:T(8,128)(2,1)} %collective-permute-done.5, bf16[384,2048]{1,0:T(8,128)(2,1)} %bitcast.10, pred[]{:T(512)S(6)} %eq.134, pred[]{:T(512)S(6)} %eq.135), kind=kLoop, calls=%fused_computation.29 | loop fusion | flops 1572864 | bytes 6291458 | tf_op jit(solution)/shard_map/jit(_where)/select_n | solution.py:51
  110.5 0.7 copy-done.14
  111.2 0.2 copy-done.15
  111.4 0.2 copy-done.16
  111.7 0.3 copy-done.17
  112.0 0.5 copy-done.21
  112.5 6.5 %fusion.24 = bf16[384,768]{1,0:T(8,128)(2,1)S(1)} fusion(bf16[1,768,4096]{2,1,0:T(8,128)(2,1)} %param.11, f32[384,768]{1,0:T(8,128)S(1)} %copy-done.21, bf16[384,1024]{1,0:T(8,128)(2,1)S(1)} %get-tuple-element.55, bf16[384,1024]{1,0:T(8,128)(2,1)S(1)} %get-tuple-element.53, bf16[384,1024]{1,0:T(8,128)(2,1)S(1)} %get-tuple-element.54, ...), kind=kOutput, calls=%fused_computation.33 | convolution fusion | flops 2434105344 | bytes 11206656 | tf_op jit(solution)/shard_map/sd,hd->sh/dot_general | solution.py:149
  119.0 2.6 %fusion.11 = f32[384,4096]{1,0:T(8,128)S(1)} fusion(bf16[384,768]{1,0:T(8,128)(2,1)S(1)} %fusion.24, bf16[1,4096,768]{2,1,0:T(8,128)(2,1)S(1)} %bitcast.89), kind=kOutput, calls=%fused_computation.9 | convolution fusion | flops 2419064832 | bytes 13172736 | tf_op jit(solution)/shard_map/sh,dh->sd/dot_general | solution.py:154
  121.6 1.1 fusion.65
  122.8 1.9 select_convert_fusion
  124.7 0.3 copy-done.2
  124.9 0.5 copy-done.4
  125.5 0.5 copy-done.6
  125.9 0.5 collective-permute-start.6
  126.5 10.7 %fusion.36 = f32[768,4096]{1,0:T(8,128)} fusion(bf16[384,1024]{1,0:T(8,128)(2,1)} %copy-done.17, bf16[384,1024]{1,0:T(8,128)(2,1)} %copy-done.15, bf16[384,1024]{1,0:T(8,128)(2,1)} %copy-done.16, bf16[384,1024]{1,0:T(8,128)(2,1)} %copy-done.14, f32[384,768]{1,0:T(8,128)} %copy-done.20), kind=kOutput, calls=%fused_computation.58 | convolution fusion | flops 2431156224 | bytes 16908288 | tf_op jit(solution)/shard_map/sh,sd->hd/dot_general | solution.py:157
  137.2 2.3 %add_convert_fusion = bf16[384,2048]{1,0:T(8,128)(2,1)S(1)} fusion(bf16[384,2048]{1,0:T(8,128)(2,1)} %collective-permute-done.6, f32[384,1024]{1,0:T(8,128)S(1)} %copy-done.3, f32[384,1024]{1,0:T(8,128)S(1)} %copy-done.5, f32[384,1024]{1,0:T(8,128)S(1)} %copy-done.7, f32[384,1024]{1,0:T(8,128)S(1)} %copy-done.1, pred[]{:T(512)S(6)} %eq.128), kind=kLoop, calls=%fused_computation.18 | loop fusion | flops 4718592 | bytes 9437185 | tf_op jit(solution)/shard_map/convert_element_type | solution.py:138
  139.5 1.3 broadcast_select_fusion.3
  140.8 5.0 %all-to-all-done.3 = bf16[8,48,2048]{2,1,0:T(8,128)(2,1)} async-done(((bf16[8,48,2048]{2,1,0:T(8,128)(2,1)}), bf16[8,48,2048]{2,1,0:T(8,128)(2,1)}, u32[]{:S(2)}, u32[]{:S(2)}) %all-to-all-start.3) | async-done | bytes 1572896 | tf_op jit(solution)/shard_map/all_to_all | solution.py:79
  145.8 4.2 %all-to-all-start.5 = ((bf16[8,48,1024]{2,1,0:T(8,128)(2,1)}), bf16[8,48,1024]{2,1,0:T(8,128)(2,1)}, u32[]{:S(2)}, u32[]{:S(2)}) async-start(bf16[8,48,1024]{2,1,0:T(8,128)(2,1)} %bitcast.79), calls=%async_computation.5 | async-start | bytes 1572864 | tf_op jit(solution)/shard_map/all_to_all | solution.py:79
  150.1 2.0 %convolution_multiply_fusion.1 = f32[192,2048]{1,0:T(8,128)S(1)} fusion(bf16[384,2048]{1,0:T(8,128)(2,1)} %bitcast.12, f32[192]{0:T(256)S(1)} %bitcast.86, s32[192]{0:T(256)S(1)} %get-tuple-element.33, pred[192]{0:T(512)(128)(4,1)S(1)} %get-tuple-element.35), kind=kOutput, calls=%fused_computation.25 | convolution fusion | flops 302530560 | bytes 3147456 | tf_op jit(solution)/shard_map/dot_general | solution.py:171
  152.1 2.0 %fusion.20 = f32[192,2048]{1,0:T(8,128)S(1)} fusion(f32[192,2048]{1,0:T(8,128)S(1)} %convolution_multiply_fusion.1, bf16[384,2048]{1,0:T(8,128)(2,1)} %bitcast.12, f32[192]{0:T(256)S(1)} %bitcast.84, s32[192]{0:T(256)S(1)} %get-tuple-element.32, pred[192]{0:T(512)(128)(4,1)S(1)} %get-tuple-element.34), kind=kOutput, calls=%fused_computation.24 | convolution fusion | flops 302923776 | bytes 4720320 | tf_op jit(solution)/shard_map/dot_general | solution.py:171
  154.2 1.1 copy-done.8
  155.3 1.0 slice_select_fusion
  156.3 0.5 collective-permute-start.4
  156.8 13.6 %all-to-all-done.5 = bf16[8,48,1024]{2,1,0:T(8,128)(2,1)} async-done(((bf16[8,48,1024]{2,1,0:T(8,128)(2,1)}), bf16[8,48,1024]{2,1,0:T(8,128)(2,1)}, u32[]{:S(2)}, u32[]{:S(2)}) %all-to-all-start.5) | async-done | bytes 786464 | tf_op jit(solution)/shard_map/all_to_all | solution.py:79
  170.4 4.4 %all-to-all-start.4 = ((bf16[8,48,1024]{2,1,0:T(8,128)(2,1)}), bf16[8,48,1024]{2,1,0:T(8,128)(2,1)}, u32[]{:S(2)}, u32[]{:S(2)}) async-start(bf16[8,48,1024]{2,1,0:T(8,128)(2,1)} %bitcast.78), calls=%async_computation.4 | async-start | bytes 1572864 | tf_op jit(solution)/shard_map/all_to_all | solution.py:79
  174.9 2.6 %fusion.60 = f32[192,1024]{1,0:T(8,128)} fusion(bf16[384,1024]{1,0:T(8,128)(2,1)} %bitcast.16, s32[192]{0:T(256)S(1)} %get-tuple-element.32, s32[192]{0:T(256)S(1)} %get-tuple-element.33, pred[192]{0:T(512)(128)(4,1)S(1)} %get-tuple-element.34, pred[192]{0:T(512)(128)(4,1)S(1)} %get-tuple-element.35), kind=kOutput, calls=%fused_computation.101 | convolution fusion | flops 151363584 | bytes 1574784 | tf_op jit(solution)/shard_map/dot_general | solution.py:161
  177.5 0.5 collective-permute-start.7
  178.0 2.0 %add_convert_fusion.2 = bf16[192,1024]{1,0:T(8,128)(2,1)} fusion(f32[192,1024]{1,0:T(8,128)} %collective-permute-done.4, f32[192,2048]{1,0:T(8,128)S(1)} %copy-done.9, pred[]{:T(512)S(6)} %eq.113), kind=kLoop, calls=%fused_computation.46 | loop fusion | flops 589824 | bytes 2752513 | tf_op jit(solution)/shard_map/convert_element_type | solution.py:144
  180.0 6.6 %fusion.70 = f32[4096,768]{1,0:T(8,128)} fusion(bf16[384,4096]{1,0:T(8,128)(2,1)S(1)} %pad_maximum_fusion, bf16[384,768]{1,0:T(8,128)(2,1)S(1)} %copy-done.23), kind=kOutput, calls=%fused_computation.107 | convolution fusion | flops 2415919104 | bytes 16318464 | tf_op jit(solution)/shard_map/sd,sh->dh/dot_general | solution.py:165
  186.7 8.0 %all-to-all-done.4 = bf16[8,48,1024]{2,1,0:T(8,128)(2,1)} async-done(((bf16[8,48,1024]{2,1,0:T(8,128)(2,1)}), bf16[8,48,1024]{2,1,0:T(8,128)(2,1)}, u32[]{:S(2)}, u32[]{:S(2)}) %all-to-all-start.4) | async-done | bytes 786464 | tf_op jit(solution)/shard_map/all_to_all | solution.py:79
  194.7 1.6 collective-permute-done.7
  196.3 2.6 %fusion.27 = bf16[192,1024]{1,0:T(8,128)(2,1)} fusion(f32[192,1024]{1,0:T(8,128)} %collective-permute-done.7, bf16[384,1024]{1,0:T(8,128)(2,1)} %bitcast.14, s32[192]{0:T(256)S(1)} %get-tuple-element.32, s32[192]{0:T(256)S(1)} %get-tuple-element.33, pred[192]{0:T(512)(128)(4,1)S(1)} %get-tuple-element.34, pred[192]{0:T(512)(128)(4,1)S(1)} %get-tuple-element.35), kind=kOutput, calls=%fused_computation.35 | convolution fusion | flops 151756800 | bytes 1968000 | tf_op jit(solution)/shard_map/dot_general | solution.py:167
  (68 shorter events, 1.6 us)
Async XLA Ops:
  0.6 6.8 %copy-start.18 = (bf16[192,1024]{1,0:T(8,128)(2,1)S(1)}, bf16[192,1024]{1,0:T(8,128)(2,1)}, u32[]{:S(2)}) copy-start(bf16[192,1024]{1,0:T(8,128)(2,1)} %param.6) | copy-start | bytes 1179652
  0.6 4.2 %copy-start.24 = (s32[192,2]{0,1:T(2,128)S(1)}, s32[192,2]{0,1:T(2,128)}, u32[]{:S(2)}) copy-start(s32[192,2]{0,1:T(2,128)} %param.8) | copy-start | bytes 4612
  1.9 20.5 %collective-permute-start = (bf16[192,2048]{1,0:T(8,128)(2,1)S(1)}, bf16[192,2048]{1,0:T(8,128)(2,1)S(1)}, u32[]{:S(2)}, u32[]{:S(2)}) collective-permute-start(bf16[192,2048]{1,0:T(8,128)(2,1)S(1)} %pad_maximum_fusion.6), channel_id=1, source_target_pairs={{0,2},{1,3},{2,0},{3,1},{4,6},{5,7},{6,4},{7,5},{8,10},{9,11},{10,... | collective-permute-start | bytes 2359304 | tf_op jit(solution)/shard_map/ppermute | solution.py:84
  7.1 7.7 %copy-start.25 = (f32[192,2]{0,1:T(2,128)S(1)}, f32[192,2]{0,1:T(2,128)}, u32[]{:S(2)}) copy-start(f32[192,2]{0,1:T(2,128)} %param.9) | copy-start | bytes 4612
  8.9 14.9 %copy-start.19 = (bf16[192,1024]{1,0:T(8,128)(2,1)S(1)}, bf16[192,1024]{1,0:T(8,128)(2,1)}, u32[]{:S(2)}) copy-start(bf16[192,1024]{1,0:T(8,128)(2,1)} %param.7) | copy-start | bytes 1179652
  8.9 25.9 %all-to-all-start = ((bf16[8,48,1024]{2,1,0:T(8,128)(2,1)}), bf16[8,48,1024]{2,1,0:T(8,128)(2,1)S(1)}, u32[]{:S(2)}, u32[]{:S(2)}) async-start(bf16[8,48,1024]{2,1,0:T(8,128)(2,1)} %bitcast.3), calls=%async_computation | async-start | bytes 1572864 | tf_op jit(solution)/shard_map/all_to_all | solution.py:79
  34.8 23.9 %all-to-all-start.1 = ((bf16[8,48,1024]{2,1,0:T(8,128)(2,1)}), bf16[8,48,1024]{2,1,0:T(8,128)(2,1)S(1)}, u32[]{:S(2)}, u32[]{:S(2)}) async-start(bf16[8,48,1024]{2,1,0:T(8,128)(2,1)} %bitcast.5), calls=%async_computation.1 | async-start | bytes 1572864 | tf_op jit(solution)/shard_map/all_to_all | solution.py:79
  38.4 20.3 %collective-permute-start.1 = (bf16[384,1024]{1,0:T(8,128)(2,1)S(1)}, bf16[384,1024]{1,0:T(8,128)(2,1)S(1)}, u32[]{:S(2)}, u32[]{:S(2)}) collective-permute-start(bf16[384,1024]{1,0:T(8,128)(2,1)S(1)} %bitcast.80), channel_id=1, source_target_pairs={{0,1},{1,0},{2,3},{3,2},{4,5},{5,4},{6,7},{7,6},{8,9},{9,8},{10,11... | collective-permute-start | bytes 2359304 | tf_op jit(solution)/shard_map/ppermute | solution.py:95
  58.7 2.3 %collective-permute-start.2 = (bf16[384,1024]{1,0:T(8,128)(2,1)S(1)}, bf16[384,1024]{1,0:T(8,128)(2,1)S(1)}, u32[]{:S(2)}, u32[]{:S(2)}) collective-permute-start(bf16[384,1024]{1,0:T(8,128)(2,1)S(1)} %bitcast.81), channel_id=1, source_target_pairs={{0,1},{1,0},{2,3},{3,2},{4,5},{5,4},{6,7},{7,6},{8,9},{9,8},{10,11... | collective-permute-start | bytes 2359304 | tf_op jit(solution)/shard_map/ppermute | solution.py:96
  61.7 41.9 %all-to-all-start.2 = ((bf16[8,48,2048]{2,1,0:T(8,128)(2,1)}), bf16[8,48,2048]{2,1,0:T(8,128)(2,1)}, u32[]{:S(2)}, u32[]{:S(2)}) async-start(bf16[8,48,2048]{2,1,0:T(8,128)(2,1)} %bitcast.82), calls=%async_computation.2 | async-start | bytes 3145728 | tf_op jit(solution)/shard_map/all_to_all | solution.py:79
  71.4 1.0 copy-start.20
  78.4 1.9 copy-start.10
  78.4 2.1 %copy-start.11 = (f32[384,1024]{1,0:T(8,128)}, f32[384,1024]{1,0:T(8,128)S(1)}, u32[]{:S(2)}) copy-start(f32[384,1024]{1,0:T(8,128)S(1)} %get-tuple-element.41) | copy-start | bytes 4718596
  78.4 2.6 %copy-start.12 = (f32[384,1024]{1,0:T(8,128)}, f32[384,1024]{1,0:T(8,128)S(1)}, u32[]{:S(2)}) copy-start(f32[384,1024]{1,0:T(8,128)S(1)} %get-tuple-element.42) | copy-start | bytes 4718596
  78.5 3.2 %copy-start.13 = (f32[384,1024]{1,0:T(8,128)}, f32[384,1024]{1,0:T(8,128)S(1)}, u32[]{:S(2)}) copy-start(f32[384,1024]{1,0:T(8,128)S(1)} %get-tuple-element.43) | copy-start | bytes 4718596
  81.7 3.8 %collective-permute-start.3 = (bf16[384,2048]{1,0:T(8,128)(2,1)}, bf16[384,2048]{1,0:T(8,128)(2,1)}, u32[]{:S(2)}, u32[]{:S(2)}) collective-permute-start(bf16[384,2048]{1,0:T(8,128)(2,1)} %select_convert_fusion.1), channel_id=1, source_target_pairs={{0,1},{1,0},{2,3},{3,2},{4,5},{5,4},{6,7},{7,6},{8,9},{9,8},{10,11... | collective-permute-start | bytes 4718600 | tf_op jit(solution)/shard_map/ppermute | solution.py:136
  103.6 4.5 %collective-permute-start.5 = (bf16[384,2048]{1,0:T(8,128)(2,1)}, bf16[384,2048]{1,0:T(8,128)(2,1)}, u32[]{:S(2)}, u32[]{:S(2)}) collective-permute-start(bf16[384,2048]{1,0:T(8,128)(2,1)} %bitcast.10), channel_id=1, source_target_pairs={{0,1},{1,0},{2,3},{3,2},{4,5},{5,4},{6,7},{7,6},{8,9},{9,8},{10,11... | collective-permute-start | bytes 4718600 | tf_op jit(solution)/shard_map/ppermute | solution.py:55
  103.6 42.3 %all-to-all-start.3 = ((bf16[8,48,2048]{2,1,0:T(8,128)(2,1)}), bf16[8,48,2048]{2,1,0:T(8,128)(2,1)}, u32[]{:S(2)}, u32[]{:S(2)}) async-start(bf16[8,48,2048]{2,1,0:T(8,128)(2,1)} %bitcast.77), calls=%async_computation.3 | async-start | bytes 3145728 | tf_op jit(solution)/shard_map/all_to_all | solution.py:79
  110.3 0.9 copy-start.14
  110.3 1.1 copy-start.15
  110.3 2.2 %copy-start.21 = (f32[384,768]{1,0:T(8,128)S(1)}, f32[384,768]{1,0:T(8,128)}, u32[]{:S(2)}) copy-start(f32[384,768]{1,0:T(8,128)} %copy-done.20) | copy-start | bytes 3538948
  110.3 8.6 %slice-start = ((s8[6291456]{0:T(1024)(128)(4,1)}), s8[4194304]{0:T(1024)(128)(4,1)S(1)}, s32[]{:S(2)}) async-start(s8[6291456]{0:T(1024)(128)(4,1)} %bitcast.88), calls=%async_computation.6 | async-start | bytes 8388608
  110.5 1.2 copy-start.16
  110.5 1.5 copy-start.17
  112.5 6.5 %slice-start.1 = ((s8[6291456]{0:T(1024)(128)(4,1)}), s8[2097152]{0:T(1024)(128)(4,1)S(1)}, s32[]{:S(2)}) async-start(s8[6291456]{0:T(1024)(128)(4,1)} %bitcast.88), calls=%async_computation.7 | async-start | bytes 4194304
  119.0 2.7 %copy-start.22 = (bf16[384,768]{1,0:T(8,128)(2,1)}, bf16[384,768]{1,0:T(8,128)(2,1)S(1)}, u32[]{:S(2)}) copy-start(bf16[384,768]{1,0:T(8,128)(2,1)S(1)} %fusion.24) | copy-start | bytes 1769476
  122.8 1.9 copy-start
  122.8 2.2 %copy-start.2 = (f32[384,1024]{1,0:T(8,128)}, f32[384,1024]{1,0:T(8,128)S(1)}, u32[]{:S(2)}) copy-start(f32[384,1024]{1,0:T(8,128)S(1)} %get-tuple-element.37) | copy-start | bytes 4718596
  122.8 2.7 %copy-start.4 = (f32[384,1024]{1,0:T(8,128)}, f32[384,1024]{1,0:T(8,128)S(1)}, u32[]{:S(2)}) copy-start(f32[384,1024]{1,0:T(8,128)S(1)} %get-tuple-element.38) | copy-start | bytes 4718596
  122.8 3.1 %copy-start.6 = (f32[384,1024]{1,0:T(8,128)}, f32[384,1024]{1,0:T(8,128)S(1)}, u32[]{:S(2)}) copy-start(f32[384,1024]{1,0:T(8,128)S(1)} %get-tuple-element.39) | copy-start | bytes 4718596
  125.9 11.2 %collective-permute-start.6 = (bf16[384,2048]{1,0:T(8,128)(2,1)}, bf16[384,2048]{1,0:T(8,128)(2,1)}, u32[]{:S(2)}, u32[]{:S(2)}) collective-permute-start(bf16[384,2048]{1,0:T(8,128)(2,1)} %select_convert_fusion), channel_id=1, source_target_pairs={{0,1},{1,0},{2,3},{3,2},{4,5},{5,4},{6,7},{7,6},{8,9},{9,8},{10,11... | collective-permute-start | bytes 4718600 | tf_op jit(solution)/shard_map/ppermute | solution.py:136
  126.4 10.7 %copy-start.1 = (f32[384,1024]{1,0:T(8,128)S(1)}, f32[384,1024]{1,0:T(8,128)}, u32[]{:S(2)}) copy-start(f32[384,1024]{1,0:T(8,128)} %copy-done) | copy-start | bytes 4718596
  126.4 10.7 %copy-start.3 = (f32[384,1024]{1,0:T(8,128)S(1)}, f32[384,1024]{1,0:T(8,128)}, u32[]{:S(2)}) copy-start(f32[384,1024]{1,0:T(8,128)} %copy-done.2) | copy-start | bytes 4718596
  126.4 10.7 %copy-start.5 = (f32[384,1024]{1,0:T(8,128)S(1)}, f32[384,1024]{1,0:T(8,128)}, u32[]{:S(2)}) copy-start(f32[384,1024]{1,0:T(8,128)} %copy-done.4) | copy-start | bytes 4718596
  126.5 10.7 %copy-start.7 = (f32[384,1024]{1,0:T(8,128)S(1)}, f32[384,1024]{1,0:T(8,128)}, u32[]{:S(2)}) copy-start(f32[384,1024]{1,0:T(8,128)} %copy-done.6) | copy-start | bytes 4718596
  145.8 24.6 %all-to-all-start.5 = ((bf16[8,48,1024]{2,1,0:T(8,128)(2,1)}), bf16[8,48,1024]{2,1,0:T(8,128)(2,1)}, u32[]{:S(2)}, u32[]{:S(2)}) async-start(bf16[8,48,1024]{2,1,0:T(8,128)(2,1)} %bitcast.79), calls=%async_computation.5 | async-start | bytes 1572864 | tf_op jit(solution)/shard_map/all_to_all | solution.py:79
  154.1 1.1 copy-start.8
  156.3 21.7 %collective-permute-start.4 = (f32[192,1024]{1,0:T(8,128)}, f32[192,1024]{1,0:T(8,128)}, u32[]{:S(2)}, u32[]{:S(2)}) collective-permute-start(f32[192,1024]{1,0:T(8,128)} %slice_select_fusion), channel_id=1, source_target_pairs={{0,2},{1,3},{2,0},{3,1},{4,6},{5,7},{6,4},{7,5},{8,10},{9,11},{10,... | collective-permute-start | bytes 2359304 | tf_op jit(solution)/shard_map/ppermute | solution.py:144
  170.4 24.3 %all-to-all-start.4 = ((bf16[8,48,1024]{2,1,0:T(8,128)(2,1)}), bf16[8,48,1024]{2,1,0:T(8,128)(2,1)}, u32[]{:S(2)}, u32[]{:S(2)}) async-start(bf16[8,48,1024]{2,1,0:T(8,128)(2,1)} %bitcast.78), calls=%async_computation.4 | async-start | bytes 1572864 | tf_op jit(solution)/shard_map/all_to_all | solution.py:79
  174.9 3.1 %copy-start.9 = (f32[192,2048]{1,0:T(8,128)S(1)}, f32[192,2048]{1,0:T(8,128)}, u32[]{:S(2)}) copy-start(f32[192,2048]{1,0:T(8,128)} %copy-done.8) | copy-start | bytes 4718596
  177.5 2.6 %copy-start.23 = (bf16[384,768]{1,0:T(8,128)(2,1)S(1)}, bf16[384,768]{1,0:T(8,128)(2,1)}, u32[]{:S(2)}) copy-start(bf16[384,768]{1,0:T(8,128)(2,1)} %copy-done.22) | copy-start | bytes 1769476
  177.5 18.8 %collective-permute-start.7 = (f32[192,1024]{1,0:T(8,128)}, f32[192,1024]{1,0:T(8,128)}, u32[]{:S(2)}, u32[]{:S(2)}) collective-permute-start(f32[192,1024]{1,0:T(8,128)} %fusion.60), channel_id=1, source_target_pairs={{0,2},{1,3},{2,0},{3,1},{4,6},{5,7},{6,4},{7,5},{8,10},{9,11},{10,... | collective-permute-start | bytes 2359304 | tf_op jit(solution)/shard_map/ppermute | solution.py:162

commit v10 on v9

--- a/solution.py
+++ b/solution.py
@@ -102,7 +102,6 @@
                 jnp.where(p == half, pick_by(shift, own_all), pick_by(shift, other_all))
             )
     x_rows = jnp.concatenate(x_pieces, axis=1)
-    d_buf, x_rows = lax.optimization_barrier((d_buf, x_rows))
     got_d = send(d_buf)
 
     if n_loc == 1:

time: 200 us -> 197 us (0.985)
  matrix products: 50.7 us -> 46.7 us
    dot_general x1, matrix products: 10.7 us -> 7.49 us  [on_device(): jnp.einsum('sh,sd->hd', activation, d_rows, preferred_element_type=f32)]
    all_to_all x6, waiting for transfers between devices: 68.7 us -> 71.8 us  [send(): lax.all_to_all(buf.reshape(sections, capacity, width), 'attn', split_axis...]
    ppermute x1, waiting for transfers between devices: 2.28 us -> 0.01 us  [on_device(): lax.ppermute(got_other, 'exp', core_shift(s))]
    dot_general x1, matrix products: 4.91 us -> 2.75 us  [on_device(): out_g = jnp.dot(activation[:, part], w_down[g], preferred_element_type=f32)]
    unnamed x57 -> x75, local copies, waits for them, and re-layouts: 6.96 us -> 6.9 us
  transfers between devices with their start and end apart: 14 -> 14, of which waited for: 10 -> 9; matrix products, arithmetic and copies ran while one was open for 36% -> 35% of each run, Pallas kernels for 0% -> 0%
where the time goes in v10:
time: 197 us; the launch traced here: 196 us
  waiting for transfers between devices  84.1 us (43%)
  matrix products  46.7 us (24%)
  starting transfers between devices  32.1 us (16%)
  other arithmetic  21.5 us (11%)
  local copies, waits for them, and re-layouts  10.3 us (5%)
    all_to_all x6, waiting for transfers between devices, send(): lax.all_to_all(buf.reshape(sections, capacity, width), 'attn', split_axis...  71.8 us
    all_to_all x6, starting transfers between devices, send(): lax.all_to_all(buf.reshape(sections, capacity, width), 'attn', split_axis...  26.9 us
    dot_general x1, matrix products, on_device(): jnp.einsum('sh,sd->hd', activation, d_rows, preferred_element_type=f32)  7.49 us
    ppermute x1, waiting for transfers between devices, on_device(): lax.ppermute(jnp.concatenate([patches, grad_out], axis=1), 'exp', half_swap)  7.34 us
    unnamed x75, local copies, waits for them, and re-layouts  6.9 us
    dot_general x1, matrix products, on_device(): pre_act = jnp.dot(x_rows, up_mat, preferred_element_type=f32)  6.74 us
    convert_element_type x2, other arithmetic, group_sum(): return lax.optimization_barrier((summed.astype(bf16), hold))  6.65 us
    dot_general x1, matrix products, on_device(): jnp.einsum('sd,sh->dh', x_late, pre_late, preferred_element_type=f32)  6.61 us
  transfers between devices with their start and end apart: 14, of which 9 were waited for; matrix products, arithmetic and copies ran while one was open for 35% of the time, Pallas kernels for 0%

profile of v10, /device:TPU:0, one launch (start us, length us, event | category | flops | bytes accessed | tf_op | source)
XLA Modules:
  0.0 195.9 jit_solution(13845300013235953420)
XLA Ops:
  0.7 1.2 pad_maximum_fusion.6
  1.9 3.0 %collective-permute-start.1 = (bf16[192,2048]{1,0:T(8,128)(2,1)S(1)}, bf16[192,2048]{1,0:T(8,128)(2,1)S(1)}, u32[]{:S(2)}, u32[]{:S(2)}) collective-permute-start(bf16[192,2048]{1,0:T(8,128)(2,1)S(1)} %pad_maximum_fusion.6), channel_id=1, source_target_pairs={{0,2},{1,3},{2,0},{3,1},{4,6},{5,7},{6,4},{7,5},{8,10},{9,11},{10,... | collective-permute-start | bytes 2359304 | tf_op jit(solution)/shard_map/ppermute | solution.py:84
  5.5 0.9 reduce-window.6
  6.4 0.2 slice_reduce_fusion.4
  6.7 0.2 slice_reduce_fusion.3
  7.4 1.4 convolution_convert_fusion.1
  8.9 6.0 %all-to-all-start = ((bf16[8,48,1024]{2,1,0:T(8,128)(2,1)}), bf16[8,48,1024]{2,1,0:T(8,128)(2,1)S(1)}, u32[]{:S(2)}, u32[]{:S(2)}) async-start(bf16[8,48,1024]{2,1,0:T(8,128)(2,1)} %bitcast.2), calls=%async_computation | async-start | bytes 1572864 | tf_op jit(solution)/shard_map/all_to_all | solution.py:79
  14.8 0.2 select_reduce_fusion
  15.1 7.3 %collective-permute-done.1 = bf16[192,2048]{1,0:T(8,128)(2,1)S(1)} collective-permute-done((bf16[192,2048]{1,0:T(8,128)(2,1)S(1)}, bf16[192,2048]{1,0:T(8,128)(2,1)S(1)}, u32[]{:S(2)}, u32[]{:S(2)}) %collective-permute-start.1) | collective-permute-done | bytes 786464 | tf_op jit(solution)/shard_map/ppermute | solution.py:84
  22.4 1.4 convolution_convert_fusion
  23.9 1.9 multiply_convert_fusion
  25.9 8.9 %all-to-all-done = bf16[8,48,1024]{2,1,0:T(8,128)(2,1)S(1)} async-done(((bf16[8,48,1024]{2,1,0:T(8,128)(2,1)}), bf16[8,48,1024]{2,1,0:T(8,128)(2,1)S(1)}, u32[]{:S(2)}, u32[]{:S(2)}) %all-to-all-start) | async-done | bytes 786464 | tf_op jit(solution)/shard_map/all_to_all | solution.py:79
  34.8 3.5 %all-to-all-start.1 = ((bf16[8,48,1024]{2,1,0:T(8,128)(2,1)}), bf16[8,48,1024]{2,1,0:T(8,128)(2,1)S(1)}, u32[]{:S(2)}, u32[]{:S(2)}) async-start(bf16[8,48,1024]{2,1,0:T(8,128)(2,1)} %bitcast.5), calls=%async_computation.1 | async-start | bytes 1572864 | tf_op jit(solution)/shard_map/all_to_all | solution.py:79
  38.4 20.2 %all-to-all-done.1 = bf16[8,48,1024]{2,1,0:T(8,128)(2,1)S(1)} async-done(((bf16[8,48,1024]{2,1,0:T(8,128)(2,1)}), bf16[8,48,1024]{2,1,0:T(8,128)(2,1)S(1)}, u32[]{:S(2)}, u32[]{:S(2)}) %all-to-all-start.1) | async-done | bytes 786464 | tf_op jit(solution)/shard_map/all_to_all | solution.py:79
  58.7 4.3 %all-to-all-start.2 = ((bf16[8,48,2048]{2,1,0:T(8,128)(2,1)}), bf16[8,48,2048]{2,1,0:T(8,128)(2,1)}, u32[]{:S(2)}, u32[]{:S(2)}) async-start(bf16[8,48,2048]{2,1,0:T(8,128)(2,1)} %bitcast.9), calls=%async_computation.2 | async-start | bytes 3145728 | tf_op jit(solution)/shard_map/all_to_all | solution.py:79
  63.0 0.4 broadcast_select_fusion.11
  63.4 6.7 %fusion.6 = f32[384,768]{1,0:T(8,128)S(1)} fusion(bf16[1,4096,768]{2,1,0:T(8,128)(2,1)} %param.10, bf16[384,1024]{1,0:T(8,128)(2,1)S(1)} %get-tuple-element.43, bf16[384,1024]{1,0:T(8,128)(2,1)S(1)} %get-tuple-element.44, bf16[384,1024]{1,0:T(8,128)(2,1)S(1)} %get-tuple-element.45, bf16[384,1024]{1,0:T(8,128)(2,1)S(1)} %get-tuple-element.42), kind=kOutput, calls=%fused_computation.6 | convolution fusion | flops 2428502016 | bytes 10616832 | tf_op jit(solution)/shard_map/dot_general | solution.py:113
  70.2 1.0 copy-done.26
  71.3 2.7 %fusion.17 = f32[384,4096]{1,0:T(8,128)S(1)} fusion(bf16[1,768,4096]{2,1,0:T(8,128)(2,1)S(1)} %bitcast.87, f32[384,768]{1,0:T(8,128)S(1)} %fusion.6), kind=kOutput, calls=%fused_computation.11 | convolution fusion | flops 2421719040 | bytes 13762560 | tf_op jit(solution)/shard_map/dot_general | solution.py:120
  74.0 0.8 fusion.66
  74.9 1.9 select_convert_fusion.1
  76.8 0.3 copy-done.11
  77.1 0.5 collective-permute-start.3
  77.6 3.4 %collective-permute-done.3 = bf16[384,2048]{1,0:T(8,128)(2,1)} collective-permute-done((bf16[384,2048]{1,0:T(8,128)(2,1)}, bf16[384,2048]{1,0:T(8,128)(2,1)}, u32[]{:S(2)}, u32[]{:S(2)}) %collective-permute-start.3) | collective-permute-done | bytes 1572896 | tf_op jit(solution)/shard_map/ppermute | solution.py:135
  81.0 4.3 %add_convert_fusion.1 = bf16[384,2048]{1,0:T(8,128)(2,1)} fusion(bf16[384,2048]{1,0:T(8,128)(2,1)} %collective-permute-done.3, f32[384,1024]{1,0:T(8,128)S(1)} %get-tuple-element.37, f32[384,1024]{1,0:T(8,128)} %copy-done.10, f32[384,1024]{1,0:T(8,128)} %copy-done.11, f32[384,1024]{1,0:T(8,128)S(1)} %get-tuple-element.36, pred[]{:T(512)S(6)} %eq.128), kind=kLoop, calls=%fused_computation.20 | loop fusion | flops 4718592 | bytes 9437185 | tf_op jit(solution)/shard_map/convert_element_type | solution.py:137
  85.3 15.6 %all-to-all-done.2 = bf16[8,48,2048]{2,1,0:T(8,128)(2,1)} async-done(((bf16[8,48,2048]{2,1,0:T(8,128)(2,1)}), bf16[8,48,2048]{2,1,0:T(8,128)(2,1)}, u32[]{:S(2)}, u32[]{:S(2)}) %all-to-all-start.2) | async-done | bytes 1572896 | tf_op jit(solution)/shard_map/all_to_all | solution.py:79
  100.9 4.5 %all-to-all-start.3 = ((bf16[8,48,2048]{2,1,0:T(8,128)(2,1)}), bf16[8,48,2048]{2,1,0:T(8,128)(2,1)}, u32[]{:S(2)}, u32[]{:S(2)}) async-start(bf16[8,48,2048]{2,1,0:T(8,128)(2,1)} %bitcast.76), calls=%async_computation.3 | async-start | bytes 3145728 | tf_op jit(solution)/shard_map/all_to_all | solution.py:79
  105.4 1.6 broadcast_select_fusion.1
  107.3 0.7 copy-done.12
  108.0 0.3 copy-done.14
  108.3 0.2 copy-done.16
  108.5 0.3 copy-done.18
  108.8 0.5 copy-done.27
  109.3 6.5 %fusion.24 = bf16[384,768]{1,0:T(8,128)(2,1)S(1)} fusion(bf16[1,768,4096]{2,1,0:T(8,128)(2,1)} %param.11, f32[384,768]{1,0:T(8,128)S(1)} %copy-done.27, bf16[384,1024]{1,0:T(8,128)(2,1)S(1)} %get-tuple-element.51, bf16[384,1024]{1,0:T(8,128)(2,1)S(1)} %get-tuple-element.49, bf16[384,1024]{1,0:T(8,128)(2,1)S(1)} %get-tuple-element.50, ...), kind=kOutput, calls=%fused_computation.33 | convolution fusion | flops 2434105344 | bytes 11206656 | tf_op jit(solution)/shard_map/sd,hd->sh/dot_general | solution.py:148
  115.9 2.6 %fusion.11 = f32[384,4096]{1,0:T(8,128)S(1)} fusion(bf16[384,768]{1,0:T(8,128)(2,1)S(1)} %fusion.24, bf16[1,4096,768]{2,1,0:T(8,128)(2,1)S(1)} %bitcast.89), kind=kOutput, calls=%fused_computation.9 | convolution fusion | flops 2419064832 | bytes 13172736 | tf_op jit(solution)/shard_map/sh,dh->sd/dot_general | solution.py:153
  118.5 1.1 fusion.65
  119.7 1.9 select_convert_fusion
  121.6 0.3 copy-done.2
  121.8 0.5 copy-done.4
  122.3 0.5 copy-done.6
  122.8 0.5 collective-permute-start.6
  123.3 2.2 %pad_maximum_fusion = bf16[384,4096]{1,0:T(8,128)(2,1)S(1)} fusion(bf16[384,1024]{1,0:T(8,128)(2,1)} %copy-done.21, bf16[384,1024]{1,0:T(8,128)(2,1)} %copy-done.22, bf16[384,1024]{1,0:T(8,128)(2,1)} %copy-done.23, bf16[384,1024]{1,0:T(8,128)(2,1)} %copy-done.20), kind=kLoop, calls=%fused_computation.12 | loop fusion | flops 12582912 | bytes 6291456 | tf_op jit(solution)/shard_map/concatenate | solution.py:104
  125.6 0.2 copy-done.17
  125.8 0.2 copy-done.19
  126.1 0.4 copy-done.28
  126.5 7.5 %fusion.36 = f32[768,4096]{1,0:T(8,128)} fusion(bf16[384,1024]{1,0:T(8,128)(2,1)S(1)} %copy-done.19, bf16[384,1024]{1,0:T(8,128)(2,1)S(1)} %copy-done.15, bf16[384,1024]{1,0:T(8,128)(2,1)S(1)} %copy-done.17, bf16[384,1024]{1,0:T(8,128)(2,1)S(1)} %copy-done.13, f32[384,768]{1,0:T(8,128)S(1)} %copy-done.28), kind=kOutput, calls=%fused_computation.58 | convolution fusion | flops 2431156224 | bytes 16908288 | tf_op jit(solution)/shard_map/sh,sd->hd/dot_general | solution.py:156
  134.0 2.3 %add_convert_fusion = bf16[384,2048]{1,0:T(8,128)(2,1)S(1)} fusion(bf16[384,2048]{1,0:T(8,128)(2,1)} %collective-permute-done.6, f32[384,1024]{1,0:T(8,128)S(1)} %copy-done.3, f32[384,1024]{1,0:T(8,128)S(1)} %copy-done.5, f32[384,1024]{1,0:T(8,128)S(1)} %copy-done.7, f32[384,1024]{1,0:T(8,128)S(1)} %copy-done.1, pred[]{:T(512)S(6)} %eq.128), kind=kLoop, calls=%fused_computation.18 | loop fusion | flops 4718592 | bytes 9437185 | tf_op jit(solution)/shard_map/convert_element_type | solution.py:137
  136.3 1.3 broadcast_select_fusion.3
  137.6 5.6 %all-to-all-done.3 = bf16[8,48,2048]{2,1,0:T(8,128)(2,1)} async-done(((bf16[8,48,2048]{2,1,0:T(8,128)(2,1)}), bf16[8,48,2048]{2,1,0:T(8,128)(2,1)}, u32[]{:S(2)}, u32[]{:S(2)}) %all-to-all-start.3) | async-done | bytes 1572896 | tf_op jit(solution)/shard_map/all_to_all | solution.py:79
  143.2 4.2 %all-to-all-start.5 = ((bf16[8,48,1024]{2,1,0:T(8,128)(2,1)}), bf16[8,48,1024]{2,1,0:T(8,128)(2,1)}, u32[]{:S(2)}, u32[]{:S(2)}) async-start(bf16[8,48,1024]{2,1,0:T(8,128)(2,1)} %bitcast.78), calls=%async_computation.5 | async-start | bytes 1572864 | tf_op jit(solution)/shard_map/all_to_all | solution.py:79
  147.4 2.0 %convolution_multiply_fusion.1 = f32[192,2048]{1,0:T(8,128)S(1)} fusion(bf16[384,2048]{1,0:T(8,128)(2,1)} %bitcast.12, f32[192]{0:T(256)S(1)} %bitcast.84, s32[192]{0:T(256)S(1)} %get-tuple-element.28, pred[192]{0:T(512)(128)(4,1)S(1)} %get-tuple-element.30), kind=kOutput, calls=%fused_computation.25 | convolution fusion | flops 302530560 | bytes 3147456 | tf_op jit(solution)/shard_map/dot_general | solution.py:170
  149.4 2.0 %fusion.20 = f32[192,2048]{1,0:T(8,128)S(1)} fusion(f32[192,2048]{1,0:T(8,128)S(1)} %convolution_multiply_fusion.1, bf16[384,2048]{1,0:T(8,128)(2,1)} %bitcast.12, f32[192]{0:T(256)S(1)} %bitcast.82, s32[192]{0:T(256)S(1)} %get-tuple-element.29, pred[192]{0:T(512)(128)(4,1)S(1)} %get-tuple-element.31), kind=kOutput, calls=%fused_computation.24 | convolution fusion | flops 302923776 | bytes 4720320 | tf_op jit(solution)/shard_map/dot_general | solution.py:170
  151.5 1.1 copy-done.8
  152.6 1.0 slice_select_fusion
  153.6 0.5 collective-permute-start.4
  154.1 13.6 %all-to-all-done.5 = bf16[8,48,1024]{2,1,0:T(8,128)(2,1)} async-done(((bf16[8,48,1024]{2,1,0:T(8,128)(2,1)}), bf16[8,48,1024]{2,1,0:T(8,128)(2,1)}, u32[]{:S(2)}, u32[]{:S(2)}) %all-to-all-start.5) | async-done | bytes 786464 | tf_op jit(solution)/shard_map/all_to_all | solution.py:79
  167.7 4.4 %all-to-all-start.4 = ((bf16[8,48,1024]{2,1,0:T(8,128)(2,1)}), bf16[8,48,1024]{2,1,0:T(8,128)(2,1)}, u32[]{:S(2)}, u32[]{:S(2)}) async-start(bf16[8,48,1024]{2,1,0:T(8,128)(2,1)} %bitcast.77), calls=%async_computation.4 | async-start | bytes 1572864 | tf_op jit(solution)/shard_map/all_to_all | solution.py:79
  172.2 2.6 %fusion.60 = f32[192,1024]{1,0:T(8,128)} fusion(bf16[384,1024]{1,0:T(8,128)(2,1)} %bitcast.16, s32[192]{0:T(256)S(1)} %get-tuple-element.29, s32[192]{0:T(256)S(1)} %get-tuple-element.28, pred[192]{0:T(512)(128)(4,1)S(1)} %get-tuple-element.31, pred[192]{0:T(512)(128)(4,1)S(1)} %get-tuple-element.30), kind=kOutput, calls=%fused_computation.101 | convolution fusion | flops 151363584 | bytes 1574784 | tf_op jit(solution)/shard_map/dot_general | solution.py:160
  174.8 0.5 collective-permute-start.7
  175.3 2.0 %add_convert_fusion.2 = bf16[192,1024]{1,0:T(8,128)(2,1)} fusion(f32[192,1024]{1,0:T(8,128)} %collective-permute-done.4, f32[192,2048]{1,0:T(8,128)S(1)} %copy-done.9, pred[]{:T(512)S(6)} %eq.113), kind=kLoop, calls=%fused_computation.46 | loop fusion | flops 589824 | bytes 2752513 | tf_op jit(solution)/shard_map/convert_element_type | solution.py:143
  177.3 6.6 %fusion.70 = f32[4096,768]{1,0:T(8,128)} fusion(bf16[384,4096]{1,0:T(8,128)(2,1)S(1)} %pad_maximum_fusion, bf16[384,768]{1,0:T(8,128)(2,1)S(1)} %copy-done.30), kind=kOutput, calls=%fused_computation.107 | convolution fusion | flops 2415919104 | bytes 16318464 | tf_op jit(solution)/shard_map/sd,sh->dh/dot_general | solution.py:164
  184.0 7.8 %all-to-all-done.4 = bf16[8,48,1024]{2,1,0:T(8,128)(2,1)} async-done(((bf16[8,48,1024]{2,1,0:T(8,128)(2,1)}), bf16[8,48,1024]{2,1,0:T(8,128)(2,1)}, u32[]{:S(2)}, u32[]{:S(2)}) %all-to-all-start.4) | async-done | bytes 786464 | tf_op jit(solution)/shard_map/all_to_all | solution.py:79
  191.8 1.6 collective-permute-done.7
  193.4 2.6 %fusion.27 = bf16[192,1024]{1,0:T(8,128)(2,1)} fusion(f32[192,1024]{1,0:T(8,128)} %collective-permute-done.7, bf16[384,1024]{1,0:T(8,128)(2,1)} %bitcast.14, s32[192]{0:T(256)S(1)} %get-tuple-element.29, s32[192]{0:T(256)S(1)} %get-tuple-element.28, pred[192]{0:T(512)(128)(4,1)S(1)} %get-tuple-element.31, pred[192]{0:T(512)(128)(4,1)S(1)} %get-tuple-element.30), kind=kOutput, calls=%fused_computation.35 | convolution fusion | flops 151756800 | bytes 1968000 | tf_op jit(solution)/shard_map/dot_general | solution.py:166
  (87 shorter events, 1.8 us)
Async XLA Ops:
  0.6 6.8 %copy-start.24 = (bf16[192,1024]{1,0:T(8,128)(2,1)S(1)}, bf16[192,1024]{1,0:T(8,128)(2,1)}, u32[]{:S(2)}) copy-start(bf16[192,1024]{1,0:T(8,128)(2,1)} %param.6) | copy-start | bytes 1179652
  0.6 4.2 %copy-start.31 = (s32[192,2]{0,1:T(2,128)S(1)}, s32[192,2]{0,1:T(2,128)}, u32[]{:S(2)}) copy-start(s32[192,2]{0,1:T(2,128)} %param.8) | copy-start | bytes 4612
  1.9 20.5 %collective-permute-start.1 = (bf16[192,2048]{1,0:T(8,128)(2,1)S(1)}, bf16[192,2048]{1,0:T(8,128)(2,1)S(1)}, u32[]{:S(2)}, u32[]{:S(2)}) collective-permute-start(bf16[192,2048]{1,0:T(8,128)(2,1)S(1)} %pad_maximum_fusion.6), channel_id=1, source_target_pairs={{0,2},{1,3},{2,0},{3,1},{4,6},{5,7},{6,4},{7,5},{8,10},{9,11},{10,... | collective-permute-start | bytes 2359304 | tf_op jit(solution)/shard_map/ppermute | solution.py:84
  7.1 7.7 %copy-start.32 = (f32[192,2]{0,1:T(2,128)S(1)}, f32[192,2]{0,1:T(2,128)}, u32[]{:S(2)}) copy-start(f32[192,2]{0,1:T(2,128)} %param.9) | copy-start | bytes 4612
  8.9 15.0 %copy-start.25 = (bf16[192,1024]{1,0:T(8,128)(2,1)S(1)}, bf16[192,1024]{1,0:T(8,128)(2,1)}, u32[]{:S(2)}) copy-start(bf16[192,1024]{1,0:T(8,128)(2,1)} %param.7) | copy-start | bytes 1179652
  8.9 25.9 %all-to-all-start = ((bf16[8,48,1024]{2,1,0:T(8,128)(2,1)}), bf16[8,48,1024]{2,1,0:T(8,128)(2,1)S(1)}, u32[]{:S(2)}, u32[]{:S(2)}) async-start(bf16[8,48,1024]{2,1,0:T(8,128)(2,1)} %bitcast.2), calls=%async_computation | async-start | bytes 1572864 | tf_op jit(solution)/shard_map/all_to_all | solution.py:79
  34.8 23.9 %all-to-all-start.1 = ((bf16[8,48,1024]{2,1,0:T(8,128)(2,1)}), bf16[8,48,1024]{2,1,0:T(8,128)(2,1)S(1)}, u32[]{:S(2)}, u32[]{:S(2)}) async-start(bf16[8,48,1024]{2,1,0:T(8,128)(2,1)} %bitcast.5), calls=%async_computation.1 | async-start | bytes 1572864 | tf_op jit(solution)/shard_map/all_to_all | solution.py:79
  38.3 24.6 %collective-permute-start = (bf16[384,1024]{1,0:T(8,128)(2,1)S(1)}, bf16[384,1024]{1,0:T(8,128)(2,1)S(1)}, u32[]{:S(2)}, u32[]{:S(2)}) collective-permute-start(bf16[384,1024]{1,0:T(8,128)(2,1)S(1)} %bitcast.79), channel_id=1, source_target_pairs={{0,1},{1,0},{2,3},{3,2},{4,5},{5,4},{6,7},{7,6},{8,9},{9,8},{10,11... | collective-permute-start | bytes 2359304 | tf_op jit(solution)/shard_map/ppermute | solution.py:95
  58.7 4.3 %collective-permute-start.2 = (bf16[384,1024]{1,0:T(8,128)(2,1)S(1)}, bf16[384,1024]{1,0:T(8,128)(2,1)S(1)}, u32[]{:S(2)}, u32[]{:S(2)}) collective-permute-start(bf16[384,1024]{1,0:T(8,128)(2,1)S(1)} %bitcast.80), channel_id=1, source_target_pairs={{0,1},{1,0},{2,3},{3,2},{4,5},{5,4},{6,7},{7,6},{8,9},{9,8},{10,11... | collective-permute-start | bytes 2359304 | tf_op jit(solution)/shard_map/ppermute | solution.py:96
  58.7 42.2 %all-to-all-start.2 = ((bf16[8,48,2048]{2,1,0:T(8,128)(2,1)}), bf16[8,48,2048]{2,1,0:T(8,128)(2,1)}, u32[]{:S(2)}, u32[]{:S(2)}) async-start(bf16[8,48,2048]{2,1,0:T(8,128)(2,1)} %bitcast.9), calls=%async_computation.2 | async-start | bytes 3145728 | tf_op jit(solution)/shard_map/all_to_all | solution.py:79
  63.0 8.3 %slice-start = ((s8[6291456]{0:T(1024)(128)(4,1)}), s8[4194304]{0:T(1024)(128)(4,1)S(1)}, s32[]{:S(2)}) async-start(s8[6291456]{0:T(1024)(128)(4,1)} %bitcast.86), calls=%async_computation.6 | async-start | bytes 8388608
  63.4 6.8 %copy-start.20 = (bf16[384,1024]{1,0:T(8,128)(2,1)}, bf16[384,1024]{1,0:T(8,128)(2,1)S(1)}, u32[]{:S(2)}) copy-start(bf16[384,1024]{1,0:T(8,128)(2,1)S(1)} %get-tuple-element.42) | copy-start | bytes 2359300
  63.4 6.8 %copy-start.21 = (bf16[384,1024]{1,0:T(8,128)(2,1)}, bf16[384,1024]{1,0:T(8,128)(2,1)S(1)}, u32[]{:S(2)}) copy-start(bf16[384,1024]{1,0:T(8,128)(2,1)S(1)} %get-tuple-element.43) | copy-start | bytes 2359300
  63.4 6.8 %copy-start.22 = (bf16[384,1024]{1,0:T(8,128)(2,1)}, bf16[384,1024]{1,0:T(8,128)(2,1)S(1)}, u32[]{:S(2)}) copy-start(bf16[384,1024]{1,0:T(8,128)(2,1)S(1)} %get-tuple-element.44) | copy-start | bytes 2359300
  63.4 6.8 %copy-start.23 = (bf16[384,1024]{1,0:T(8,128)(2,1)}, bf16[384,1024]{1,0:T(8,128)(2,1)S(1)}, u32[]{:S(2)}) copy-start(bf16[384,1024]{1,0:T(8,128)(2,1)S(1)} %get-tuple-element.45) | copy-start | bytes 2359300
  63.4 7.9 %slice-start.1 = ((s8[6291456]{0:T(1024)(128)(4,1)}), s8[2097152]{0:T(1024)(128)(4,1)S(1)}, s32[]{:S(2)}) async-start(s8[6291456]{0:T(1024)(128)(4,1)} %bitcast.86), calls=%async_computation.7 | async-start | bytes 4194304
  70.2 1.1 copy-start.26
  74.9 1.9 copy-start.10
  74.9 2.2 %copy-start.11 = (f32[384,1024]{1,0:T(8,128)}, f32[384,1024]{1,0:T(8,128)S(1)}, u32[]{:S(2)}) copy-start(f32[384,1024]{1,0:T(8,128)S(1)} %get-tuple-element.39) | copy-start | bytes 4718596
  77.1 3.9 %collective-permute-start.3 = (bf16[384,2048]{1,0:T(8,128)(2,1)}, bf16[384,2048]{1,0:T(8,128)(2,1)}, u32[]{:S(2)}, u32[]{:S(2)}) collective-permute-start(bf16[384,2048]{1,0:T(8,128)(2,1)} %select_convert_fusion.1), channel_id=1, source_target_pairs={{0,1},{1,0},{2,3},{3,2},{4,5},{5,4},{6,7},{7,6},{8,9},{9,8},{10,11... | collective-permute-start | bytes 4718600 | tf_op jit(solution)/shard_map/ppermute | solution.py:135
  100.9 4.5 %collective-permute-start.5 = (bf16[384,2048]{1,0:T(8,128)(2,1)}, bf16[384,2048]{1,0:T(8,128)(2,1)S(1)}, u32[]{:S(2)}, u32[]{:S(2)}) collective-permute-start(bf16[384,2048]{1,0:T(8,128)(2,1)} %bitcast.10), channel_id=1, source_target_pairs={{0,1},{1,0},{2,3},{3,2},{4,5},{5,4},{6,7},{7,6},{8,9},{9,8},{10,11... | collective-permute-start | bytes 4718600 | tf_op jit(solution)/shard_map/ppermute | solution.py:55
  100.9 42.2 %all-to-all-start.3 = ((bf16[8,48,2048]{2,1,0:T(8,128)(2,1)}), bf16[8,48,2048]{2,1,0:T(8,128)(2,1)}, u32[]{:S(2)}, u32[]{:S(2)}) async-start(bf16[8,48,2048]{2,1,0:T(8,128)(2,1)} %bitcast.76), calls=%async_computation.3 | async-start | bytes 3145728 | tf_op jit(solution)/shard_map/all_to_all | solution.py:79
  107.2 0.9 copy-start.12
  107.2 1.1 copy-start.14
  107.2 2.2 %copy-start.27 = (f32[384,768]{1,0:T(8,128)S(1)}, f32[384,768]{1,0:T(8,128)}, u32[]{:S(2)}) copy-start(f32[384,768]{1,0:T(8,128)} %copy-done.26) | copy-start | bytes 3538948
  107.2 8.6 %slice-start.2 = ((s8[6291456]{0:T(1024)(128)(4,1)}), s8[4194304]{0:T(1024)(128)(4,1)S(1)}, s32[]{:S(2)}) async-start(s8[6291456]{0:T(1024)(128)(4,1)} %bitcast.88), calls=%async_computation.8 | async-start | bytes 8388608
  107.3 1.2 copy-start.16
  107.3 1.5 copy-start.18
  109.3 6.5 %slice-start.3 = ((s8[6291456]{0:T(1024)(128)(4,1)}), s8[2097152]{0:T(1024)(128)(4,1)S(1)}, s32[]{:S(2)}) async-start(s8[6291456]{0:T(1024)(128)(4,1)} %bitcast.88), calls=%async_computation.9 | async-start | bytes 4194304
  115.8 2.7 %copy-start.29 = (bf16[384,768]{1,0:T(8,128)(2,1)}, bf16[384,768]{1,0:T(8,128)(2,1)S(1)}, u32[]{:S(2)}) copy-start(bf16[384,768]{1,0:T(8,128)(2,1)S(1)} %fusion.24) | copy-start | bytes 1769476
  119.6 1.9 copy-start
  119.6 2.2 %copy-start.2 = (f32[384,1024]{1,0:T(8,128)}, f32[384,1024]{1,0:T(8,128)S(1)}, u32[]{:S(2)}) copy-start(f32[384,1024]{1,0:T(8,128)S(1)} %get-tuple-element.33) | copy-start | bytes 4718596
  119.7 2.7 %copy-start.4 = (f32[384,1024]{1,0:T(8,128)}, f32[384,1024]{1,0:T(8,128)S(1)}, u32[]{:S(2)}) copy-start(f32[384,1024]{1,0:T(8,128)S(1)} %get-tuple-element.34) | copy-start | bytes 4718596
  119.7 3.1 %copy-start.6 = (f32[384,1024]{1,0:T(8,128)}, f32[384,1024]{1,0:T(8,128)S(1)}, u32[]{:S(2)}) copy-start(f32[384,1024]{1,0:T(8,128)S(1)} %get-tuple-element.35) | copy-start | bytes 4718596
  122.8 11.2 %collective-permute-start.6 = (bf16[384,2048]{1,0:T(8,128)(2,1)}, bf16[384,2048]{1,0:T(8,128)(2,1)}, u32[]{:S(2)}, u32[]{:S(2)}) collective-permute-start(bf16[384,2048]{1,0:T(8,128)(2,1)} %select_convert_fusion), channel_id=1, source_target_pairs={{0,1},{1,0},{2,3},{3,2},{4,5},{5,4},{6,7},{7,6},{8,9},{9,8},{10,11... | collective-permute-start | bytes 4718600 | tf_op jit(solution)/shard_map/ppermute | solution.py:135
  123.3 2.2 %copy-start.13 = (bf16[384,1024]{1,0:T(8,128)(2,1)S(1)}, bf16[384,1024]{1,0:T(8,128)(2,1)}, u32[]{:S(2)}) copy-start(bf16[384,1024]{1,0:T(8,128)(2,1)} %copy-done.12) | copy-start | bytes 2359300
  123.3 2.3 %copy-start.15 = (bf16[384,1024]{1,0:T(8,128)(2,1)S(1)}, bf16[384,1024]{1,0:T(8,128)(2,1)}, u32[]{:S(2)}) copy-start(bf16[384,1024]{1,0:T(8,128)(2,1)} %copy-done.14) | copy-start | bytes 2359300
  123.3 2.5 %copy-start.17 = (bf16[384,1024]{1,0:T(8,128)(2,1)S(1)}, bf16[384,1024]{1,0:T(8,128)(2,1)}, u32[]{:S(2)}) copy-start(bf16[384,1024]{1,0:T(8,128)(2,1)} %copy-done.16) | copy-start | bytes 2359300
  123.3 2.8 %copy-start.19 = (bf16[384,1024]{1,0:T(8,128)(2,1)S(1)}, bf16[384,1024]{1,0:T(8,128)(2,1)}, u32[]{:S(2)}) copy-start(bf16[384,1024]{1,0:T(8,128)(2,1)} %copy-done.18) | copy-start | bytes 2359300
  123.3 3.2 %copy-start.28 = (f32[384,768]{1,0:T(8,128)S(1)}, f32[384,768]{1,0:T(8,128)}, u32[]{:S(2)}) copy-start(f32[384,768]{1,0:T(8,128)} %copy-done.26) | copy-start | bytes 3538948
  126.5 7.5 %copy-start.1 = (f32[384,1024]{1,0:T(8,128)S(1)}, f32[384,1024]{1,0:T(8,128)}, u32[]{:S(2)}) copy-start(f32[384,1024]{1,0:T(8,128)} %copy-done) | copy-start | bytes 4718596
  126.5 7.5 %copy-start.3 = (f32[384,1024]{1,0:T(8,128)S(1)}, f32[384,1024]{1,0:T(8,128)}, u32[]{:S(2)}) copy-start(f32[384,1024]{1,0:T(8,128)} %copy-done.2) | copy-start | bytes 4718596
  126.5 7.5 %copy-start.5 = (f32[384,1024]{1,0:T(8,128)S(1)}, f32[384,1024]{1,0:T(8,128)}, u32[]{:S(2)}) copy-start(f32[384,1024]{1,0:T(8,128)} %copy-done.4) | copy-start | bytes 4718596
  126.5 7.5 %copy-start.7 = (f32[384,1024]{1,0:T(8,128)S(1)}, f32[384,1024]{1,0:T(8,128)}, u32[]{:S(2)}) copy-start(f32[384,1024]{1,0:T(8,128)} %copy-done.6) | copy-start | bytes 4718596
  143.2 24.6 %all-to-all-start.5 = ((bf16[8,48,1024]{2,1,0:T(8,128)(2,1)}), bf16[8,48,1024]{2,1,0:T(8,128)(2,1)}, u32[]{:S(2)}, u32[]{:S(2)}) async-start(bf16[8,48,1024]{2,1,0:T(8,128)(2,1)} %bitcast.78), calls=%async_computation.5 | async-start | bytes 1572864 | tf_op jit(solution)/shard_map/all_to_all | solution.py:79
  151.5 1.1 copy-start.8
  153.6 21.7 %collective-permute-start.4 = (f32[192,1024]{1,0:T(8,128)}, f32[192,1024]{1,0:T(8,128)}, u32[]{:S(2)}, u32[]{:S(2)}) collective-permute-start(f32[192,1024]{1,0:T(8,128)} %slice_select_fusion), channel_id=1, source_target_pairs={{0,2},{1,3},{2,0},{3,1},{4,6},{5,7},{6,4},{7,5},{8,10},{9,11},{10,... | collective-permute-start | bytes 2359304 | tf_op jit(solution)/shard_map/ppermute | solution.py:143
  167.7 24.1 %all-to-all-start.4 = ((bf16[8,48,1024]{2,1,0:T(8,128)(2,1)}), bf16[8,48,1024]{2,1,0:T(8,128)(2,1)}, u32[]{:S(2)}, u32[]{:S(2)}) async-start(bf16[8,48,1024]{2,1,0:T(8,128)(2,1)} %bitcast.77), calls=%async_computation.4 | async-start | bytes 1572864 | tf_op jit(solution)/shard_map/all_to_all | solution.py:79
  172.2 3.1 %copy-start.9 = (f32[192,2048]{1,0:T(8,128)S(1)}, f32[192,2048]{1,0:T(8,128)}, u32[]{:S(2)}) copy-start(f32[192,2048]{1,0:T(8,128)} %copy-done.8) | copy-start | bytes 4718596
  174.8 2.6 %copy-start.30 = (bf16[384,768]{1,0:T(8,128)(2,1)S(1)}, bf16[384,768]{1,0:T(8,128)(2,1)}, u32[]{:S(2)}) copy-start(bf16[384,768]{1,0:T(8,128)(2,1)} %copy-done.29) | copy-start | bytes 1769476
  174.8 18.6 %collective-permute-start.7 = (f32[192,1024]{1,0:T(8,128)}, f32[192,1024]{1,0:T(8,128)}, u32[]{:S(2)}, u32[]{:S(2)}) collective-permute-start(f32[192,1024]{1,0:T(8,128)} %fusion.60), channel_id=1, source_target_pairs={{0,2},{1,3},{2,0},{3,1},{4,6},{5,7},{6,4},{7,5},{8,10},{9,11},{10,... | collective-permute-start | bytes 2359304 | tf_op jit(solution)/shard_map/ppermute | solution.py:161
